TPU v7x, 256 devices: a whole 4x4x8 slice. The times are simulated.
256 devices in a mesh: dp: 16 (over y, x), expert: 16 (over z, core).
Axes of the slice: x: 4, y: 4, z: 8, core: 2. Of those that a mesh axis runs over, the one named last changes fastest.
Arguments:
- tokens: bfloat16 [32768, 768], P(('dp', 'expert')), may hold values from -24 to 24
- expert_ids: int32 [32768, 2], P(('dp', 'expert')), may hold values from 0 to 15, all different within a row; in each aligned block of 128 rows (0 to 127, 128 to 255, ...) at most 32 rows name the same one
- router: bfloat16 [768, 16], replicated, may hold values from -0.4375 to 0.4375
- weight_in: bfloat16 [16, 768, 3072], P('expert'), may hold values from -0.21875 to 0.21875
- weight_out: bfloat16 [16, 3072, 768], P('expert'), may hold values from -0.4375 to 0.4375
- premises: bfloat16 [2048, 768], P('dp'), may hold values from -6 to 6
- positive: int32 [512], replicated, may hold values from 0 to 2047
- tile_mask: int32 [256, 16], replicated, may hold values 0 or 1
Outputs:
- grad_in: float32 [16, 768, 3072], P('expert', 'dp')
- grad_out: float32 [16, 3072, 768], P('expert', 'dp')
Inputs may be any that keep to these rules, and one draw needn't show every extreme that they name: `expert_ids`: among the 128 tokens of one device no expert is named by more than 32 pairs, and one expert is named by exactly 32; the two experts of a token differ.
All inputs are finite; a program needn't handle non-finite values.
Results may differ from a plain program's by a relative error of at most 0.02.
Values may be sent and summed in bfloat16 or wider, within the bound.
No kernel may reach another device: no remote copies, remote signals or barrier semaphores. Data moves between devices by JAX's collectives and lax.ppermute only.
A program may use at most 128 MiB of HBM per device.

v0:
```python
import jax
import jax.numpy as jnp
from jax import lax
from jax.sharding import PartitionSpec as P

LEN = 64


SCORE_SCALE = 20.0
LOSS_SCALE = 64.0
EPSILON = 1e-06
HIGHEST = lax.Precision.HIGHEST


def gelu_parts(pre_act):
    inner_arg = 0.7978845608028654 * (pre_act + 0.044715 * pre_act * pre_act * pre_act)
    tangent = jnp.tanh(inner_arg)
    gelu_val = 0.5 * pre_act * (1.0 + tangent)
    slope_val = 0.5 * (1.0 + tangent) + 0.5 * pre_act * (
        1.0 - tangent * tangent
    ) * 0.7978845608028654 * (1.0 + 0.134145 * pre_act * pre_act)
    return (gelu_val, slope_val)


def route_slots(expert_ids, logits, experts, capacity):
    pick_hot = expert_ids[:, :, None] == jnp.arange(experts, dtype=jnp.int32)[None, None, :]
    picked = jnp.sum(jnp.where(pick_hot, logits[:, None, :], jnp.zeros((), logits.dtype)), axis=2)
    gate_wts = jax.nn.sigmoid(picked - picked[:, ::-1]).astype(jnp.bfloat16)
    flat_ids = expert_ids.reshape(-1)
    flat_hot = (flat_ids[:, None] == jnp.arange(experts, dtype=jnp.int32)[None, :]).astype(
        jnp.int32
    )
    running = jnp.cumsum(flat_hot, axis=0)
    position = jnp.sum(running * flat_hot, axis=1) - 1
    slot_ids = flat_ids * capacity + position
    return (gate_wts, slot_ids.reshape(expert_ids.shape))


def split_dot(a, b, dims):
    a_hi = a.astype(jnp.bfloat16)
    a_lo = (a - a_hi.astype(jnp.float32)).astype(jnp.bfloat16)
    hi = lax.dot_general(a_hi, b, dims, preferred_element_type=jnp.float32)
    lo = lax.dot_general(a_lo, b, dims, preferred_element_type=jnp.float32)
    return hi + lo


def contrast_terms(query_vec, key_rows, key_scale, open_mask, pos_hot):
    include = jnp.logical_or(open_mask, pos_hot)
    scores = (
        SCORE_SCALE
        * lax.dot_general(
            query_vec, key_rows, (((1,), (1,)), ((), ())), preferred_element_type=jnp.float32
        )
        * key_scale[None, :]
    )
    exp_scores = jnp.where(include, jnp.exp(scores), jnp.zeros((), scores.dtype))
    partition = jnp.sum(exp_scores, axis=1)
    soft_weight = (exp_scores * key_scale[None, :]).astype(jnp.bfloat16)
    weighted_sum = jnp.dot(soft_weight, key_rows, preferred_element_type=jnp.float32)
    pos_scale = jnp.sum(
        jnp.where(pos_hot, key_scale[None, :], jnp.zeros((), key_scale.dtype)), axis=1
    )
    pos_vec = (
        jnp.dot(pos_hot.astype(jnp.bfloat16), key_rows, preferred_element_type=jnp.float32)
        * pos_scale[:, None]
    )
    return (weighted_sum, partition, pos_vec)


def ring_pairs(nx, ny, along_x, step):
    pairs = []
    for y in range(ny):
        for x in range(nx):
            if along_x:
                pairs.append((y * nx + x, y * nx + (x + step) % nx))
            else:
                pairs.append((y * nx + x, ((y + step) % ny) * nx + x))
    return pairs


def take_chunk(chunks, index, count):
    return lax.dynamic_index_in_dim(chunks, lax.rem(index + 2 * count, count), 0, keepdims=False)


def ring_start(fwd, bwd, count, pos):
    return dict(fwd=fwd, bwd=bwd, count=count, pos=pos,
                acc_f=take_chunk(fwd, pos - 1, count).astype(jnp.float32),
                acc_b=take_chunk(bwd, pos + 1, count).astype(jnp.float32))


def ring_step(state, k, fwd_pairs, bwd_pairs):
    count, pos = state["count"], state["pos"]
    got_f = lax.ppermute(state["acc_f"].astype(jnp.bfloat16), "dp", fwd_pairs)
    got_b = lax.ppermute(state["acc_b"].astype(jnp.bfloat16), "dp", bwd_pairs)
    state = dict(state)
    state["acc_f"] = got_f.astype(jnp.float32) + take_chunk(state["fwd"], pos - 2 - k, count).astype(jnp.float32)
    state["acc_b"] = got_b.astype(jnp.float32) + take_chunk(state["bwd"], pos + 2 + k, count).astype(jnp.float32)
    return state


def reduce_scatter_2d(part_in, part_out, nx, ny, x_pos, y_pos):
    def grid(part):
        rows = part.shape[0] // (nx * ny)
        return part.reshape(ny, nx, rows, part.shape[1])

    gin, gout = grid(part_in), grid(part_out)
    hin, hout = gin.shape[-1] // 2, gout.shape[-1] // 2
    x_f, x_b = ring_pairs(nx, ny, True, 1), ring_pairs(nx, ny, True, -1)
    y_f, y_b = ring_pairs(nx, ny, False, 1), ring_pairs(nx, ny, False, -1)
    ra = ring_start(jnp.transpose(gin[..., :hin], (1, 0, 2, 3)),
                    jnp.transpose(gout[..., :hout], (1, 0, 2, 3)), nx, x_pos)
    rb = ring_start(gin[..., hin:], gout[..., hout:], ny, y_pos)
    for k in range(max(nx, ny) - 1):
        if k < nx - 1:
            ra = ring_step(ra, k, x_f, x_b)
        if k < ny - 1:
            rb = ring_step(rb, k, y_f, y_b)
    ra = ring_start(ra["acc_f"], ra["acc_b"], ny, y_pos)
    rb = ring_start(rb["acc_f"], rb["acc_b"], nx, x_pos)
    for k in range(max(nx, ny) - 1):
        if k < ny - 1:
            ra = ring_step(ra, k, y_f, y_b)
        if k < nx - 1:
            rb = ring_step(rb, k, x_f, x_b)
    total_in = jnp.concatenate([ra["acc_f"], rb["acc_f"]], axis=-1)
    total_out = jnp.concatenate([ra["acc_b"], rb["acc_b"]], axis=-1)
    return total_in, total_out


def on_device(tokens, expert_ids, router, weight_in, weight_out, premises, positive, tile_mask):
    token_count, model_width = tokens.shape
    ffn_width = weight_in.shape[2]
    experts = router.shape[1]
    expert_size = lax.axis_size("expert")
    dp_size = lax.axis_size("dp")
    nx = 4
    ny = dp_size // nx
    capacity = 4 * token_count // expert_size
    slot_total = experts * capacity
    seq_count = token_count // LEN
    row_seqs = expert_size * seq_count
    dp_index = lax.axis_index("dp")
    col_index = lax.axis_index("expert")
    device = dp_index * expert_size + col_index

    logits = jnp.dot(tokens, router, preferred_element_type=jnp.float32)
    gate_wts, slot_ids = route_slots(expert_ids, logits, experts, capacity)
    slot_hot = slot_ids[:, :, None] == jnp.arange(slot_total, dtype=jnp.int32)[None, None, :]
    placing = jnp.sum(slot_hot.astype(jnp.bfloat16), axis=1)
    combine = jnp.sum(
        jnp.where(slot_hot, gate_wts[:, :, None], jnp.zeros((), jnp.bfloat16)), axis=1
    )
    extra = 128
    seq_hot = (
        (jnp.arange(token_count, dtype=jnp.int32) // LEN)[:, None]
        == jnp.arange(extra, dtype=jnp.int32)[None, :]
    ).astype(jnp.bfloat16)
    payload = jnp.concatenate([tokens, seq_hot], axis=1)
    outgoing = lax.dot_general(
        placing, payload, (((0,), (0,)), ((), ())), preferred_element_type=jnp.float32
    )
    outgoing = jnp.concatenate(
        [outgoing[:, :model_width],
         lax.dot_general(combine, seq_hot, (((0,), (0,)), ((), ())),
                         preferred_element_type=jnp.float32)],
        axis=1,
    ).astype(jnp.bfloat16)
    outgoing = outgoing.reshape(experts, capacity, model_width + extra)
    arrived = lax.all_to_all(outgoing, "expert", split_axis=0, concat_axis=0, tiled=True)
    input_flat = arrived[:, :, :model_width].reshape(expert_size * capacity, model_width)
    my_meta = arrived[:, :, model_width:model_width + seq_count].astype(jnp.float32)
    same_src = jnp.eye(expert_size, dtype=jnp.float32)
    meta_t = jnp.transpose(my_meta, (2, 0, 1))
    sel_gate = same_src[:, None, :, None] * meta_t[None, :, :, :]
    sel_gate = sel_gate.reshape(row_seqs, expert_size * capacity)

    pre_act = jnp.dot(input_flat, weight_in[0], preferred_element_type=jnp.float32)
    gelu_val, slope_flat = gelu_parts(pre_act)
    hidden = gelu_val.astype(jnp.bfloat16)
    seq_hidden = jnp.dot(sel_gate.astype(jnp.bfloat16), hidden, preferred_element_type=jnp.float32)
    moe_seq = split_dot(seq_hidden, weight_out[0], (((1,), (0,)), ((), ())))
    moe_back = lax.all_to_all(
        moe_seq.reshape(expert_size, seq_count, model_width), "expert",
        split_axis=0, concat_axis=0, tiled=True,
    )
    moe_mine = jnp.sum(moe_back, axis=0)

    token_sum = jnp.sum(tokens.astype(jnp.float32).reshape(seq_count, LEN, model_width), axis=1)
    pooled = (token_sum + moe_mine) / LEN
    row_scale = lax.rsqrt(jnp.sum(pooled * pooled, axis=1) + EPSILON)
    unit_vec = pooled * row_scale[:, None]
    query_vec = unit_vec.astype(jnp.bfloat16)
    prem_count = premises.shape[0]
    key_rows = lax.all_gather(premises, "dp", axis=0, tiled=True)
    key_scale = lax.rsqrt(jnp.sum(jnp.square(key_rows.astype(jnp.float32)), axis=1) + EPSILON)
    key_index = jnp.arange(key_rows.shape[0], dtype=jnp.int32)
    own_positive = lax.dynamic_slice_in_dim(positive, device * seq_count, seq_count)
    mask_row = lax.dynamic_index_in_dim(tile_mask, device, 0, keepdims=False)
    key_open = jnp.repeat(mask_row, prem_count) == 1
    weighted_sum, partition, pos_vec = contrast_terms(
        query_vec,
        key_rows,
        key_scale,
        key_open[None, :],
        key_index[None, :] == own_positive[:, None],
    )
    delta_unit = LOSS_SCALE * SCORE_SCALE * (weighted_sum / partition[:, None] - pos_vec)
    delta_pooled = row_scale[:, None] * (
        delta_unit - unit_vec * jnp.sum(unit_vec * delta_unit, axis=1, keepdims=True)
    )
    delta_seq = (delta_pooled / LEN).astype(jnp.bfloat16)
    delta_row = lax.all_gather(delta_seq, "expert", axis=0, tiled=True)

    dims_t = (((0,), (0,)), ((), ()))
    spread = lax.dot_general(
        delta_row, weight_out[0], (((1,), (1,)), ((), ())), preferred_element_type=jnp.float32
    ).astype(jnp.bfloat16)
    dhidden = lax.dot_general(
        sel_gate.astype(jnp.bfloat16), spread, dims_t, preferred_element_type=jnp.float32
    )
    delta_pre = (dhidden * slope_flat).astype(jnp.bfloat16)
    grad_in_term = lax.dot_general(
        input_flat, delta_pre, dims_t, preferred_element_type=jnp.float32
    ).astype(jnp.bfloat16)
    grad_out_term = lax.dot_general(
        seq_hidden.astype(jnp.bfloat16), delta_row, dims_t, preferred_element_type=jnp.float32
    ).astype(jnp.bfloat16)
    grad_in, grad_out = reduce_scatter_2d(
        grad_in_term, grad_out_term, nx, ny, lax.rem(dp_index, nx), dp_index // nx
    )
    return (grad_in[None], grad_out[None])


def solution(mesh):
    in_specs = (
        P(("dp", "expert"), None),
        P(("dp", "expert"), None),
        P(),
        P("expert", None, None),
        P("expert", None, None),
        P("dp", None),
        P(),
        P(),
    )
    out_specs = (P("expert", "dp", None), P("expert", "dp", None))
    return jax.shard_map(
        on_device, mesh=mesh, in_specs=in_specs, out_specs=out_specs, check_vma=False
    )
```

profile of v0, /device:TPU:32, one launch (start us, length us, event | category | flops | bytes accessed | tf_op | source)
XLA Modules:
  0.0 193.8 jit_solution(2256210469696915239)
XLA Ops:
  7.9 0.8 copy.66
  10.8 1.0 fusion.84
  11.9 0.8 select_reduce_fusion.1
  13.1 1.3 fusion.46
  14.8 1.0 pad_maximum_fusion
  15.8 8.6 %all-to-all-start = ((bf16[16,32,896]{2,1,0:T(8,128)(2,1)}), bf16[16,32,896]{2,1,0:T(8,128)(2,1)S(1)}, u32[]{:S(2)}, u32[]{:S(2)}) async-start(bf16[16,32,896]{2,1,0:T(8,128)(2,1)} %pad_maximum_fusion), calls=%async_computation | async-start | bytes 1835008 | tf_op jit(solution)/shard_map/all_to_all | solution.py:169
  24.4 0.8 dynamic_slice.92
  25.4 20.8 %all-to-all-done = bf16[16,32,896]{2,1,0:T(8,128)(2,1)S(1)} async-done(((bf16[16,32,896]{2,1,0:T(8,128)(2,1)}), bf16[16,32,896]{2,1,0:T(8,128)(2,1)S(1)}, u32[]{:S(2)}, u32[]{:S(2)}) %all-to-all-start) | async-done | bytes 917536 | tf_op jit(solution)/shard_map/all_to_all | solution.py:169
  46.8 4.5 %fusion.13 = f32[512,3072]{1,0:T(8,128)S(1)} fusion(bf16[512,768]{1,0:T(8,128)(2,1)S(1)} %bitcast.173, bf16[1,768,3072]{2,1,0:T(8,128)(2,1)} %param.11), kind=kOutput, calls=%fused_computation.19 | convolution fusion | flops 2415919104 | bytes 11796480 | tf_op jit(solution)/shard_map/dot_general | solution.py:177
  51.3 2.5 %fusion.18 = f32[32,3072]{1,0:T(8,128)S(1)} fusion(bf16[32,512]{1,0:T(8,128)(2,1)S(1)} %convert_element_type.304, f32[512,3072]{1,0:T(8,128)S(1)} %fusion.13), kind=kOutput, calls=%fused_computation.22 | convolution fusion | flops 114819072 | bytes 6717440 | tf_op jit(solution)/shard_map/dot_general | solution.py:180
  54.5 1.3 slice-done.1
  55.8 0.9 fusion.9
  56.7 0.9 fusion.29
  58.3 6.8 %all-to-all-start.1 = ((f32[16,2,768]{2,1,0:T(2,128)}), f32[16,2,768]{2,1,0:T(2,128)S(1)}, u32[]{:S(2)}, u32[]{:S(2)}) async-start(f32[16,2,768]{2,1,0:T(2,128)} %reshape.154), calls=%async_computation.1 | async-start | bytes 196608 | tf_op jit(solution)/shard_map/all_to_all | solution.py:182
  65.2 6.7 %all-to-all-done.1 = f32[16,2,768]{2,1,0:T(2,128)S(1)} async-done(((f32[16,2,768]{2,1,0:T(2,128)}), f32[16,2,768]{2,1,0:T(2,128)S(1)}, u32[]{:S(2)}, u32[]{:S(2)}) %all-to-all-start.1) | async-done | bytes 98336 | tf_op jit(solution)/shard_map/all_to_all | solution.py:182
  72.0 2.7 %multiply_reduce_fusion = f32[2048]{0:T(1024)S(1)} fusion(bf16[2048,768]{1,0:T(8,128)(2,1)} %all-gather.3.cloned.1.call-done), kind=kLoop, calls=%fused_computation.9 | loop fusion | flops 4716544 | bytes 3153920 | tf_op jit(solution)/shard_map/reduce_sum | solution.py:195
  75.0 1.0 fusion.83
  77.3 16.1 %all-gather = bf16[16,2,768]{2,1,0:T(2,128)(2,1)S(1)} all-gather(bf16[1,2,768]{2,1,0:T(2,128)(2,1)S(1)} %fusion.66), channel_id=1, replica_groups=mesh['dp'=16,'expert'=16] {'expert'}, dimensions={0}, use_global_device_ids=true | all-gather | bytes 52224 | tf_op jit(solution)/shard_map/all_gather | solution.py:212
  93.4 3.8 %fusion.15 = bf16[32,3072]{1,0:T(8,128)(2,1)S(1)} fusion(bf16[32,768]{1,0:T(8,128)(2,1)S(1)} %reshape.172, bf16[1,3072,768]{2,1,0:T(8,128)(2,1)} %param.12), kind=kOutput, calls=%fused_computation.21 | convolution fusion | flops 151093248 | bytes 4964352 | tf_op jit(solution)/shard_map/dot_general | solution.py:215
  97.2 3.7 %convolution_convert_fusion = bf16[3072,768]{1,0:T(8,128)(2,1)} fusion(bf16[32,768]{1,0:T(8,128)(2,1)S(1)} %reshape.172, f32[32,3072]{1,0:T(8,128)S(1)} %fusion.18), kind=kOutput, calls=%fused_computation.11 | convolution fusion | flops 153452544 | bytes 5160960 | tf_op jit(solution)/shard_map/dot_general | solution.py:225
  100.9 9.1 %convolution_convert_fusion.1 = bf16[768,3072]{1,0:T(8,128)(2,1)} fusion(bf16[512,768]{1,0:T(8,128)(2,1)S(1)} %bitcast.174, f32[512,3072]{1,0:T(8,128)} %copy-done.3, bf16[32,512]{1,0:T(8,128)(2,1)S(1)} %convert_element_type.304, bf16[32,3072]{1,0:T(8,128)(2,1)S(1)} %fusion.15), kind=kOutput, calls=%fused_computation.12 | convolution fusion | flops 2548826112 | bytes 12025856 | tf_op jit(solution)/shard_map/dot_general | solution.py:222
  110.0 3.0 %fusion.82 = (bf16[4,4,48,1536]{3,2,1,0:T(8,128)(2,1)S(1)}, bf16[4,4,48,1536]{3,2,1,0:T(8,128)(2,1)S(1)}) fusion(bf16[4,4,48,3072]{3,2,1,0:T(8,128)(2,1)} %bitcast.172), kind=kLoop, calls=%fused_computation.157 | loop fusion | bytes 9437184 | tf_op jit(solution)/shard_map/slice | solution.py:110
  113.1 1.6 collective-permute-start.6
  114.8 1.5 collective-permute-start
  116.4 0.8 fusion.81
  117.3 1.8 collective-permute-start.18
  119.1 1.8 collective-permute-start.12
  120.9 9.1 %collective-permute-done.6 = bf16[4,48,1536]{2,1,0:T(8,128)(2,1)S(1)} collective-permute-done((bf16[4,48,1536]{2,1,0:T(8,128)(2,1)S(1)}, bf16[4,48,1536]{2,1,0:T(8,128)(2,1)S(1)}, u32[]{:S(2)}, u32[]{:S(2)}) %collective-permute-start.6) | collective-permute-done | bytes 589856 | tf_op jit(solution)/shard_map/ppermute | solution.py:93
  130.6 0.8 collective-permute-done
  131.5 0.7 collective-permute-start.1
  132.5 3.1 %collective-permute-start.19 = (bf16[4,192,384]{2,1,0:T(8,128)(2,1)S(1)}, bf16[4,192,384]{2,1,0:T(8,128)(2,1)S(1)}, u32[]{:S(2)}, u32[]{:S(2)}) collective-permute-start(bf16[4,192,384]{2,1,0:T(8,128)(2,1)S(1)} %fusion.22), channel_id=1, source_target_pairs={{0,192},{16,208},{32,224},{48,240},{64,0},{80,16},{96,32},{112,48}... | collective-permute-start | bytes 1769480 | tf_op jit(solution)/shard_map/ppermute | solution.py:94
  135.8 2.1 %collective-permute-start.13 = (bf16[4,192,384]{2,1,0:T(8,128)(2,1)S(1)}, bf16[4,192,384]{2,1,0:T(8,128)(2,1)S(1)}, u32[]{:S(2)}, u32[]{:S(2)}) collective-permute-start(bf16[4,192,384]{2,1,0:T(8,128)(2,1)S(1)} %fusion.24), channel_id=1, source_target_pairs={{0,48},{16,0},{32,16},{48,32},{64,112},{80,64},{96,80},{112,96},{1... | collective-permute-start | bytes 1769480 | tf_op jit(solution)/shard_map/ppermute | solution.py:94
  137.9 8.4 %collective-permute-done.7 = bf16[4,48,1536]{2,1,0:T(8,128)(2,1)S(1)} collective-permute-done((bf16[4,48,1536]{2,1,0:T(8,128)(2,1)S(1)}, bf16[4,48,1536]{2,1,0:T(8,128)(2,1)S(1)}, u32[]{:S(2)}, u32[]{:S(2)}) %collective-permute-start.7) | collective-permute-done | bytes 589856 | tf_op jit(solution)/shard_map/ppermute | solution.py:93
  147.5 1.2 collective-permute-start.2
  148.8 3.3 %collective-permute-start.20 = (bf16[4,192,384]{2,1,0:T(8,128)(2,1)S(1)}, bf16[4,192,384]{2,1,0:T(8,128)(2,1)S(1)}, u32[]{:S(2)}, u32[]{:S(2)}) collective-permute-start(bf16[4,192,384]{2,1,0:T(8,128)(2,1)S(1)} %fusion.21), channel_id=1, source_target_pairs={{0,192},{16,208},{32,224},{48,240},{64,0},{80,16},{96,32},{112,48}... | collective-permute-start | bytes 1769480 | tf_op jit(solution)/shard_map/ppermute | solution.py:94
  152.3 1.7 collective-permute-start.14
  153.9 8.0 %collective-permute-done.8 = bf16[4,48,1536]{2,1,0:T(8,128)(2,1)S(1)} collective-permute-done((bf16[4,48,1536]{2,1,0:T(8,128)(2,1)S(1)}, bf16[4,48,1536]{2,1,0:T(8,128)(2,1)S(1)}, u32[]{:S(2)}, u32[]{:S(2)}) %collective-permute-start.8) | collective-permute-done | bytes 589856 | tf_op jit(solution)/shard_map/ppermute | solution.py:93
  162.1 1.8 collective-permute-start.9
  164.8 1.2 collective-permute-start.21
  166.5 3.0 %collective-permute-start.15 = (bf16[192,384]{1,0:T(8,128)(2,1)S(1)}, bf16[192,384]{1,0:T(8,128)(2,1)S(1)}, u32[]{:S(2)}, u32[]{:S(2)}) collective-permute-start(bf16[192,384]{1,0:T(8,128)(2,1)S(1)} %fusion.52), channel_id=1, source_target_pairs={{0,192},{16,208},{32,224},{48,240},{64,0},{80,16},{96,32},{112,48}... | collective-permute-start | bytes 442376 | tf_op jit(solution)/shard_map/ppermute | solution.py:94
  170.8 2.2 %collective-permute-start.22 = (bf16[192,384]{1,0:T(8,128)(2,1)S(1)}, bf16[192,384]{1,0:T(8,128)(2,1)S(1)}, u32[]{:S(2)}, u32[]{:S(2)}) collective-permute-start(bf16[192,384]{1,0:T(8,128)(2,1)S(1)} %fusion.37), channel_id=1, source_target_pairs={{0,48},{16,0},{32,16},{48,32},{64,112},{80,64},{96,80},{112,96},{1... | collective-permute-start | bytes 442376 | tf_op jit(solution)/shard_map/ppermute | solution.py:94
  173.1 3.3 %collective-permute-start.16 = (bf16[192,384]{1,0:T(8,128)(2,1)S(1)}, bf16[192,384]{1,0:T(8,128)(2,1)S(1)}, u32[]{:S(2)}, u32[]{:S(2)}) collective-permute-start(bf16[192,384]{1,0:T(8,128)(2,1)S(1)} %fusion.39), channel_id=1, source_target_pairs={{0,192},{16,208},{32,224},{48,240},{64,0},{80,16},{96,32},{112,48}... | collective-permute-start | bytes 442376 | tf_op jit(solution)/shard_map/ppermute | solution.py:94
  176.6 0.8 collective-permute-done.4
  177.7 2.3 %collective-permute-start.23 = (bf16[192,384]{1,0:T(8,128)(2,1)S(1)}, bf16[192,384]{1,0:T(8,128)(2,1)S(1)}, u32[]{:S(2)}, u32[]{:S(2)}) collective-permute-start(bf16[192,384]{1,0:T(8,128)(2,1)S(1)} %fusion.36), channel_id=1, source_target_pairs={{0,48},{16,0},{32,16},{48,32},{64,112},{80,64},{96,80},{112,96},{1... | collective-permute-start | bytes 442376 | tf_op jit(solution)/shard_map/ppermute | solution.py:94
  180.0 3.4 %collective-permute-start.17 = (bf16[192,384]{1,0:T(8,128)(2,1)S(1)}, bf16[192,384]{1,0:T(8,128)(2,1)S(1)}, u32[]{:S(2)}, u32[]{:S(2)}) collective-permute-start(bf16[192,384]{1,0:T(8,128)(2,1)S(1)} %fusion.38), channel_id=1, source_target_pairs={{0,192},{16,208},{32,224},{48,240},{64,0},{80,16},{96,32},{112,48}... | collective-permute-start | bytes 442376 | tf_op jit(solution)/shard_map/ppermute | solution.py:94
  184.0 0.9 maximum_bitcast_fusion
  184.9 1.2 collective-permute-done.17
  186.1 0.9 maximum_bitcast_fusion.1
  (120 shorter events, 14.2 us)
Async XLA Ops:
  7.2 3.7 %copy-start = (bf16[768,16]{0,1:T(8,128)(2,1)S(1)}, bf16[768,16]{0,1:T(8,128)(2,1)}, u32[]{:S(2)}) copy-start(bf16[768,16]{0,1:T(8,128)(2,1)} %param.10) | copy-start | bytes 73732
  7.2 64.8 %all-gather.3.cloned.1.call-start = ((), (), s32[]{:S(2)}) async-start(), calls=%async_computation.2 | async-start | bytes 3342336 | tf_op jit(solution)/shard_map/all_gather | solution.py:194
  14.4 10.7 %copy-start.5 = (s32[256,16]{0,1:T(8,128)S(1)}, s32[256,16]{0,1:T(8,128)}, u32[]{:S(2)}) copy-start(s32[256,16]{0,1:T(8,128)} %param.15) | copy-start | bytes 49156
  14.5 10.9 %copy-start.4 = (bf16[128,768]{1,0:T(8,128)(2,1)S(1)}, bf16[128,768]{1,0:T(8,128)(2,1)}, u32[]{:S(2)}) copy-start(bf16[128,768]{1,0:T(8,128)(2,1)} %param.8) | copy-start | bytes 589828
  15.8 30.4 %all-to-all-start = ((bf16[16,32,896]{2,1,0:T(8,128)(2,1)}), bf16[16,32,896]{2,1,0:T(8,128)(2,1)S(1)}, u32[]{:S(2)}, u32[]{:S(2)}) async-start(bf16[16,32,896]{2,1,0:T(8,128)(2,1)} %pad_maximum_fusion), calls=%async_computation | async-start | bytes 1835008 | tf_op jit(solution)/shard_map/all_to_all | solution.py:169
  46.8 7.8 %slice-start = ((s8[4718592]{0:T(1024)(128)(4,1)}), s8[524288]{0:T(1024)(128)(4,1)S(1)}, s32[]{:S(2)}) async-start(s8[4718592]{0:T(1024)(128)(4,1)} %bitcast.167), calls=%async_computation.3 | async-start | bytes 1048576
  51.3 3.2 %copy-start.3 = (f32[512,3072]{1,0:T(8,128)}, f32[512,3072]{1,0:T(8,128)S(1)}, u32[]{:S(2)}) copy-start(f32[512,3072]{1,0:T(8,128)S(1)} %fusion.13) | copy-start | bytes 18874372
  51.3 4.5 %slice-start.1 = ((s8[4718592]{0:T(1024)(128)(4,1)}), s8[4194304]{0:T(1024)(128)(4,1)S(1)}, s32[]{:S(2)}) async-start(s8[4718592]{0:T(1024)(128)(4,1)} %bitcast.167), calls=%async_computation.4 | async-start | bytes 8388608
  58.3 13.5 %all-to-all-start.1 = ((f32[16,2,768]{2,1,0:T(2,128)}), f32[16,2,768]{2,1,0:T(2,128)S(1)}, u32[]{:S(2)}, u32[]{:S(2)}) async-start(f32[16,2,768]{2,1,0:T(2,128)} %reshape.154), calls=%async_computation.1 | async-start | bytes 196608 | tf_op jit(solution)/shard_map/all_to_all | solution.py:182
  72.0 3.0 %copy-start.2 = (bf16[2048,768]{1,0:T(8,128)(2,1)S(1)}, bf16[2048,768]{1,0:T(8,128)(2,1)}, u32[]{:S(2)}) copy-start(bf16[2048,768]{1,0:T(8,128)(2,1)} %all-gather.3.cloned.1.call-done) | copy-start | bytes 9437188
  110.0 6.3 %slice-start.2 = ((s8[4718592]{0:T(1024)(128)(4,1)}), s8[4194304]{0:T(1024)(128)(4,1)S(1)}, s32[]{:S(2)}) async-start(s8[4718592]{0:T(1024)(128)(4,1)} %bitcast.169), calls=%async_computation.5 | async-start | bytes 8388608
  110.0 6.3 %slice-start.3 = ((s8[4718592]{0:T(1024)(128)(4,1)}), s8[524288]{0:T(1024)(128)(4,1)S(1)}, s32[]{:S(2)}) async-start(s8[4718592]{0:T(1024)(128)(4,1)} %bitcast.169), calls=%async_computation.6 | async-start | bytes 1048576
  113.1 16.9 %collective-permute-start.6 = (bf16[4,48,1536]{2,1,0:T(8,128)(2,1)S(1)}, bf16[4,48,1536]{2,1,0:T(8,128)(2,1)S(1)}, u32[]{:S(2)}, u32[]{:S(2)}) collective-permute-start(bf16[4,48,1536]{2,1,0:T(8,128)(2,1)S(1)} %dynamic-slice_bitcast_fusion.2), channel_id=1, source_target_pairs={{0,64},{16,80},{32,96},{48,112},{64,128},{80,144},{96,160},{112,17... | collective-permute-start | bytes 1769480 | tf_op jit(solution)/shard_map/ppermute | solution.py:93
  114.8 16.6 %collective-permute-start = (bf16[4,48,1536]{2,1,0:T(8,128)(2,1)S(1)}, bf16[4,48,1536]{2,1,0:T(8,128)(2,1)S(1)}, u32[]{:S(2)}, u32[]{:S(2)}) collective-permute-start(bf16[4,48,1536]{2,1,0:T(8,128)(2,1)S(1)} %dynamic-slice_bitcast_fusion.3), channel_id=1, source_target_pairs={{0,16},{16,32},{32,48},{48,0},{64,80},{80,96},{96,112},{112,64},{1... | collective-permute-start | bytes 1769480 | tf_op jit(solution)/shard_map/ppermute | solution.py:93
  117.3 15.1 %collective-permute-start.18 = (bf16[4,192,384]{2,1,0:T(8,128)(2,1)S(1)}, bf16[4,192,384]{2,1,0:T(8,128)(2,1)S(1)}, u32[]{:S(2)}, u32[]{:S(2)}) collective-permute-start(bf16[4,192,384]{2,1,0:T(8,128)(2,1)S(1)} %dynamic-slice_bitcast_fusion), channel_id=1, source_target_pairs={{0,192},{16,208},{32,224},{48,240},{64,0},{80,16},{96,32},{112,48}... | collective-permute-start | bytes 1769480 | tf_op jit(solution)/shard_map/ppermute | solution.py:94
  119.1 16.6 %collective-permute-start.12 = (bf16[4,192,384]{2,1,0:T(8,128)(2,1)S(1)}, bf16[4,192,384]{2,1,0:T(8,128)(2,1)S(1)}, u32[]{:S(2)}, u32[]{:S(2)}) collective-permute-start(bf16[4,192,384]{2,1,0:T(8,128)(2,1)S(1)} %dynamic-slice_bitcast_fusion.1), channel_id=1, source_target_pairs={{0,48},{16,0},{32,16},{48,32},{64,112},{80,64},{96,80},{112,96},{1... | collective-permute-start | bytes 1769480 | tf_op jit(solution)/shard_map/ppermute | solution.py:94
  130.2 16.1 %collective-permute-start.7 = (bf16[4,48,1536]{2,1,0:T(8,128)(2,1)S(1)}, bf16[4,48,1536]{2,1,0:T(8,128)(2,1)S(1)}, u32[]{:S(2)}, u32[]{:S(2)}) collective-permute-start(bf16[4,48,1536]{2,1,0:T(8,128)(2,1)S(1)} %fusion.26), channel_id=1, source_target_pairs={{0,64},{16,80},{32,96},{48,112},{64,128},{80,144},{96,160},{112,17... | collective-permute-start | bytes 1769480 | tf_op jit(solution)/shard_map/ppermute | solution.py:93
  131.5 15.7 %collective-permute-start.1 = (bf16[4,48,1536]{2,1,0:T(8,128)(2,1)S(1)}, bf16[4,48,1536]{2,1,0:T(8,128)(2,1)S(1)}, u32[]{:S(2)}, u32[]{:S(2)}) collective-permute-start(bf16[4,48,1536]{2,1,0:T(8,128)(2,1)S(1)} %fusion.28), channel_id=1, source_target_pairs={{0,16},{16,32},{32,48},{48,0},{64,80},{80,96},{96,112},{112,64},{1... | collective-permute-start | bytes 1769480 | tf_op jit(solution)/shard_map/ppermute | solution.py:93
  132.5 16.1 %collective-permute-start.19 = (bf16[4,192,384]{2,1,0:T(8,128)(2,1)S(1)}, bf16[4,192,384]{2,1,0:T(8,128)(2,1)S(1)}, u32[]{:S(2)}, u32[]{:S(2)}) collective-permute-start(bf16[4,192,384]{2,1,0:T(8,128)(2,1)S(1)} %fusion.22), channel_id=1, source_target_pairs={{0,192},{16,208},{32,224},{48,240},{64,0},{80,16},{96,32},{112,48}... | collective-permute-start | bytes 1769480 | tf_op jit(solution)/shard_map/ppermute | solution.py:94
  135.8 16.3 %collective-permute-start.13 = (bf16[4,192,384]{2,1,0:T(8,128)(2,1)S(1)}, bf16[4,192,384]{2,1,0:T(8,128)(2,1)S(1)}, u32[]{:S(2)}, u32[]{:S(2)}) collective-permute-start(bf16[4,192,384]{2,1,0:T(8,128)(2,1)S(1)} %fusion.24), channel_id=1, source_target_pairs={{0,48},{16,0},{32,16},{48,32},{64,112},{80,64},{96,80},{112,96},{1... | collective-permute-start | bytes 1769480 | tf_op jit(solution)/shard_map/ppermute | solution.py:94
  146.4 15.4 %collective-permute-start.8 = (bf16[4,48,1536]{2,1,0:T(8,128)(2,1)S(1)}, bf16[4,48,1536]{2,1,0:T(8,128)(2,1)S(1)}, u32[]{:S(2)}, u32[]{:S(2)}) collective-permute-start(bf16[4,48,1536]{2,1,0:T(8,128)(2,1)S(1)} %fusion.25), channel_id=1, source_target_pairs={{0,64},{16,80},{32,96},{48,112},{64,128},{80,144},{96,160},{112,17... | collective-permute-start | bytes 1769480 | tf_op jit(solution)/shard_map/ppermute | solution.py:93
  147.5 16.5 %collective-permute-start.2 = (bf16[4,48,1536]{2,1,0:T(8,128)(2,1)S(1)}, bf16[4,48,1536]{2,1,0:T(8,128)(2,1)S(1)}, u32[]{:S(2)}, u32[]{:S(2)}) collective-permute-start(bf16[4,48,1536]{2,1,0:T(8,128)(2,1)S(1)} %fusion.27), channel_id=1, source_target_pairs={{0,16},{16,32},{32,48},{48,0},{64,80},{80,96},{96,112},{112,64},{1... | collective-permute-start | bytes 1769480 | tf_op jit(solution)/shard_map/ppermute | solution.py:93
  148.8 15.8 %collective-permute-start.20 = (bf16[4,192,384]{2,1,0:T(8,128)(2,1)S(1)}, bf16[4,192,384]{2,1,0:T(8,128)(2,1)S(1)}, u32[]{:S(2)}, u32[]{:S(2)}) collective-permute-start(bf16[4,192,384]{2,1,0:T(8,128)(2,1)S(1)} %fusion.21), channel_id=1, source_target_pairs={{0,192},{16,208},{32,224},{48,240},{64,0},{80,16},{96,32},{112,48}... | collective-permute-start | bytes 1769480 | tf_op jit(solution)/shard_map/ppermute | solution.py:94
  152.3 14.0 %collective-permute-start.14 = (bf16[4,192,384]{2,1,0:T(8,128)(2,1)S(1)}, bf16[4,192,384]{2,1,0:T(8,128)(2,1)S(1)}, u32[]{:S(2)}, u32[]{:S(2)}) collective-permute-start(bf16[4,192,384]{2,1,0:T(8,128)(2,1)S(1)} %fusion.23), channel_id=1, source_target_pairs={{0,48},{16,0},{32,16},{48,32},{64,112},{80,64},{96,80},{112,96},{1... | collective-permute-start | bytes 1769480 | tf_op jit(solution)/shard_map/ppermute | solution.py:94
  162.1 7.3 %collective-permute-start.9 = (bf16[48,1536]{1,0:T(8,128)(2,1)S(1)}, bf16[48,1536]{1,0:T(8,128)(2,1)S(1)}, u32[]{:S(2)}, u32[]{:S(2)}) collective-permute-start(bf16[48,1536]{1,0:T(8,128)(2,1)S(1)} %fusion.51), channel_id=1, source_target_pairs={{0,16},{16,32},{32,48},{48,0},{64,80},{80,96},{96,112},{112,64},{1... | collective-permute-start | bytes 442376 | tf_op jit(solution)/shard_map/ppermute | solution.py:93
  164.1 6.4 %collective-permute-start.3 = (bf16[48,1536]{1,0:T(8,128)(2,1)S(1)}, bf16[48,1536]{1,0:T(8,128)(2,1)S(1)}, u32[]{:S(2)}, u32[]{:S(2)}) collective-permute-start(bf16[48,1536]{1,0:T(8,128)(2,1)S(1)} %fusion.50), channel_id=1, source_target_pairs={{0,64},{16,80},{32,96},{48,112},{64,128},{80,144},{96,160},{112,17... | collective-permute-start | bytes 442376 | tf_op jit(solution)/shard_map/ppermute | solution.py:93
  164.8 6.0 %collective-permute-start.21 = (bf16[192,384]{1,0:T(8,128)(2,1)S(1)}, bf16[192,384]{1,0:T(8,128)(2,1)S(1)}, u32[]{:S(2)}, u32[]{:S(2)}) collective-permute-start(bf16[192,384]{1,0:T(8,128)(2,1)S(1)} %fusion.53), channel_id=1, source_target_pairs={{0,48},{16,0},{32,16},{48,32},{64,112},{80,64},{96,80},{112,96},{1... | collective-permute-start | bytes 442376 | tf_op jit(solution)/shard_map/ppermute | solution.py:94
  166.5 6.6 %collective-permute-start.15 = (bf16[192,384]{1,0:T(8,128)(2,1)S(1)}, bf16[192,384]{1,0:T(8,128)(2,1)S(1)}, u32[]{:S(2)}, u32[]{:S(2)}) collective-permute-start(bf16[192,384]{1,0:T(8,128)(2,1)S(1)} %fusion.52), channel_id=1, source_target_pairs={{0,192},{16,208},{32,224},{48,240},{64,0},{80,16},{96,32},{112,48}... | collective-permute-start | bytes 442376 | tf_op jit(solution)/shard_map/ppermute | solution.py:94
  169.5 6.9 %collective-permute-start.10 = (bf16[48,1536]{1,0:T(8,128)(2,1)S(1)}, bf16[48,1536]{1,0:T(8,128)(2,1)S(1)}, u32[]{:S(2)}, u32[]{:S(2)}) collective-permute-start(bf16[48,1536]{1,0:T(8,128)(2,1)S(1)} %fusion.41), channel_id=1, source_target_pairs={{0,16},{16,32},{32,48},{48,0},{64,80},{80,96},{96,112},{112,64},{1... | collective-permute-start | bytes 442376 | tf_op jit(solution)/shard_map/ppermute | solution.py:93
  170.6 6.9 %collective-permute-start.4 = (bf16[48,1536]{1,0:T(8,128)(2,1)S(1)}, bf16[48,1536]{1,0:T(8,128)(2,1)S(1)}, u32[]{:S(2)}, u32[]{:S(2)}) collective-permute-start(bf16[48,1536]{1,0:T(8,128)(2,1)S(1)} %fusion.43), channel_id=1, source_target_pairs={{0,64},{16,80},{32,96},{48,112},{64,128},{80,144},{96,160},{112,17... | collective-permute-start | bytes 442376 | tf_op jit(solution)/shard_map/ppermute | solution.py:93
  170.8 6.8 %collective-permute-start.22 = (bf16[192,384]{1,0:T(8,128)(2,1)S(1)}, bf16[192,384]{1,0:T(8,128)(2,1)S(1)}, u32[]{:S(2)}, u32[]{:S(2)}) collective-permute-start(bf16[192,384]{1,0:T(8,128)(2,1)S(1)} %fusion.37), channel_id=1, source_target_pairs={{0,48},{16,0},{32,16},{48,32},{64,112},{80,64},{96,80},{112,96},{1... | collective-permute-start | bytes 442376 | tf_op jit(solution)/shard_map/ppermute | solution.py:94
  173.1 6.9 %collective-permute-start.16 = (bf16[192,384]{1,0:T(8,128)(2,1)S(1)}, bf16[192,384]{1,0:T(8,128)(2,1)S(1)}, u32[]{:S(2)}, u32[]{:S(2)}) collective-permute-start(bf16[192,384]{1,0:T(8,128)(2,1)S(1)} %fusion.39), channel_id=1, source_target_pairs={{0,192},{16,208},{32,224},{48,240},{64,0},{80,16},{96,32},{112,48}... | collective-permute-start | bytes 442376 | tf_op jit(solution)/shard_map/ppermute | solution.py:94
  176.4 7.0 %collective-permute-start.11 = (bf16[48,1536]{1,0:T(8,128)(2,1)S(1)}, bf16[48,1536]{1,0:T(8,128)(2,1)S(1)}, u32[]{:S(2)}, u32[]{:S(2)}) collective-permute-start(bf16[48,1536]{1,0:T(8,128)(2,1)S(1)} %fusion.40), channel_id=1, source_target_pairs={{0,16},{16,32},{32,48},{48,0},{64,80},{80,96},{96,112},{112,64},{1... | collective-permute-start | bytes 442376 | tf_op jit(solution)/shard_map/ppermute | solution.py:93
  177.5 9.5 %copy-start.1 = (bf16[768,16]{0,1:T(8,128)(2,1)S(1)}, bf16[768,16]{0,1:T(8,128)(2,1)}, u32[]{:S(2)}) copy-start(bf16[768,16]{0,1:T(8,128)(2,1)} %param.10) | copy-start | bytes 73732
  177.5 6.4 %collective-permute-start.5 = (bf16[48,1536]{1,0:T(8,128)(2,1)S(1)}, bf16[48,1536]{1,0:T(8,128)(2,1)S(1)}, u32[]{:S(2)}, u32[]{:S(2)}) collective-permute-start(bf16[48,1536]{1,0:T(8,128)(2,1)S(1)} %fusion.42), channel_id=1, source_target_pairs={{0,64},{16,80},{32,96},{48,112},{64,128},{80,144},{96,160},{112,17... | collective-permute-start | bytes 442376 | tf_op jit(solution)/shard_map/ppermute | solution.py:93
  177.7 7.2 %collective-permute-start.23 = (bf16[192,384]{1,0:T(8,128)(2,1)S(1)}, bf16[192,384]{1,0:T(8,128)(2,1)S(1)}, u32[]{:S(2)}, u32[]{:S(2)}) collective-permute-start(bf16[192,384]{1,0:T(8,128)(2,1)S(1)} %fusion.36), channel_id=1, source_target_pairs={{0,48},{16,0},{32,16},{48,32},{64,112},{80,64},{96,80},{112,96},{1... | collective-permute-start | bytes 442376 | tf_op jit(solution)/shard_map/ppermute | solution.py:94
  180.0 6.0 %collective-permute-start.17 = (bf16[192,384]{1,0:T(8,128)(2,1)S(1)}, bf16[192,384]{1,0:T(8,128)(2,1)S(1)}, u32[]{:S(2)}, u32[]{:S(2)}) collective-permute-start(bf16[192,384]{1,0:T(8,128)(2,1)S(1)} %fusion.38), channel_id=1, source_target_pairs={{0,192},{16,208},{32,224},{48,240},{64,0},{80,16},{96,32},{112,48}... | collective-permute-start | bytes 442376 | tf_op jit(solution)/shard_map/ppermute | solution.py:94
Sparse Core Ops, SparseCore 0:
  10.4 55.4 all-gather.2
where the time goes:
time: 196 us; the launch traced here: 194 us
  waiting for transfers between devices  58.5 us (30%)
  starting transfers between devices  53.7 us (27%)
  matrix products  30.3 us (15%)
  blocking collectives  16.1 us (8%)
  between operations  14.5 us (7%)
  other arithmetic  10.9 us (6%)
  local copies, waits for them, and re-layouts  9.84 us (5%)
    ppermute x12, starting transfers between devices, ring_step(): got_b = lax.ppermute(state['acc_b'].astype(jnp.bfloat16), 'dp', bwd_pairs)  29.2 us
    ppermute x12, waiting for transfers between devices, ring_step(): got_f = lax.ppermute(state['acc_f'].astype(jnp.bfloat16), 'dp', fwd_pairs)  28.7 us
    all_to_all x1, waiting for transfers between devices, on_device(): lax.all_to_all(outgoing, 'expert', split_axis=0, concat_axis=0, tiled=True)  20.8 us
    all_gather x1, blocking collectives, on_device(): delta_row = lax.all_gather(delta_seq, 'expert', axis=0, tiled=True)  16.1 us
    ppermute x12, starting transfers between devices, ring_step(): got_f = lax.ppermute(state['acc_f'].astype(jnp.bfloat16), 'dp', fwd_pairs)  9.14 us
    dot_general x1, matrix products, on_device(): lax.dot_general(input_flat, delta_pre, dims_t, preferred_element_type=jnp...  9.14 us
    all_to_all x1, starting transfers between devices, on_device(): lax.all_to_all(outgoing, 'expert', split_axis=0, concat_axis=0, tiled=True)  8.59 us
    all_to_all x1, starting transfers between devices, on_device(): lax.all_to_all(moe_seq.reshape(expert_size, seq_count, model_width), 'exp...  6.8 us
  transfers between devices with their start and end apart: 27, of which 13 were waited for; matrix products, arithmetic and copies ran while one was open for 12% of the time, Pallas kernels for 0%

commit v1 on v0

--- a/solution.py
+++ b/solution.py
@@ -78,23 +78,23 @@
     return pairs
 
 
-def take_chunk(chunks, index, count):
-    return lax.dynamic_index_in_dim(chunks, lax.rem(index + 2 * count, count), 0, keepdims=False)
-
-
-def ring_start(fwd, bwd, count, pos):
-    return dict(fwd=fwd, bwd=bwd, count=count, pos=pos,
-                acc_f=take_chunk(fwd, pos - 1, count).astype(jnp.float32),
-                acc_b=take_chunk(bwd, pos + 1, count).astype(jnp.float32))
+def take_chunk(chunks, index, count, axis=0):
+    return lax.dynamic_index_in_dim(chunks, lax.rem(index + 2 * count, count), axis, keepdims=False)
+
+
+def ring_start(fwd, bwd, count, pos, axis=0):
+    return dict(fwd=fwd, bwd=bwd, count=count, pos=pos, axis=axis,
+                acc_f=take_chunk(fwd, pos - 1, count, axis).astype(jnp.float32),
+                acc_b=take_chunk(bwd, pos + 1, count, axis).astype(jnp.float32))
 
 
 def ring_step(state, k, fwd_pairs, bwd_pairs):
-    count, pos = state["count"], state["pos"]
+    count, pos, axis = state["count"], state["pos"], state["axis"]
     got_f = lax.ppermute(state["acc_f"].astype(jnp.bfloat16), "dp", fwd_pairs)
     got_b = lax.ppermute(state["acc_b"].astype(jnp.bfloat16), "dp", bwd_pairs)
     state = dict(state)
-    state["acc_f"] = got_f.astype(jnp.float32) + take_chunk(state["fwd"], pos - 2 - k, count).astype(jnp.float32)
-    state["acc_b"] = got_b.astype(jnp.float32) + take_chunk(state["bwd"], pos + 2 + k, count).astype(jnp.float32)
+    state["acc_f"] = got_f.astype(jnp.float32) + take_chunk(state["fwd"], pos - 2 - k, count, axis).astype(jnp.float32)
+    state["acc_b"] = got_b.astype(jnp.float32) + take_chunk(state["bwd"], pos + 2 + k, count, axis).astype(jnp.float32)
     return state
 
 
@@ -107,8 +107,7 @@
     hin, hout = gin.shape[-1] // 2, gout.shape[-1] // 2
     x_f, x_b = ring_pairs(nx, ny, True, 1), ring_pairs(nx, ny, True, -1)
     y_f, y_b = ring_pairs(nx, ny, False, 1), ring_pairs(nx, ny, False, -1)
-    ra = ring_start(jnp.transpose(gin[..., :hin], (1, 0, 2, 3)),
-                    jnp.transpose(gout[..., :hout], (1, 0, 2, 3)), nx, x_pos)
+    ra = ring_start(gin[..., :hin], gout[..., :hout], nx, x_pos, axis=1)
     rb = ring_start(gin[..., hin:], gout[..., hout:], ny, y_pos)
     for k in range(max(nx, ny) - 1):
         if k < nx - 1:
@@ -212,13 +211,14 @@
     delta_row = lax.all_gather(delta_seq, "expert", axis=0, tiled=True)
 
     dims_t = (((0,), (0,)), ((), ()))
-    spread = lax.dot_general(
-        delta_row, weight_out[0], (((1,), (1,)), ((), ())), preferred_element_type=jnp.float32
+    spread_t = lax.dot_general(
+        weight_out[0], delta_row, (((1,), (1,)), ((), ())), preferred_element_type=jnp.float32
     ).astype(jnp.bfloat16)
     dhidden = lax.dot_general(
-        sel_gate.astype(jnp.bfloat16), spread, dims_t, preferred_element_type=jnp.float32
-    )
-    delta_pre = (dhidden * slope_flat).astype(jnp.bfloat16)
+        sel_gate.astype(jnp.bfloat16), spread_t, (((0,), (1,)), ((), ())),
+        preferred_element_type=jnp.float32,
+    )
+    delta_pre = lax.optimization_barrier((dhidden * slope_flat).astype(jnp.bfloat16))
     grad_in_term = lax.dot_general(
         input_flat, delta_pre, dims_t, preferred_element_type=jnp.float32
     ).astype(jnp.bfloat16)

time: 196 us -> 191 us (0.974)
  matrix products: 30.3 us -> 27.3 us
    dot_general x1, matrix products: 9.14 us -> 2.88 us  [on_device(): lax.dot_general(input_flat, delta_pre, dims_t, preferred_element_type=jnp...]
    dot_general x1, matrix products: 3.79 us -> 9.36 us  [on_device(): lax.dot_general(sel_gate.astype(jnp.bfloat16), spread_t, (((0,), (1,)), (...]
    slice x3, local copies, waits for them, and re-layouts: 4.03 us -> 1.65 us  [the longest x2 1.46 us: reduce_scatter_2d(): ra = ring_start(gin[..., :hin], gout[..., :hout], nx, x_pos, axis=1)]
    dot_general x1, matrix products: 3.69 us -> 1.43 us  [on_device(): lax.dot_general(seq_hidden.astype(jnp.bfloat16), delta_row, dims_t, prefe...]
where the time goes in v1:
time: 191 us; the launch traced here: 189 us
  waiting for transfers between devices  58.5 us (31%)
  starting transfers between devices  53.7 us (28%)
  matrix products  27.3 us (14%)
  blocking collectives  16.1 us (8%)
  between operations  14.5 us (8%)
  other arithmetic  10.9 us (6%)
  local copies, waits for them, and re-layouts  7.9 us (4%)
    ppermute x12, starting transfers between devices, ring_step(): got_b = lax.ppermute(state['acc_b'].astype(jnp.bfloat16), 'dp', bwd_pairs)  28.6 us
    ppermute x12, waiting for transfers between devices, ring_step(): got_f = lax.ppermute(state['acc_f'].astype(jnp.bfloat16), 'dp', fwd_pairs)  28.5 us
    all_to_all x1, waiting for transfers between devices, on_device(): lax.all_to_all(outgoing, 'expert', split_axis=0, concat_axis=0, tiled=True)  20.8 us
    all_gather x1, blocking collectives, on_device(): delta_row = lax.all_gather(delta_seq, 'expert', axis=0, tiled=True)  16.1 us
    ppermute x12, starting transfers between devices, ring_step(): got_f = lax.ppermute(state['acc_f'].astype(jnp.bfloat16), 'dp', fwd_pairs)  9.61 us
    dot_general x1, matrix products, on_device(): lax.dot_general(sel_gate.astype(jnp.bfloat16), spread_t, (((0,), (1,)), (...  9.36 us
    all_to_all x1, starting transfers between devices, on_device(): lax.all_to_all(outgoing, 'expert', split_axis=0, concat_axis=0, tiled=True)  8.59 us
    all_to_all x1, starting transfers between devices, on_device(): lax.all_to_all(moe_seq.reshape(expert_size, seq_count, model_width), 'exp...  6.8 us
  transfers between devices with their start and end apart: 27, of which 13 were waited for; matrix products, arithmetic and copies ran while one was open for 12% of the time, Pallas kernels for 0%

profile of v1, /device:TPU:32, one launch (start us, length us, event | category | flops | bytes accessed | tf_op | source)
XLA Modules:
  0.0 188.9 jit_solution(14430622999055500313)
XLA Ops:
  7.9 0.8 copy.66
  10.8 1.0 fusion.81
  11.9 0.8 select_reduce_fusion.1
  13.1 1.3 fusion.48
  14.8 1.0 pad_maximum_fusion
  15.8 8.6 %all-to-all-start = ((bf16[16,32,896]{2,1,0:T(8,128)(2,1)}), bf16[16,32,896]{2,1,0:T(8,128)(2,1)S(1)}, u32[]{:S(2)}, u32[]{:S(2)}) async-start(bf16[16,32,896]{2,1,0:T(8,128)(2,1)} %pad_maximum_fusion), calls=%async_computation | async-start | bytes 1835008 | tf_op jit(solution)/shard_map/all_to_all | solution.py:168
  24.4 0.8 dynamic_slice.110
  25.4 20.8 %all-to-all-done = bf16[16,32,896]{2,1,0:T(8,128)(2,1)S(1)} async-done(((bf16[16,32,896]{2,1,0:T(8,128)(2,1)}), bf16[16,32,896]{2,1,0:T(8,128)(2,1)S(1)}, u32[]{:S(2)}, u32[]{:S(2)}) %all-to-all-start) | async-done | bytes 917536 | tf_op jit(solution)/shard_map/all_to_all | solution.py:168
  46.8 4.5 %fusion.13 = f32[512,3072]{1,0:T(8,128)S(1)} fusion(bf16[512,768]{1,0:T(8,128)(2,1)S(1)} %bitcast.173, bf16[1,768,3072]{2,1,0:T(8,128)(2,1)} %param.11), kind=kOutput, calls=%fused_computation.19 | convolution fusion | flops 2415919104 | bytes 11796480 | tf_op jit(solution)/shard_map/dot_general | solution.py:176
  51.3 2.5 %fusion.18 = f32[32,3072]{1,0:T(8,128)S(1)} fusion(bf16[32,512]{1,0:T(8,128)(2,1)S(1)} %convert_element_type.305, f32[512,3072]{1,0:T(8,128)S(1)} %fusion.13), kind=kOutput, calls=%fused_computation.22 | convolution fusion | flops 114819072 | bytes 6717440 | tf_op jit(solution)/shard_map/dot_general | solution.py:179
  54.5 1.3 slice-done.1
  55.8 0.9 fusion.9
  56.7 0.9 fusion.31
  58.3 6.8 %all-to-all-start.1 = ((f32[16,2,768]{2,1,0:T(2,128)}), f32[16,2,768]{2,1,0:T(2,128)S(1)}, u32[]{:S(2)}, u32[]{:S(2)}) async-start(f32[16,2,768]{2,1,0:T(2,128)} %reshape.138), calls=%async_computation.1 | async-start | bytes 196608 | tf_op jit(solution)/shard_map/all_to_all | solution.py:181
  65.2 6.7 %all-to-all-done.1 = f32[16,2,768]{2,1,0:T(2,128)S(1)} async-done(((f32[16,2,768]{2,1,0:T(2,128)}), f32[16,2,768]{2,1,0:T(2,128)S(1)}, u32[]{:S(2)}, u32[]{:S(2)}) %all-to-all-start.1) | async-done | bytes 98336 | tf_op jit(solution)/shard_map/all_to_all | solution.py:181
  72.0 2.7 %multiply_reduce_fusion = f32[2048]{0:T(1024)S(1)} fusion(bf16[2048,768]{1,0:T(8,128)(2,1)} %all-gather.3.cloned.1.call-done), kind=kLoop, calls=%fused_computation.9 | loop fusion | flops 4716544 | bytes 3153920 | tf_op jit(solution)/shard_map/reduce_sum | solution.py:194
  75.0 1.0 fusion.80
  77.3 16.1 %all-gather = bf16[16,2,768]{2,1,0:T(2,128)(2,1)S(1)} all-gather(bf16[1,2,768]{2,1,0:T(2,128)(2,1)S(1)} %fusion.68), channel_id=1, replica_groups=mesh['dp'=16,'expert'=16] {'expert'}, dimensions={0}, use_global_device_ids=true | all-gather | bytes 52224 | tf_op jit(solution)/shard_map/all_gather | solution.py:211
  93.4 9.4 %fusion.6 = bf16[512,3072]{1,0:T(8,128)(2,1)} fusion(f32[512,3072]{1,0:T(8,128)} %copy-done.3, bf16[32,512]{1,0:T(8,128)(2,1)S(1)} %convert_element_type.305, bf16[32,768]{1,0:T(8,128)(2,1)S(1)} %reshape.156, bf16[1,3072,768]{2,1,0:T(8,128)(2,1)} %param.12), kind=kOutput, calls=%fused_computation.8 | convolution fusion | flops 281640960 | bytes 14237696 | tf_op jit(solution)/shard_map/dot_general | solution.py:217
  102.8 1.4 convolution_convert_fusion
  104.7 2.9 %convolution_convert_fusion.1 = bf16[768,3072]{1,0:T(8,128)(2,1)S(1)} fusion(bf16[512,768]{1,0:T(8,128)(2,1)S(1)} %bitcast.174, bf16[512,3072]{1,0:T(8,128)(2,1)S(1)} %copy-done.6), kind=kOutput, calls=%fused_computation.12 | convolution fusion | flops 2418278400 | bytes 8650752 | tf_op jit(solution)/shard_map/dot_general | solution.py:222
  108.2 1.6 collective-permute-start.6
  109.9 1.5 collective-permute-start
  111.5 0.8 fusion.78
  112.4 1.8 collective-permute-start.18
  114.2 1.8 collective-permute-start.12
  116.1 9.1 %collective-permute-done.6 = bf16[4,48,1536]{2,1,0:T(8,128)(2,1)S(1)} collective-permute-done((bf16[4,48,1536]{2,1,0:T(8,128)(2,1)S(1)}, bf16[4,48,1536]{2,1,0:T(8,128)(2,1)S(1)}, u32[]{:S(2)}, u32[]{:S(2)}) %collective-permute-start.6) | collective-permute-done | bytes 589856 | tf_op jit(solution)/shard_map/ppermute | solution.py:93
  125.7 0.8 collective-permute-done
  126.7 0.7 collective-permute-start.1
  127.6 3.3 %collective-permute-start.19 = (bf16[4,192,384]{2,1,0:T(8,128)(2,1)S(1)}, bf16[4,192,384]{2,1,0:T(8,128)(2,1)S(1)}, u32[]{:S(2)}, u32[]{:S(2)}) collective-permute-start(bf16[4,192,384]{2,1,0:T(8,128)(2,1)S(1)} %fusion.22), channel_id=1, source_target_pairs={{0,192},{16,208},{32,224},{48,240},{64,0},{80,16},{96,32},{112,48}... | collective-permute-start | bytes 1769480 | tf_op jit(solution)/shard_map/ppermute | solution.py:94
  131.2 1.7 collective-permute-start.13
  132.9 8.5 %collective-permute-done.7 = bf16[4,48,1536]{2,1,0:T(8,128)(2,1)S(1)} collective-permute-done((bf16[4,48,1536]{2,1,0:T(8,128)(2,1)S(1)}, bf16[4,48,1536]{2,1,0:T(8,128)(2,1)S(1)}, u32[]{:S(2)}, u32[]{:S(2)}) %collective-permute-start.7) | collective-permute-done | bytes 589856 | tf_op jit(solution)/shard_map/ppermute | solution.py:93
  141.6 0.7 collective-permute-done.1
  142.6 1.0 collective-permute-start.2
  143.7 3.3 %collective-permute-start.20 = (bf16[4,192,384]{2,1,0:T(8,128)(2,1)S(1)}, bf16[4,192,384]{2,1,0:T(8,128)(2,1)S(1)}, u32[]{:S(2)}, u32[]{:S(2)}) collective-permute-start(bf16[4,192,384]{2,1,0:T(8,128)(2,1)S(1)} %fusion.21), channel_id=1, source_target_pairs={{0,192},{16,208},{32,224},{48,240},{64,0},{80,16},{96,32},{112,48}... | collective-permute-start | bytes 1769480 | tf_op jit(solution)/shard_map/ppermute | solution.py:94
  147.2 1.7 collective-permute-start.14
  148.8 7.9 %collective-permute-done.8 = bf16[4,48,1536]{2,1,0:T(8,128)(2,1)S(1)} collective-permute-done((bf16[4,48,1536]{2,1,0:T(8,128)(2,1)S(1)}, bf16[4,48,1536]{2,1,0:T(8,128)(2,1)S(1)}, u32[]{:S(2)}, u32[]{:S(2)}) %collective-permute-start.8) | collective-permute-done | bytes 589856 | tf_op jit(solution)/shard_map/ppermute | solution.py:93
  157.0 1.8 collective-permute-start.9
  159.0 0.8 collective-permute-start.3
  160.0 0.8 collective-permute-start.21
  161.4 3.0 %collective-permute-start.15 = (bf16[192,384]{1,0:T(8,128)(2,1)S(1)}, bf16[192,384]{1,0:T(8,128)(2,1)S(1)}, u32[]{:S(2)}, u32[]{:S(2)}) collective-permute-start(bf16[192,384]{1,0:T(8,128)(2,1)S(1)} %fusion.54), channel_id=1, source_target_pairs={{0,192},{16,208},{32,224},{48,240},{64,0},{80,16},{96,32},{112,48}... | collective-permute-start | bytes 442376 | tf_op jit(solution)/shard_map/ppermute | solution.py:94
  165.9 2.0 %collective-permute-start.22 = (bf16[192,384]{1,0:T(8,128)(2,1)S(1)}, bf16[192,384]{1,0:T(8,128)(2,1)S(1)}, u32[]{:S(2)}, u32[]{:S(2)}) collective-permute-start(bf16[192,384]{1,0:T(8,128)(2,1)S(1)} %fusion.39), channel_id=1, source_target_pairs={{0,48},{16,0},{32,16},{48,32},{64,112},{80,64},{96,80},{112,96},{1... | collective-permute-start | bytes 442376 | tf_op jit(solution)/shard_map/ppermute | solution.py:94
  168.0 3.3 %collective-permute-start.16 = (bf16[192,384]{1,0:T(8,128)(2,1)S(1)}, bf16[192,384]{1,0:T(8,128)(2,1)S(1)}, u32[]{:S(2)}, u32[]{:S(2)}) collective-permute-start(bf16[192,384]{1,0:T(8,128)(2,1)S(1)} %fusion.41), channel_id=1, source_target_pairs={{0,192},{16,208},{32,224},{48,240},{64,0},{80,16},{96,32},{112,48}... | collective-permute-start | bytes 442376 | tf_op jit(solution)/shard_map/ppermute | solution.py:94
  172.5 2.6 %collective-permute-start.23 = (bf16[192,384]{1,0:T(8,128)(2,1)S(1)}, bf16[192,384]{1,0:T(8,128)(2,1)S(1)}, u32[]{:S(2)}, u32[]{:S(2)}) collective-permute-start(bf16[192,384]{1,0:T(8,128)(2,1)S(1)} %fusion.38), channel_id=1, source_target_pairs={{0,48},{16,0},{32,16},{48,32},{64,112},{80,64},{96,80},{112,96},{1... | collective-permute-start | bytes 442376 | tf_op jit(solution)/shard_map/ppermute | solution.py:94
  175.2 3.3 %collective-permute-start.17 = (bf16[192,384]{1,0:T(8,128)(2,1)S(1)}, bf16[192,384]{1,0:T(8,128)(2,1)S(1)}, u32[]{:S(2)}, u32[]{:S(2)}) collective-permute-start(bf16[192,384]{1,0:T(8,128)(2,1)S(1)} %fusion.40), channel_id=1, source_target_pairs={{0,192},{16,208},{32,224},{48,240},{64,0},{80,16},{96,32},{112,48}... | collective-permute-start | bytes 442376 | tf_op jit(solution)/shard_map/ppermute | solution.py:94
  178.8 0.9 maximum_bitcast_fusion
  179.7 1.4 collective-permute-done.17
  181.2 0.9 maximum_bitcast_fusion.1
  (117 shorter events, 14.9 us)
Async XLA Ops:
  7.2 3.7 %copy-start = (bf16[768,16]{0,1:T(8,128)(2,1)S(1)}, bf16[768,16]{0,1:T(8,128)(2,1)}, u32[]{:S(2)}) copy-start(bf16[768,16]{0,1:T(8,128)(2,1)} %param.10) | copy-start | bytes 73732
  7.2 64.8 %all-gather.3.cloned.1.call-start = ((), (), s32[]{:S(2)}) async-start(), calls=%async_computation.2 | async-start | bytes 3342336 | tf_op jit(solution)/shard_map/all_gather | solution.py:193
  14.4 10.7 %copy-start.5 = (s32[256,16]{0,1:T(8,128)S(1)}, s32[256,16]{0,1:T(8,128)}, u32[]{:S(2)}) copy-start(s32[256,16]{0,1:T(8,128)} %param.15) | copy-start | bytes 49156
  14.5 10.9 %copy-start.4 = (bf16[128,768]{1,0:T(8,128)(2,1)S(1)}, bf16[128,768]{1,0:T(8,128)(2,1)}, u32[]{:S(2)}) copy-start(bf16[128,768]{1,0:T(8,128)(2,1)} %param.8) | copy-start | bytes 589828
  15.8 30.4 %all-to-all-start = ((bf16[16,32,896]{2,1,0:T(8,128)(2,1)}), bf16[16,32,896]{2,1,0:T(8,128)(2,1)S(1)}, u32[]{:S(2)}, u32[]{:S(2)}) async-start(bf16[16,32,896]{2,1,0:T(8,128)(2,1)} %pad_maximum_fusion), calls=%async_computation | async-start | bytes 1835008 | tf_op jit(solution)/shard_map/all_to_all | solution.py:168
  46.7 7.8 %slice-start = ((s8[4718592]{0:T(1024)(128)(4,1)}), s8[524288]{0:T(1024)(128)(4,1)S(1)}, s32[]{:S(2)}) async-start(s8[4718592]{0:T(1024)(128)(4,1)} %bitcast.169), calls=%async_computation.3 | async-start | bytes 1048576
  51.3 3.2 %copy-start.3 = (f32[512,3072]{1,0:T(8,128)}, f32[512,3072]{1,0:T(8,128)S(1)}, u32[]{:S(2)}) copy-start(f32[512,3072]{1,0:T(8,128)S(1)} %fusion.13) | copy-start | bytes 18874372
  51.3 4.5 %slice-start.1 = ((s8[4718592]{0:T(1024)(128)(4,1)}), s8[4194304]{0:T(1024)(128)(4,1)S(1)}, s32[]{:S(2)}) async-start(s8[4718592]{0:T(1024)(128)(4,1)} %bitcast.169), calls=%async_computation.4 | async-start | bytes 8388608
  58.3 13.5 %all-to-all-start.1 = ((f32[16,2,768]{2,1,0:T(2,128)}), f32[16,2,768]{2,1,0:T(2,128)S(1)}, u32[]{:S(2)}, u32[]{:S(2)}) async-start(f32[16,2,768]{2,1,0:T(2,128)} %reshape.138), calls=%async_computation.1 | async-start | bytes 196608 | tf_op jit(solution)/shard_map/all_to_all | solution.py:181
  72.0 3.0 %copy-start.2 = (bf16[2048,768]{1,0:T(8,128)(2,1)S(1)}, bf16[2048,768]{1,0:T(8,128)(2,1)}, u32[]{:S(2)}) copy-start(bf16[2048,768]{1,0:T(8,128)(2,1)} %all-gather.3.cloned.1.call-done) | copy-start | bytes 9437188
  102.8 1.9 %copy-start.6 = (bf16[512,3072]{1,0:T(8,128)(2,1)S(1)}, bf16[512,3072]{1,0:T(8,128)(2,1)}, u32[]{:S(2)}) copy-start(bf16[512,3072]{1,0:T(8,128)(2,1)} %fusion.6) | copy-start | bytes 9437188
  108.2 16.9 %collective-permute-start.6 = (bf16[4,48,1536]{2,1,0:T(8,128)(2,1)S(1)}, bf16[4,48,1536]{2,1,0:T(8,128)(2,1)S(1)}, u32[]{:S(2)}, u32[]{:S(2)}) collective-permute-start(bf16[4,48,1536]{2,1,0:T(8,128)(2,1)S(1)} %dynamic-slice_bitcast_fusion.2), channel_id=1, source_target_pairs={{0,64},{16,80},{32,96},{48,112},{64,128},{80,144},{96,160},{112,17... | collective-permute-start | bytes 1769480 | tf_op jit(solution)/shard_map/ppermute | solution.py:93
  109.9 16.6 %collective-permute-start = (bf16[4,48,1536]{2,1,0:T(8,128)(2,1)S(1)}, bf16[4,48,1536]{2,1,0:T(8,128)(2,1)S(1)}, u32[]{:S(2)}, u32[]{:S(2)}) collective-permute-start(bf16[4,48,1536]{2,1,0:T(8,128)(2,1)S(1)} %dynamic-slice_bitcast_fusion.3), channel_id=1, source_target_pairs={{0,16},{16,32},{32,48},{48,0},{64,80},{80,96},{96,112},{112,64},{1... | collective-permute-start | bytes 1769480 | tf_op jit(solution)/shard_map/ppermute | solution.py:93
  112.4 15.1 %collective-permute-start.18 = (bf16[4,192,384]{2,1,0:T(8,128)(2,1)S(1)}, bf16[4,192,384]{2,1,0:T(8,128)(2,1)S(1)}, u32[]{:S(2)}, u32[]{:S(2)}) collective-permute-start(bf16[4,192,384]{2,1,0:T(8,128)(2,1)S(1)} %dynamic-slice_bitcast_fusion), channel_id=1, source_target_pairs={{0,192},{16,208},{32,224},{48,240},{64,0},{80,16},{96,32},{112,48}... | collective-permute-start | bytes 1769480 | tf_op jit(solution)/shard_map/ppermute | solution.py:94
  114.2 16.8 %collective-permute-start.12 = (bf16[4,192,384]{2,1,0:T(8,128)(2,1)S(1)}, bf16[4,192,384]{2,1,0:T(8,128)(2,1)S(1)}, u32[]{:S(2)}, u32[]{:S(2)}) collective-permute-start(bf16[4,192,384]{2,1,0:T(8,128)(2,1)S(1)} %dynamic-slice_bitcast_fusion.1), channel_id=1, source_target_pairs={{0,48},{16,0},{32,16},{48,32},{64,112},{80,64},{96,80},{112,96},{1... | collective-permute-start | bytes 1769480 | tf_op jit(solution)/shard_map/ppermute | solution.py:94
  125.3 16.1 %collective-permute-start.7 = (bf16[4,48,1536]{2,1,0:T(8,128)(2,1)S(1)}, bf16[4,48,1536]{2,1,0:T(8,128)(2,1)S(1)}, u32[]{:S(2)}, u32[]{:S(2)}) collective-permute-start(bf16[4,48,1536]{2,1,0:T(8,128)(2,1)S(1)} %fusion.26), channel_id=1, source_target_pairs={{0,64},{16,80},{32,96},{48,112},{64,128},{80,144},{96,160},{112,17... | collective-permute-start | bytes 1769480 | tf_op jit(solution)/shard_map/ppermute | solution.py:93
  126.7 15.7 %collective-permute-start.1 = (bf16[4,48,1536]{2,1,0:T(8,128)(2,1)S(1)}, bf16[4,48,1536]{2,1,0:T(8,128)(2,1)S(1)}, u32[]{:S(2)}, u32[]{:S(2)}) collective-permute-start(bf16[4,48,1536]{2,1,0:T(8,128)(2,1)S(1)} %fusion.28), channel_id=1, source_target_pairs={{0,16},{16,32},{32,48},{48,0},{64,80},{80,96},{96,112},{112,64},{1... | collective-permute-start | bytes 1769480 | tf_op jit(solution)/shard_map/ppermute | solution.py:93
  127.6 15.9 %collective-permute-start.19 = (bf16[4,192,384]{2,1,0:T(8,128)(2,1)S(1)}, bf16[4,192,384]{2,1,0:T(8,128)(2,1)S(1)}, u32[]{:S(2)}, u32[]{:S(2)}) collective-permute-start(bf16[4,192,384]{2,1,0:T(8,128)(2,1)S(1)} %fusion.22), channel_id=1, source_target_pairs={{0,192},{16,208},{32,224},{48,240},{64,0},{80,16},{96,32},{112,48}... | collective-permute-start | bytes 1769480 | tf_op jit(solution)/shard_map/ppermute | solution.py:94
  131.2 15.9 %collective-permute-start.13 = (bf16[4,192,384]{2,1,0:T(8,128)(2,1)S(1)}, bf16[4,192,384]{2,1,0:T(8,128)(2,1)S(1)}, u32[]{:S(2)}, u32[]{:S(2)}) collective-permute-start(bf16[4,192,384]{2,1,0:T(8,128)(2,1)S(1)} %fusion.24), channel_id=1, source_target_pairs={{0,48},{16,0},{32,16},{48,32},{64,112},{80,64},{96,80},{112,96},{1... | collective-permute-start | bytes 1769480 | tf_op jit(solution)/shard_map/ppermute | solution.py:94
  141.5 15.2 %collective-permute-start.8 = (bf16[4,48,1536]{2,1,0:T(8,128)(2,1)S(1)}, bf16[4,48,1536]{2,1,0:T(8,128)(2,1)S(1)}, u32[]{:S(2)}, u32[]{:S(2)}) collective-permute-start(bf16[4,48,1536]{2,1,0:T(8,128)(2,1)S(1)} %fusion.25), channel_id=1, source_target_pairs={{0,64},{16,80},{32,96},{48,112},{64,128},{80,144},{96,160},{112,17... | collective-permute-start | bytes 1769480 | tf_op jit(solution)/shard_map/ppermute | solution.py:93
  142.6 16.3 %collective-permute-start.2 = (bf16[4,48,1536]{2,1,0:T(8,128)(2,1)S(1)}, bf16[4,48,1536]{2,1,0:T(8,128)(2,1)S(1)}, u32[]{:S(2)}, u32[]{:S(2)}) collective-permute-start(bf16[4,48,1536]{2,1,0:T(8,128)(2,1)S(1)} %fusion.27), channel_id=1, source_target_pairs={{0,16},{16,32},{32,48},{48,0},{64,80},{80,96},{96,112},{112,64},{1... | collective-permute-start | bytes 1769480 | tf_op jit(solution)/shard_map/ppermute | solution.py:93
  143.7 16.2 %collective-permute-start.20 = (bf16[4,192,384]{2,1,0:T(8,128)(2,1)S(1)}, bf16[4,192,384]{2,1,0:T(8,128)(2,1)S(1)}, u32[]{:S(2)}, u32[]{:S(2)}) collective-permute-start(bf16[4,192,384]{2,1,0:T(8,128)(2,1)S(1)} %fusion.21), channel_id=1, source_target_pairs={{0,192},{16,208},{32,224},{48,240},{64,0},{80,16},{96,32},{112,48}... | collective-permute-start | bytes 1769480 | tf_op jit(solution)/shard_map/ppermute | solution.py:94
  147.2 14.0 %collective-permute-start.14 = (bf16[4,192,384]{2,1,0:T(8,128)(2,1)S(1)}, bf16[4,192,384]{2,1,0:T(8,128)(2,1)S(1)}, u32[]{:S(2)}, u32[]{:S(2)}) collective-permute-start(bf16[4,192,384]{2,1,0:T(8,128)(2,1)S(1)} %fusion.23), channel_id=1, source_target_pairs={{0,48},{16,0},{32,16},{48,32},{64,112},{80,64},{96,80},{112,96},{1... | collective-permute-start | bytes 1769480 | tf_op jit(solution)/shard_map/ppermute | solution.py:94
  157.0 7.3 %collective-permute-start.9 = (bf16[48,1536]{1,0:T(8,128)(2,1)S(1)}, bf16[48,1536]{1,0:T(8,128)(2,1)S(1)}, u32[]{:S(2)}, u32[]{:S(2)}) collective-permute-start(bf16[48,1536]{1,0:T(8,128)(2,1)S(1)} %fusion.53), channel_id=1, source_target_pairs={{0,16},{16,32},{32,48},{48,0},{64,80},{80,96},{96,112},{112,64},{1... | collective-permute-start | bytes 442376 | tf_op jit(solution)/shard_map/ppermute | solution.py:93
  159.0 6.4 %collective-permute-start.3 = (bf16[48,1536]{1,0:T(8,128)(2,1)S(1)}, bf16[48,1536]{1,0:T(8,128)(2,1)S(1)}, u32[]{:S(2)}, u32[]{:S(2)}) collective-permute-start(bf16[48,1536]{1,0:T(8,128)(2,1)S(1)} %fusion.52), channel_id=1, source_target_pairs={{0,64},{16,80},{32,96},{48,112},{64,128},{80,144},{96,160},{112,17... | collective-permute-start | bytes 442376 | tf_op jit(solution)/shard_map/ppermute | solution.py:93
  160.0 5.8 %collective-permute-start.21 = (bf16[192,384]{1,0:T(8,128)(2,1)S(1)}, bf16[192,384]{1,0:T(8,128)(2,1)S(1)}, u32[]{:S(2)}, u32[]{:S(2)}) collective-permute-start(bf16[192,384]{1,0:T(8,128)(2,1)S(1)} %fusion.55), channel_id=1, source_target_pairs={{0,48},{16,0},{32,16},{48,32},{64,112},{80,64},{96,80},{112,96},{1... | collective-permute-start | bytes 442376 | tf_op jit(solution)/shard_map/ppermute | solution.py:94
  161.4 6.6 %collective-permute-start.15 = (bf16[192,384]{1,0:T(8,128)(2,1)S(1)}, bf16[192,384]{1,0:T(8,128)(2,1)S(1)}, u32[]{:S(2)}, u32[]{:S(2)}) collective-permute-start(bf16[192,384]{1,0:T(8,128)(2,1)S(1)} %fusion.54), channel_id=1, source_target_pairs={{0,192},{16,208},{32,224},{48,240},{64,0},{80,16},{96,32},{112,48}... | collective-permute-start | bytes 442376 | tf_op jit(solution)/shard_map/ppermute | solution.py:94
  164.4 6.9 %collective-permute-start.10 = (bf16[48,1536]{1,0:T(8,128)(2,1)S(1)}, bf16[48,1536]{1,0:T(8,128)(2,1)S(1)}, u32[]{:S(2)}, u32[]{:S(2)}) collective-permute-start(bf16[48,1536]{1,0:T(8,128)(2,1)S(1)} %fusion.43), channel_id=1, source_target_pairs={{0,16},{16,32},{32,48},{48,0},{64,80},{80,96},{96,112},{112,64},{1... | collective-permute-start | bytes 442376 | tf_op jit(solution)/shard_map/ppermute | solution.py:93
  165.5 6.8 %collective-permute-start.4 = (bf16[48,1536]{1,0:T(8,128)(2,1)S(1)}, bf16[48,1536]{1,0:T(8,128)(2,1)S(1)}, u32[]{:S(2)}, u32[]{:S(2)}) collective-permute-start(bf16[48,1536]{1,0:T(8,128)(2,1)S(1)} %fusion.45), channel_id=1, source_target_pairs={{0,64},{16,80},{32,96},{48,112},{64,128},{80,144},{96,160},{112,17... | collective-permute-start | bytes 442376 | tf_op jit(solution)/shard_map/ppermute | solution.py:93
  165.9 6.6 %collective-permute-start.22 = (bf16[192,384]{1,0:T(8,128)(2,1)S(1)}, bf16[192,384]{1,0:T(8,128)(2,1)S(1)}, u32[]{:S(2)}, u32[]{:S(2)}) collective-permute-start(bf16[192,384]{1,0:T(8,128)(2,1)S(1)} %fusion.39), channel_id=1, source_target_pairs={{0,48},{16,0},{32,16},{48,32},{64,112},{80,64},{96,80},{112,96},{1... | collective-permute-start | bytes 442376 | tf_op jit(solution)/shard_map/ppermute | solution.py:94
  168.0 7.2 %collective-permute-start.16 = (bf16[192,384]{1,0:T(8,128)(2,1)S(1)}, bf16[192,384]{1,0:T(8,128)(2,1)S(1)}, u32[]{:S(2)}, u32[]{:S(2)}) collective-permute-start(bf16[192,384]{1,0:T(8,128)(2,1)S(1)} %fusion.41), channel_id=1, source_target_pairs={{0,192},{16,208},{32,224},{48,240},{64,0},{80,16},{96,32},{112,48}... | collective-permute-start | bytes 442376 | tf_op jit(solution)/shard_map/ppermute | solution.py:94
  171.3 7.2 %collective-permute-start.11 = (bf16[48,1536]{1,0:T(8,128)(2,1)S(1)}, bf16[48,1536]{1,0:T(8,128)(2,1)S(1)}, u32[]{:S(2)}, u32[]{:S(2)}) collective-permute-start(bf16[48,1536]{1,0:T(8,128)(2,1)S(1)} %fusion.42), channel_id=1, source_target_pairs={{0,16},{16,32},{32,48},{48,0},{64,80},{80,96},{96,112},{112,64},{1... | collective-permute-start | bytes 442376 | tf_op jit(solution)/shard_map/ppermute | solution.py:93
  172.3 9.7 %copy-start.1 = (bf16[768,16]{0,1:T(8,128)(2,1)S(1)}, bf16[768,16]{0,1:T(8,128)(2,1)}, u32[]{:S(2)}) copy-start(bf16[768,16]{0,1:T(8,128)(2,1)} %param.10) | copy-start | bytes 73732
  172.4 6.4 %collective-permute-start.5 = (bf16[48,1536]{1,0:T(8,128)(2,1)S(1)}, bf16[48,1536]{1,0:T(8,128)(2,1)S(1)}, u32[]{:S(2)}, u32[]{:S(2)}) collective-permute-start(bf16[48,1536]{1,0:T(8,128)(2,1)S(1)} %fusion.44), channel_id=1, source_target_pairs={{0,64},{16,80},{32,96},{48,112},{64,128},{80,144},{96,160},{112,17... | collective-permute-start | bytes 442376 | tf_op jit(solution)/shard_map/ppermute | solution.py:93
  172.5 7.2 %collective-permute-start.23 = (bf16[192,384]{1,0:T(8,128)(2,1)S(1)}, bf16[192,384]{1,0:T(8,128)(2,1)S(1)}, u32[]{:S(2)}, u32[]{:S(2)}) collective-permute-start(bf16[192,384]{1,0:T(8,128)(2,1)S(1)} %fusion.38), channel_id=1, source_target_pairs={{0,48},{16,0},{32,16},{48,32},{64,112},{80,64},{96,80},{112,96},{1... | collective-permute-start | bytes 442376 | tf_op jit(solution)/shard_map/ppermute | solution.py:94
  175.2 6.0 %collective-permute-start.17 = (bf16[192,384]{1,0:T(8,128)(2,1)S(1)}, bf16[192,384]{1,0:T(8,128)(2,1)S(1)}, u32[]{:S(2)}, u32[]{:S(2)}) collective-permute-start(bf16[192,384]{1,0:T(8,128)(2,1)S(1)} %fusion.40), channel_id=1, source_target_pairs={{0,192},{16,208},{32,224},{48,240},{64,0},{80,16},{96,32},{112,48}... | collective-permute-start | bytes 442376 | tf_op jit(solution)/shard_map/ppermute | solution.py:94
Sparse Core Ops, SparseCore 0:
  10.4 55.4 all-gather.2

commit v2 on v1

--- a/solution.py
+++ b/solution.py
@@ -211,9 +211,9 @@
     delta_row = lax.all_gather(delta_seq, "expert", axis=0, tiled=True)
 
     dims_t = (((0,), (0,)), ((), ()))
-    spread_t = lax.dot_general(
+    spread_t = lax.optimization_barrier(lax.dot_general(
         weight_out[0], delta_row, (((1,), (1,)), ((), ())), preferred_element_type=jnp.float32
-    ).astype(jnp.bfloat16)
+    ).astype(jnp.bfloat16))
     dhidden = lax.dot_general(
         sel_gate.astype(jnp.bfloat16), spread_t, (((0,), (1,)), ((), ())),
         preferred_element_type=jnp.float32,

time: 191 us -> 190 us (level)
    dot_general x1, matrix products: 9.36 us -> 4.32 us  [on_device(): lax.dot_general(sel_gate.astype(jnp.bfloat16), spread_t, (((0,), (1,)), (...]
    dot_general x0 -> x1, matrix products: none -> 3.95 us  [on_device(): lax.dot_general(weight_out[0], delta_row, (((1,), (1,)), ((), ())), prefe...]
where the time goes in v2:
time: 190 us; the launch traced here: 187 us
  waiting for transfers between devices  58.8 us (31%)
  starting transfers between devices  53.2 us (28%)
  matrix products  26.3 us (14%)
  blocking collectives  16.1 us (8%)
  between operations  14.5 us (8%)
  other arithmetic  10.9 us (6%)
  local copies, waits for them, and re-layouts  7.46 us (4%)
    ppermute x12, waiting for transfers between devices, ring_step(): got_f = lax.ppermute(state['acc_f'].astype(jnp.bfloat16), 'dp', fwd_pairs)  29 us
    ppermute x12, starting transfers between devices, ring_step(): got_b = lax.ppermute(state['acc_b'].astype(jnp.bfloat16), 'dp', bwd_pairs)  28.4 us
    all_to_all x1, waiting for transfers between devices, on_device(): lax.all_to_all(outgoing, 'expert', split_axis=0, concat_axis=0, tiled=True)  20.8 us
    all_gather x1, blocking collectives, on_device(): delta_row = lax.all_gather(delta_seq, 'expert', axis=0, tiled=True)  16.1 us
    ppermute x12, starting transfers between devices, ring_step(): got_f = lax.ppermute(state['acc_f'].astype(jnp.bfloat16), 'dp', fwd_pairs)  9.37 us
    all_to_all x1, starting transfers between devices, on_device(): lax.all_to_all(outgoing, 'expert', split_axis=0, concat_axis=0, tiled=True)  8.59 us
    all_to_all x1, starting transfers between devices, on_device(): lax.all_to_all(moe_seq.reshape(expert_size, seq_count, model_width), 'exp...  6.8 us
    all_to_all x1, waiting for transfers between devices, on_device(): lax.all_to_all(moe_seq.reshape(expert_size, seq_count, model_width), 'exp...  6.67 us
  transfers between devices with their start and end apart: 27, of which 13 were waited for; matrix products, arithmetic and copies ran while one was open for 12% of the time, Pallas kernels for 0%

profile of v2, /device:TPU:32, one launch (start us, length us, event | category | flops | bytes accessed | tf_op | source)
XLA Modules:
  0.0 187.2 jit_solution(12813352929124780141)
XLA Ops:
  7.9 0.8 copy.66
  10.8 1.0 fusion.82
  11.9 0.8 select_reduce_fusion.1
  13.1 1.3 fusion.49
  14.8 1.0 pad_maximum_fusion
  15.8 8.6 %all-to-all-start = ((bf16[16,32,896]{2,1,0:T(8,128)(2,1)}), bf16[16,32,896]{2,1,0:T(8,128)(2,1)S(1)}, u32[]{:S(2)}, u32[]{:S(2)}) async-start(bf16[16,32,896]{2,1,0:T(8,128)(2,1)} %pad_maximum_fusion), calls=%async_computation | async-start | bytes 1835008 | tf_op jit(solution)/shard_map/all_to_all | solution.py:168
  24.4 0.8 dynamic_slice.110
  25.4 20.8 %all-to-all-done = bf16[16,32,896]{2,1,0:T(8,128)(2,1)S(1)} async-done(((bf16[16,32,896]{2,1,0:T(8,128)(2,1)}), bf16[16,32,896]{2,1,0:T(8,128)(2,1)S(1)}, u32[]{:S(2)}, u32[]{:S(2)}) %all-to-all-start) | async-done | bytes 917536 | tf_op jit(solution)/shard_map/all_to_all | solution.py:168
  46.8 4.5 %fusion.13 = f32[512,3072]{1,0:T(8,128)S(1)} fusion(bf16[512,768]{1,0:T(8,128)(2,1)S(1)} %bitcast.178, bf16[1,768,3072]{2,1,0:T(8,128)(2,1)} %param.11), kind=kOutput, calls=%fused_computation.19 | convolution fusion | flops 2415919104 | bytes 11796480 | tf_op jit(solution)/shard_map/dot_general | solution.py:176
  51.3 2.5 %fusion.21 = f32[32,3072]{1,0:T(8,128)S(1)} fusion(bf16[32,512]{1,0:T(8,128)(2,1)S(1)} %convert_element_type.307, f32[512,3072]{1,0:T(8,128)S(1)} %fusion.13), kind=kOutput, calls=%fused_computation.23 | convolution fusion | flops 114819072 | bytes 6717440 | tf_op jit(solution)/shard_map/dot_general | solution.py:179
  54.5 1.3 slice-done.1
  55.8 0.9 fusion.9
  56.7 0.9 fusion.32
  58.3 6.8 %all-to-all-start.1 = ((f32[16,2,768]{2,1,0:T(2,128)}), f32[16,2,768]{2,1,0:T(2,128)S(1)}, u32[]{:S(2)}, u32[]{:S(2)}) async-start(f32[16,2,768]{2,1,0:T(2,128)} %reshape.138), calls=%async_computation.1 | async-start | bytes 196608 | tf_op jit(solution)/shard_map/all_to_all | solution.py:181
  65.2 6.7 %all-to-all-done.1 = f32[16,2,768]{2,1,0:T(2,128)S(1)} async-done(((f32[16,2,768]{2,1,0:T(2,128)}), f32[16,2,768]{2,1,0:T(2,128)S(1)}, u32[]{:S(2)}, u32[]{:S(2)}) %all-to-all-start.1) | async-done | bytes 98336 | tf_op jit(solution)/shard_map/all_to_all | solution.py:181
  72.0 2.7 %multiply_reduce_fusion = f32[2048]{0:T(1024)S(1)} fusion(bf16[2048,768]{1,0:T(8,128)(2,1)} %all-gather.3.cloned.1.call-done), kind=kLoop, calls=%fused_computation.9 | loop fusion | flops 4716544 | bytes 3153920 | tf_op jit(solution)/shard_map/reduce_sum | solution.py:194
  75.0 1.0 fusion.81
  77.3 16.1 %all-gather = bf16[16,2,768]{2,1,0:T(2,128)(2,1)S(1)} all-gather(bf16[1,2,768]{2,1,0:T(2,128)(2,1)S(1)} %fusion.69), channel_id=1, replica_groups=mesh['dp'=16,'expert'=16] {'expert'}, dimensions={0}, use_global_device_ids=true | all-gather | bytes 52224 | tf_op jit(solution)/shard_map/all_gather | solution.py:211
  93.4 3.9 %fusion.18 = bf16[3072,32]{0,1:T(8,128)(2,1)S(1)} fusion(bf16[32,768]{1,0:T(8,128)(2,1)S(1)} %reshape.156, bf16[1,3072,768]{2,1,0:T(8,128)(2,1)} %param.12), kind=kOutput, calls=%fused_computation.22 | convolution fusion | flops 151093248 | bytes 4964352 | tf_op jit(solution)/shard_map/dot_general | solution.py:214
  97.4 1.5 convolution_convert_fusion
  98.9 4.3 %fusion.6 = bf16[512,3072]{1,0:T(8,128)(2,1)S(1)} fusion(f32[512,3072]{1,0:T(8,128)S(1)} %bitcast.176, bf16[32,512]{1,0:T(8,128)(2,1)S(1)} %convert_element_type.307, bf16[3072,32]{0,1:T(8,128)(2,1)S(1)} %fusion.18), kind=kOutput, calls=%fused_computation.8 | convolution fusion | flops 130547712 | bytes 9666560 | tf_op jit(solution)/shard_map/dot_general | solution.py:217
  103.2 2.9 %convolution_convert_fusion.1 = bf16[768,3072]{1,0:T(8,128)(2,1)S(1)} fusion(bf16[512,768]{1,0:T(8,128)(2,1)S(1)} %bitcast.179, bf16[512,3072]{1,0:T(8,128)(2,1)S(1)} %fusion.6), kind=kOutput, calls=%fused_computation.12 | convolution fusion | flops 2418278400 | bytes 8650752 | tf_op jit(solution)/shard_map/dot_general | solution.py:222
  106.8 1.6 collective-permute-start.6
  108.5 1.5 collective-permute-start
  110.0 0.8 fusion.79
  110.9 1.8 collective-permute-start.18
  112.8 1.8 collective-permute-start.12
  114.6 9.1 %collective-permute-done.6 = bf16[4,48,1536]{2,1,0:T(8,128)(2,1)S(1)} collective-permute-done((bf16[4,48,1536]{2,1,0:T(8,128)(2,1)S(1)}, bf16[4,48,1536]{2,1,0:T(8,128)(2,1)S(1)}, u32[]{:S(2)}, u32[]{:S(2)}) %collective-permute-start.6) | collective-permute-done | bytes 589856 | tf_op jit(solution)/shard_map/ppermute | solution.py:93
  124.2 0.8 collective-permute-done
  126.2 3.1 %collective-permute-start.19 = (bf16[4,192,384]{2,1,0:T(8,128)(2,1)S(1)}, bf16[4,192,384]{2,1,0:T(8,128)(2,1)S(1)}, u32[]{:S(2)}, u32[]{:S(2)}) collective-permute-start(bf16[4,192,384]{2,1,0:T(8,128)(2,1)S(1)} %fusion.25), channel_id=1, source_target_pairs={{0,192},{16,208},{32,224},{48,240},{64,0},{80,16},{96,32},{112,48}... | collective-permute-start | bytes 1769480 | tf_op jit(solution)/shard_map/ppermute | solution.py:94
  129.5 2.0 %collective-permute-start.13 = (bf16[4,192,384]{2,1,0:T(8,128)(2,1)S(1)}, bf16[4,192,384]{2,1,0:T(8,128)(2,1)S(1)}, u32[]{:S(2)}, u32[]{:S(2)}) collective-permute-start(bf16[4,192,384]{2,1,0:T(8,128)(2,1)S(1)} %fusion.27), channel_id=1, source_target_pairs={{0,48},{16,0},{32,16},{48,32},{64,112},{80,64},{96,80},{112,96},{1... | collective-permute-start | bytes 1769480 | tf_op jit(solution)/shard_map/ppermute | solution.py:94
  131.5 8.5 %collective-permute-done.7 = bf16[4,48,1536]{2,1,0:T(8,128)(2,1)S(1)} collective-permute-done((bf16[4,48,1536]{2,1,0:T(8,128)(2,1)S(1)}, bf16[4,48,1536]{2,1,0:T(8,128)(2,1)S(1)}, u32[]{:S(2)}, u32[]{:S(2)}) %collective-permute-start.7) | collective-permute-done | bytes 589856 | tf_op jit(solution)/shard_map/ppermute | solution.py:93
  141.1 1.0 collective-permute-start.2
  142.3 3.3 %collective-permute-start.20 = (bf16[4,192,384]{2,1,0:T(8,128)(2,1)S(1)}, bf16[4,192,384]{2,1,0:T(8,128)(2,1)S(1)}, u32[]{:S(2)}, u32[]{:S(2)}) collective-permute-start(bf16[4,192,384]{2,1,0:T(8,128)(2,1)S(1)} %fusion.24), channel_id=1, source_target_pairs={{0,192},{16,208},{32,224},{48,240},{64,0},{80,16},{96,32},{112,48}... | collective-permute-start | bytes 1769480 | tf_op jit(solution)/shard_map/ppermute | solution.py:94
  145.7 1.7 collective-permute-start.14
  147.4 7.9 %collective-permute-done.8 = bf16[4,48,1536]{2,1,0:T(8,128)(2,1)S(1)} collective-permute-done((bf16[4,48,1536]{2,1,0:T(8,128)(2,1)S(1)}, bf16[4,48,1536]{2,1,0:T(8,128)(2,1)S(1)}, u32[]{:S(2)}, u32[]{:S(2)}) %collective-permute-start.8) | collective-permute-done | bytes 589856 | tf_op jit(solution)/shard_map/ppermute | solution.py:93
  155.5 1.8 collective-permute-start.9
  157.6 0.9 collective-permute-start.3
  158.6 0.8 collective-permute-start.21
  159.9 3.0 %collective-permute-start.15 = (bf16[192,384]{1,0:T(8,128)(2,1)S(1)}, bf16[192,384]{1,0:T(8,128)(2,1)S(1)}, u32[]{:S(2)}, u32[]{:S(2)}) collective-permute-start(bf16[192,384]{1,0:T(8,128)(2,1)S(1)} %fusion.55), channel_id=1, source_target_pairs={{0,192},{16,208},{32,224},{48,240},{64,0},{80,16},{96,32},{112,48}... | collective-permute-start | bytes 442376 | tf_op jit(solution)/shard_map/ppermute | solution.py:94
  164.5 2.0 %collective-permute-start.22 = (bf16[192,384]{1,0:T(8,128)(2,1)S(1)}, bf16[192,384]{1,0:T(8,128)(2,1)S(1)}, u32[]{:S(2)}, u32[]{:S(2)}) collective-permute-start(bf16[192,384]{1,0:T(8,128)(2,1)S(1)} %fusion.40), channel_id=1, source_target_pairs={{0,48},{16,0},{32,16},{48,32},{64,112},{80,64},{96,80},{112,96},{1... | collective-permute-start | bytes 442376 | tf_op jit(solution)/shard_map/ppermute | solution.py:94
  166.5 3.3 %collective-permute-start.16 = (bf16[192,384]{1,0:T(8,128)(2,1)S(1)}, bf16[192,384]{1,0:T(8,128)(2,1)S(1)}, u32[]{:S(2)}, u32[]{:S(2)}) collective-permute-start(bf16[192,384]{1,0:T(8,128)(2,1)S(1)} %fusion.42), channel_id=1, source_target_pairs={{0,192},{16,208},{32,224},{48,240},{64,0},{80,16},{96,32},{112,48}... | collective-permute-start | bytes 442376 | tf_op jit(solution)/shard_map/ppermute | solution.py:94
  170.1 0.8 collective-permute-done.4
  171.1 2.3 %collective-permute-start.23 = (bf16[192,384]{1,0:T(8,128)(2,1)S(1)}, bf16[192,384]{1,0:T(8,128)(2,1)S(1)}, u32[]{:S(2)}, u32[]{:S(2)}) collective-permute-start(bf16[192,384]{1,0:T(8,128)(2,1)S(1)} %fusion.39), channel_id=1, source_target_pairs={{0,48},{16,0},{32,16},{48,32},{64,112},{80,64},{96,80},{112,96},{1... | collective-permute-start | bytes 442376 | tf_op jit(solution)/shard_map/ppermute | solution.py:94
  173.4 3.4 %collective-permute-start.17 = (bf16[192,384]{1,0:T(8,128)(2,1)S(1)}, bf16[192,384]{1,0:T(8,128)(2,1)S(1)}, u32[]{:S(2)}, u32[]{:S(2)}) collective-permute-start(bf16[192,384]{1,0:T(8,128)(2,1)S(1)} %fusion.41), channel_id=1, source_target_pairs={{0,192},{16,208},{32,224},{48,240},{64,0},{80,16},{96,32},{112,48}... | collective-permute-start | bytes 442376 | tf_op jit(solution)/shard_map/ppermute | solution.py:94
  177.4 0.9 maximum_bitcast_fusion
  178.3 1.2 collective-permute-done.17
  179.5 0.9 maximum_bitcast_fusion.1
  (121 shorter events, 15.4 us)
Async XLA Ops:
  7.2 3.7 %copy-start = (bf16[768,16]{0,1:T(8,128)(2,1)S(1)}, bf16[768,16]{0,1:T(8,128)(2,1)}, u32[]{:S(2)}) copy-start(bf16[768,16]{0,1:T(8,128)(2,1)} %param.10) | copy-start | bytes 73732
  7.2 64.8 %all-gather.3.cloned.1.call-start = ((), (), s32[]{:S(2)}) async-start(), calls=%async_computation.2 | async-start | bytes 3342336 | tf_op jit(solution)/shard_map/all_gather | solution.py:193
  14.4 10.7 %copy-start.5 = (s32[256,16]{0,1:T(8,128)S(1)}, s32[256,16]{0,1:T(8,128)}, u32[]{:S(2)}) copy-start(s32[256,16]{0,1:T(8,128)} %param.15) | copy-start | bytes 49156
  14.5 10.9 %copy-start.4 = (bf16[128,768]{1,0:T(8,128)(2,1)S(1)}, bf16[128,768]{1,0:T(8,128)(2,1)}, u32[]{:S(2)}) copy-start(bf16[128,768]{1,0:T(8,128)(2,1)} %param.8) | copy-start | bytes 589828
  15.8 30.4 %all-to-all-start = ((bf16[16,32,896]{2,1,0:T(8,128)(2,1)}), bf16[16,32,896]{2,1,0:T(8,128)(2,1)S(1)}, u32[]{:S(2)}, u32[]{:S(2)}) async-start(bf16[16,32,896]{2,1,0:T(8,128)(2,1)} %pad_maximum_fusion), calls=%async_computation | async-start | bytes 1835008 | tf_op jit(solution)/shard_map/all_to_all | solution.py:168
  46.8 7.8 %slice-start = ((s8[4718592]{0:T(1024)(128)(4,1)}), s8[524288]{0:T(1024)(128)(4,1)S(1)}, s32[]{:S(2)}) async-start(s8[4718592]{0:T(1024)(128)(4,1)} %bitcast.172), calls=%async_computation.3 | async-start | bytes 1048576
  51.3 3.2 %copy-start.3 = (f32[512,3072]{1,0:T(8,128)}, f32[512,3072]{1,0:T(8,128)S(1)}, u32[]{:S(2)}) copy-start(f32[512,3072]{1,0:T(8,128)S(1)} %fusion.13) | copy-start | bytes 18874372
  51.3 4.5 %slice-start.1 = ((s8[4718592]{0:T(1024)(128)(4,1)}), s8[4194304]{0:T(1024)(128)(4,1)S(1)}, s32[]{:S(2)}) async-start(s8[4718592]{0:T(1024)(128)(4,1)} %bitcast.172), calls=%async_computation.4 | async-start | bytes 8388608
  58.3 13.5 %all-to-all-start.1 = ((f32[16,2,768]{2,1,0:T(2,128)}), f32[16,2,768]{2,1,0:T(2,128)S(1)}, u32[]{:S(2)}, u32[]{:S(2)}) async-start(f32[16,2,768]{2,1,0:T(2,128)} %reshape.138), calls=%async_computation.1 | async-start | bytes 196608 | tf_op jit(solution)/shard_map/all_to_all | solution.py:181
  72.0 3.0 %copy-start.2 = (bf16[2048,768]{1,0:T(8,128)(2,1)S(1)}, bf16[2048,768]{1,0:T(8,128)(2,1)}, u32[]{:S(2)}) copy-start(bf16[2048,768]{1,0:T(8,128)(2,1)} %all-gather.3.cloned.1.call-done) | copy-start | bytes 9437188
  76.5 22.3 %slice-start.2 = ((s8[6291456]{0:T(1024)(128)(4,1)}), s8[2097152]{0:T(1024)(128)(4,1)S(1)}, s32[]{:S(2)}) async-start(s8[6291456]{0:T(1024)(128)(4,1)} %bitcast.175), calls=%async_computation.5 | async-start | bytes 4194304
  93.4 5.4 %slice-start.3 = ((s8[6291456]{0:T(1024)(128)(4,1)}), s8[4194304]{0:T(1024)(128)(4,1)S(1)}, s32[]{:S(2)}) async-start(s8[6291456]{0:T(1024)(128)(4,1)} %bitcast.175), calls=%async_computation.6 | async-start | bytes 8388608
  106.8 16.9 %collective-permute-start.6 = (bf16[4,48,1536]{2,1,0:T(8,128)(2,1)S(1)}, bf16[4,48,1536]{2,1,0:T(8,128)(2,1)S(1)}, u32[]{:S(2)}, u32[]{:S(2)}) collective-permute-start(bf16[4,48,1536]{2,1,0:T(8,128)(2,1)S(1)} %dynamic-slice_bitcast_fusion.2), channel_id=1, source_target_pairs={{0,64},{16,80},{32,96},{48,112},{64,128},{80,144},{96,160},{112,17... | collective-permute-start | bytes 1769480 | tf_op jit(solution)/shard_map/ppermute | solution.py:93
  108.5 16.6 %collective-permute-start = (bf16[4,48,1536]{2,1,0:T(8,128)(2,1)S(1)}, bf16[4,48,1536]{2,1,0:T(8,128)(2,1)S(1)}, u32[]{:S(2)}, u32[]{:S(2)}) collective-permute-start(bf16[4,48,1536]{2,1,0:T(8,128)(2,1)S(1)} %dynamic-slice_bitcast_fusion.3), channel_id=1, source_target_pairs={{0,16},{16,32},{32,48},{48,0},{64,80},{80,96},{96,112},{112,64},{1... | collective-permute-start | bytes 1769480 | tf_op jit(solution)/shard_map/ppermute | solution.py:93
  110.9 15.1 %collective-permute-start.18 = (bf16[4,192,384]{2,1,0:T(8,128)(2,1)S(1)}, bf16[4,192,384]{2,1,0:T(8,128)(2,1)S(1)}, u32[]{:S(2)}, u32[]{:S(2)}) collective-permute-start(bf16[4,192,384]{2,1,0:T(8,128)(2,1)S(1)} %dynamic-slice_bitcast_fusion), channel_id=1, source_target_pairs={{0,192},{16,208},{32,224},{48,240},{64,0},{80,16},{96,32},{112,48}... | collective-permute-start | bytes 1769480 | tf_op jit(solution)/shard_map/ppermute | solution.py:94
  112.8 16.6 %collective-permute-start.12 = (bf16[4,192,384]{2,1,0:T(8,128)(2,1)S(1)}, bf16[4,192,384]{2,1,0:T(8,128)(2,1)S(1)}, u32[]{:S(2)}, u32[]{:S(2)}) collective-permute-start(bf16[4,192,384]{2,1,0:T(8,128)(2,1)S(1)} %dynamic-slice_bitcast_fusion.1), channel_id=1, source_target_pairs={{0,48},{16,0},{32,16},{48,32},{64,112},{80,64},{96,80},{112,96},{1... | collective-permute-start | bytes 1769480 | tf_op jit(solution)/shard_map/ppermute | solution.py:94
  123.9 16.1 %collective-permute-start.7 = (bf16[4,48,1536]{2,1,0:T(8,128)(2,1)S(1)}, bf16[4,48,1536]{2,1,0:T(8,128)(2,1)S(1)}, u32[]{:S(2)}, u32[]{:S(2)}) collective-permute-start(bf16[4,48,1536]{2,1,0:T(8,128)(2,1)S(1)} %fusion.29), channel_id=1, source_target_pairs={{0,64},{16,80},{32,96},{48,112},{64,128},{80,144},{96,160},{112,17... | collective-permute-start | bytes 1769480 | tf_op jit(solution)/shard_map/ppermute | solution.py:93
  125.2 15.7 %collective-permute-start.1 = (bf16[4,48,1536]{2,1,0:T(8,128)(2,1)S(1)}, bf16[4,48,1536]{2,1,0:T(8,128)(2,1)S(1)}, u32[]{:S(2)}, u32[]{:S(2)}) collective-permute-start(bf16[4,48,1536]{2,1,0:T(8,128)(2,1)S(1)} %fusion.31), channel_id=1, source_target_pairs={{0,16},{16,32},{32,48},{48,0},{64,80},{80,96},{96,112},{112,64},{1... | collective-permute-start | bytes 1769480 | tf_op jit(solution)/shard_map/ppermute | solution.py:93
  126.2 15.9 %collective-permute-start.19 = (bf16[4,192,384]{2,1,0:T(8,128)(2,1)S(1)}, bf16[4,192,384]{2,1,0:T(8,128)(2,1)S(1)}, u32[]{:S(2)}, u32[]{:S(2)}) collective-permute-start(bf16[4,192,384]{2,1,0:T(8,128)(2,1)S(1)} %fusion.25), channel_id=1, source_target_pairs={{0,192},{16,208},{32,224},{48,240},{64,0},{80,16},{96,32},{112,48}... | collective-permute-start | bytes 1769480 | tf_op jit(solution)/shard_map/ppermute | solution.py:94
  129.5 16.1 %collective-permute-start.13 = (bf16[4,192,384]{2,1,0:T(8,128)(2,1)S(1)}, bf16[4,192,384]{2,1,0:T(8,128)(2,1)S(1)}, u32[]{:S(2)}, u32[]{:S(2)}) collective-permute-start(bf16[4,192,384]{2,1,0:T(8,128)(2,1)S(1)} %fusion.27), channel_id=1, source_target_pairs={{0,48},{16,0},{32,16},{48,32},{64,112},{80,64},{96,80},{112,96},{1... | collective-permute-start | bytes 1769480 | tf_op jit(solution)/shard_map/ppermute | solution.py:94
  140.1 15.2 %collective-permute-start.8 = (bf16[4,48,1536]{2,1,0:T(8,128)(2,1)S(1)}, bf16[4,48,1536]{2,1,0:T(8,128)(2,1)S(1)}, u32[]{:S(2)}, u32[]{:S(2)}) collective-permute-start(bf16[4,48,1536]{2,1,0:T(8,128)(2,1)S(1)} %fusion.28), channel_id=1, source_target_pairs={{0,64},{16,80},{32,96},{48,112},{64,128},{80,144},{96,160},{112,17... | collective-permute-start | bytes 1769480 | tf_op jit(solution)/shard_map/ppermute | solution.py:93
  141.1 16.3 %collective-permute-start.2 = (bf16[4,48,1536]{2,1,0:T(8,128)(2,1)S(1)}, bf16[4,48,1536]{2,1,0:T(8,128)(2,1)S(1)}, u32[]{:S(2)}, u32[]{:S(2)}) collective-permute-start(bf16[4,48,1536]{2,1,0:T(8,128)(2,1)S(1)} %fusion.30), channel_id=1, source_target_pairs={{0,16},{16,32},{32,48},{48,0},{64,80},{80,96},{96,112},{112,64},{1... | collective-permute-start | bytes 1769480 | tf_op jit(solution)/shard_map/ppermute | solution.py:93
  142.3 16.2 %collective-permute-start.20 = (bf16[4,192,384]{2,1,0:T(8,128)(2,1)S(1)}, bf16[4,192,384]{2,1,0:T(8,128)(2,1)S(1)}, u32[]{:S(2)}, u32[]{:S(2)}) collective-permute-start(bf16[4,192,384]{2,1,0:T(8,128)(2,1)S(1)} %fusion.24), channel_id=1, source_target_pairs={{0,192},{16,208},{32,224},{48,240},{64,0},{80,16},{96,32},{112,48}... | collective-permute-start | bytes 1769480 | tf_op jit(solution)/shard_map/ppermute | solution.py:94
  145.7 14.0 %collective-permute-start.14 = (bf16[4,192,384]{2,1,0:T(8,128)(2,1)S(1)}, bf16[4,192,384]{2,1,0:T(8,128)(2,1)S(1)}, u32[]{:S(2)}, u32[]{:S(2)}) collective-permute-start(bf16[4,192,384]{2,1,0:T(8,128)(2,1)S(1)} %fusion.26), channel_id=1, source_target_pairs={{0,48},{16,0},{32,16},{48,32},{64,112},{80,64},{96,80},{112,96},{1... | collective-permute-start | bytes 1769480 | tf_op jit(solution)/shard_map/ppermute | solution.py:94
  155.5 7.3 %collective-permute-start.9 = (bf16[48,1536]{1,0:T(8,128)(2,1)S(1)}, bf16[48,1536]{1,0:T(8,128)(2,1)S(1)}, u32[]{:S(2)}, u32[]{:S(2)}) collective-permute-start(bf16[48,1536]{1,0:T(8,128)(2,1)S(1)} %fusion.54), channel_id=1, source_target_pairs={{0,16},{16,32},{32,48},{48,0},{64,80},{80,96},{96,112},{112,64},{1... | collective-permute-start | bytes 442376 | tf_op jit(solution)/shard_map/ppermute | solution.py:93
  157.6 6.4 %collective-permute-start.3 = (bf16[48,1536]{1,0:T(8,128)(2,1)S(1)}, bf16[48,1536]{1,0:T(8,128)(2,1)S(1)}, u32[]{:S(2)}, u32[]{:S(2)}) collective-permute-start(bf16[48,1536]{1,0:T(8,128)(2,1)S(1)} %fusion.53), channel_id=1, source_target_pairs={{0,64},{16,80},{32,96},{48,112},{64,128},{80,144},{96,160},{112,17... | collective-permute-start | bytes 442376 | tf_op jit(solution)/shard_map/ppermute | solution.py:93
  158.6 5.8 %collective-permute-start.21 = (bf16[192,384]{1,0:T(8,128)(2,1)S(1)}, bf16[192,384]{1,0:T(8,128)(2,1)S(1)}, u32[]{:S(2)}, u32[]{:S(2)}) collective-permute-start(bf16[192,384]{1,0:T(8,128)(2,1)S(1)} %fusion.56), channel_id=1, source_target_pairs={{0,48},{16,0},{32,16},{48,32},{64,112},{80,64},{96,80},{112,96},{1... | collective-permute-start | bytes 442376 | tf_op jit(solution)/shard_map/ppermute | solution.py:94
  159.9 6.6 %collective-permute-start.15 = (bf16[192,384]{1,0:T(8,128)(2,1)S(1)}, bf16[192,384]{1,0:T(8,128)(2,1)S(1)}, u32[]{:S(2)}, u32[]{:S(2)}) collective-permute-start(bf16[192,384]{1,0:T(8,128)(2,1)S(1)} %fusion.55), channel_id=1, source_target_pairs={{0,192},{16,208},{32,224},{48,240},{64,0},{80,16},{96,32},{112,48}... | collective-permute-start | bytes 442376 | tf_op jit(solution)/shard_map/ppermute | solution.py:94
  162.9 6.9 %collective-permute-start.10 = (bf16[48,1536]{1,0:T(8,128)(2,1)S(1)}, bf16[48,1536]{1,0:T(8,128)(2,1)S(1)}, u32[]{:S(2)}, u32[]{:S(2)}) collective-permute-start(bf16[48,1536]{1,0:T(8,128)(2,1)S(1)} %fusion.44), channel_id=1, source_target_pairs={{0,16},{16,32},{32,48},{48,0},{64,80},{80,96},{96,112},{112,64},{1... | collective-permute-start | bytes 442376 | tf_op jit(solution)/shard_map/ppermute | solution.py:93
  164.1 6.9 %collective-permute-start.4 = (bf16[48,1536]{1,0:T(8,128)(2,1)S(1)}, bf16[48,1536]{1,0:T(8,128)(2,1)S(1)}, u32[]{:S(2)}, u32[]{:S(2)}) collective-permute-start(bf16[48,1536]{1,0:T(8,128)(2,1)S(1)} %fusion.46), channel_id=1, source_target_pairs={{0,64},{16,80},{32,96},{48,112},{64,128},{80,144},{96,160},{112,17... | collective-permute-start | bytes 442376 | tf_op jit(solution)/shard_map/ppermute | solution.py:93
  164.5 6.6 %collective-permute-start.22 = (bf16[192,384]{1,0:T(8,128)(2,1)S(1)}, bf16[192,384]{1,0:T(8,128)(2,1)S(1)}, u32[]{:S(2)}, u32[]{:S(2)}) collective-permute-start(bf16[192,384]{1,0:T(8,128)(2,1)S(1)} %fusion.40), channel_id=1, source_target_pairs={{0,48},{16,0},{32,16},{48,32},{64,112},{80,64},{96,80},{112,96},{1... | collective-permute-start | bytes 442376 | tf_op jit(solution)/shard_map/ppermute | solution.py:94
  166.5 6.9 %collective-permute-start.16 = (bf16[192,384]{1,0:T(8,128)(2,1)S(1)}, bf16[192,384]{1,0:T(8,128)(2,1)S(1)}, u32[]{:S(2)}, u32[]{:S(2)}) collective-permute-start(bf16[192,384]{1,0:T(8,128)(2,1)S(1)} %fusion.42), channel_id=1, source_target_pairs={{0,192},{16,208},{32,224},{48,240},{64,0},{80,16},{96,32},{112,48}... | collective-permute-start | bytes 442376 | tf_op jit(solution)/shard_map/ppermute | solution.py:94
  169.8 7.0 %collective-permute-start.11 = (bf16[48,1536]{1,0:T(8,128)(2,1)S(1)}, bf16[48,1536]{1,0:T(8,128)(2,1)S(1)}, u32[]{:S(2)}, u32[]{:S(2)}) collective-permute-start(bf16[48,1536]{1,0:T(8,128)(2,1)S(1)} %fusion.43), channel_id=1, source_target_pairs={{0,16},{16,32},{32,48},{48,0},{64,80},{80,96},{96,112},{112,64},{1... | collective-permute-start | bytes 442376 | tf_op jit(solution)/shard_map/ppermute | solution.py:93
  170.9 9.5 %copy-start.1 = (bf16[768,16]{0,1:T(8,128)(2,1)S(1)}, bf16[768,16]{0,1:T(8,128)(2,1)}, u32[]{:S(2)}) copy-start(bf16[768,16]{0,1:T(8,128)(2,1)} %param.10) | copy-start | bytes 73732
  171.0 6.4 %collective-permute-start.5 = (bf16[48,1536]{1,0:T(8,128)(2,1)S(1)}, bf16[48,1536]{1,0:T(8,128)(2,1)S(1)}, u32[]{:S(2)}, u32[]{:S(2)}) collective-permute-start(bf16[48,1536]{1,0:T(8,128)(2,1)S(1)} %fusion.45), channel_id=1, source_target_pairs={{0,64},{16,80},{32,96},{48,112},{64,128},{80,144},{96,160},{112,17... | collective-permute-start | bytes 442376 | tf_op jit(solution)/shard_map/ppermute | solution.py:93
  171.1 7.2 %collective-permute-start.23 = (bf16[192,384]{1,0:T(8,128)(2,1)S(1)}, bf16[192,384]{1,0:T(8,128)(2,1)S(1)}, u32[]{:S(2)}, u32[]{:S(2)}) collective-permute-start(bf16[192,384]{1,0:T(8,128)(2,1)S(1)} %fusion.39), channel_id=1, source_target_pairs={{0,48},{16,0},{32,16},{48,32},{64,112},{80,64},{96,80},{112,96},{1... | collective-permute-start | bytes 442376 | tf_op jit(solution)/shard_map/ppermute | solution.py:94
  173.4 6.0 %collective-permute-start.17 = (bf16[192,384]{1,0:T(8,128)(2,1)S(1)}, bf16[192,384]{1,0:T(8,128)(2,1)S(1)}, u32[]{:S(2)}, u32[]{:S(2)}) collective-permute-start(bf16[192,384]{1,0:T(8,128)(2,1)S(1)} %fusion.41), channel_id=1, source_target_pairs={{0,192},{16,208},{32,224},{48,240},{64,0},{80,16},{96,32},{112,48}... | collective-permute-start | bytes 442376 | tf_op jit(solution)/shard_map/ppermute | solution.py:94
Sparse Core Ops, SparseCore 0:
  10.4 55.4 all-gather.2

commit v3 on v2

--- a/solution.py
+++ b/solution.py
@@ -98,6 +98,20 @@
     return state
 
 
+def ring_stage(ra, rb, pairs_a, pairs_b):
+    steps = ra["count"] - 1
+
+    def body(k, carry):
+        sa = dict(ra, acc_f=carry[0], acc_b=carry[1])
+        sb = dict(rb, acc_f=carry[2], acc_b=carry[3])
+        sa = ring_step(sa, k, *pairs_a)
+        sb = ring_step(sb, k, *pairs_b)
+        return (sa["acc_f"], sa["acc_b"], sb["acc_f"], sb["acc_b"])
+
+    carry = lax.fori_loop(0, steps, body, (ra["acc_f"], ra["acc_b"], rb["acc_f"], rb["acc_b"]))
+    return dict(ra, acc_f=carry[0], acc_b=carry[1]), dict(rb, acc_f=carry[2], acc_b=carry[3])
+
+
 def reduce_scatter_2d(part_in, part_out, nx, ny, x_pos, y_pos):
     def grid(part):
         rows = part.shape[0] // (nx * ny)
@@ -109,18 +123,10 @@
     y_f, y_b = ring_pairs(nx, ny, False, 1), ring_pairs(nx, ny, False, -1)
     ra = ring_start(gin[..., :hin], gout[..., :hout], nx, x_pos, axis=1)
     rb = ring_start(gin[..., hin:], gout[..., hout:], ny, y_pos)
-    for k in range(max(nx, ny) - 1):
-        if k < nx - 1:
-            ra = ring_step(ra, k, x_f, x_b)
-        if k < ny - 1:
-            rb = ring_step(rb, k, y_f, y_b)
+    ra, rb = ring_stage(ra, rb, (x_f, x_b), (y_f, y_b))
     ra = ring_start(ra["acc_f"], ra["acc_b"], ny, y_pos)
     rb = ring_start(rb["acc_f"], rb["acc_b"], nx, x_pos)
-    for k in range(max(nx, ny) - 1):
-        if k < ny - 1:
-            ra = ring_step(ra, k, y_f, y_b)
-        if k < nx - 1:
-            rb = ring_step(rb, k, x_f, x_b)
+    ra, rb = ring_stage(ra, rb, (y_f, y_b), (x_f, x_b))
     total_in = jnp.concatenate([ra["acc_f"], rb["acc_f"]], axis=-1)
     total_out = jnp.concatenate([ra["acc_b"], rb["acc_b"]], axis=-1)
     return total_in, total_out

time: 190 us -> 253 us (1.33)
  other arithmetic: 10.9 us -> 66.5 us
  local copies, waits for them, and re-layouts: 7.46 us -> 20.6 us
  starting transfers between devices: 53.2 us -> 45.7 us
  waiting for transfers between devices: 58.8 us -> 62.1 us
    ppermute x12, waiting for transfers between devices: 1.63 us -> 25.8 us  [ring_step(): got_b = lax.ppermute(state['acc_b'].astype(jnp.bfloat16), 'dp', bwd_pairs)]
    add x4 -> x12, other arithmetic: 0.42 us -> 22.8 us  [ring_step(): got_f.astype(jnp.float32)]
    ppermute x12, waiting for transfers between devices: 29 us -> 8.11 us  [ring_step(): got_f = lax.ppermute(state['acc_f'].astype(jnp.bfloat16), 'dp', fwd_pairs)]
    add x4 -> x12, other arithmetic: 0.3 us -> 13.8 us  [ring_step(): got_b.astype(jnp.float32)]
    while x0 -> x42, local copies, waits for them, and re-layouts: none -> 10.8 us
    convert_element_type x8 -> x12, other arithmetic: 0.72 us -> 9.53 us  [ring_step(): got_b = lax.ppermute(state['acc_b'].astype(jnp.bfloat16), 'dp', bwd_pairs)]
    convert_element_type x8 -> x12, other arithmetic: 0.73 us -> 7.77 us  [ring_step(): got_f = lax.ppermute(state['acc_f'].astype(jnp.bfloat16), 'dp', fwd_pairs)]
    ppermute x12, starting transfers between devices: 9.37 us -> 4.72 us  [ring_step(): got_f = lax.ppermute(state['acc_f'].astype(jnp.bfloat16), 'dp', fwd_pairs)]
  transfers between devices with their start and end apart: 27 -> 27, of which waited for: 13 -> 11; matrix products, arithmetic and copies ran while one was open for 12% -> 22% of each run, Pallas kernels for 0% -> 0%
where the time goes in v3:
time: 253 us; the launch traced here: 252 us
  other arithmetic  66.5 us (26%)
  waiting for transfers between devices  62.1 us (25%)
  starting transfers between devices  45.7 us (18%)
  matrix products  26.2 us (10%)
  local copies, waits for them, and re-layouts  20.6 us (8%)
  blocking collectives  15.9 us (6%)
  between operations  14.4 us (6%)
    ppermute x12, waiting for transfers between devices, ring_step(): got_b = lax.ppermute(state['acc_b'].astype(jnp.bfloat16), 'dp', bwd_pairs)  25.8 us
    ppermute x12, starting transfers between devices, ring_step(): got_b = lax.ppermute(state['acc_b'].astype(jnp.bfloat16), 'dp', bwd_pairs)  25.5 us
    add x12, other arithmetic, ring_step(): got_f.astype(jnp.float32)  22.8 us
    all_to_all x1, waiting for transfers between devices, on_device(): lax.all_to_all(outgoing, 'expert', split_axis=0, concat_axis=0, tiled=True)  20.8 us
    all_gather x1, blocking collectives, on_device(): delta_row = lax.all_gather(delta_seq, 'expert', axis=0, tiled=True)  15.9 us
    add x12, other arithmetic, ring_step(): got_b.astype(jnp.float32)  13.8 us
    while x42, local copies, waits for them, and re-layouts  10.8 us
    convert_element_type x12, other arithmetic, ring_step(): got_b = lax.ppermute(state['acc_b'].astype(jnp.bfloat16), 'dp', bwd_pairs)  9.53 us
  transfers between devices with their start and end apart: 27, of which 11 were waited for; matrix products, arithmetic and copies ran while one was open for 22% of the time, Pallas kernels for 0%

profile of v3, /device:TPU:32, one launch (start us, length us, event | category | flops | bytes accessed | tf_op | source)
XLA Modules:
  0.0 251.6 jit_solution(1723790840939710889)
XLA Ops:
  15.8 8.6 %all-to-all-start = ((bf16[16,32,896]{2,1,0:T(8,128)(2,1)}), bf16[16,32,896]{2,1,0:T(8,128)(2,1)S(1)}, u32[]{:S(2)}, u32[]{:S(2)}) async-start(bf16[16,32,896]{2,1,0:T(8,128)(2,1)} %pad_maximum_fusion), calls=%async_computation | async-start | bytes 1835008 | tf_op jit(solution)/shard_map/all_to_all | solution.py:174
  25.4 20.8 %all-to-all-done = bf16[16,32,896]{2,1,0:T(8,128)(2,1)S(1)} async-done(((bf16[16,32,896]{2,1,0:T(8,128)(2,1)}), bf16[16,32,896]{2,1,0:T(8,128)(2,1)S(1)}, u32[]{:S(2)}, u32[]{:S(2)}) %all-to-all-start) | async-done | bytes 917536 | tf_op jit(solution)/shard_map/all_to_all | solution.py:174
  46.8 4.5 %fusion.13 = f32[512,3072]{1,0:T(8,128)S(1)} fusion(bf16[512,768]{1,0:T(8,128)(2,1)S(1)} %bitcast.138, bf16[1,768,3072]{2,1,0:T(8,128)(2,1)} %param.15), kind=kOutput, calls=%fused_computation.27 | convolution fusion | flops 2415919104 | bytes 11796480 | tf_op jit(solution)/shard_map/dot_general | solution.py:182
  51.3 2.5 fusion.21
  58.3 6.8 %all-to-all-start.1 = ((f32[16,2,768]{2,1,0:T(2,128)}), f32[16,2,768]{2,1,0:T(2,128)S(1)}, u32[]{:S(2)}, u32[]{:S(2)}) async-start(f32[16,2,768]{2,1,0:T(2,128)} %reshape.126), calls=%async_computation.1 | async-start | bytes 196608 | tf_op jit(solution)/shard_map/all_to_all | solution.py:187
  65.2 6.7 %all-to-all-done.1 = f32[16,2,768]{2,1,0:T(2,128)S(1)} async-done(((f32[16,2,768]{2,1,0:T(2,128)}), f32[16,2,768]{2,1,0:T(2,128)S(1)}, u32[]{:S(2)}, u32[]{:S(2)}) %all-to-all-start.1) | async-done | bytes 98336 | tf_op jit(solution)/shard_map/all_to_all | solution.py:187
  72.1 2.7 %multiply_reduce_fusion = f32[2048]{0:T(1024)S(1)} fusion(bf16[2048,768]{1,0:T(8,128)(2,1)} %all-gather.3.cloned.1.call-done), kind=kLoop, calls=%fused_computation.17 | loop fusion | flops 4716544 | bytes 3153920 | tf_op jit(solution)/shard_map/reduce_sum | solution.py:200
  77.3 15.9 %all-gather = bf16[16,2,768]{2,1,0:T(2,128)(2,1)S(1)} all-gather(bf16[1,2,768]{2,1,0:T(2,128)(2,1)S(1)} %fusion.48), channel_id=1, replica_groups=mesh['dp'=16,'expert'=16] {'expert'}, dimensions={0}, use_global_device_ids=true | all-gather | bytes 52224 | tf_op jit(solution)/shard_map/all_gather | solution.py:217
  93.2 1.4 convolution_convert_fusion
  94.7 3.9 %fusion.18 = bf16[3072,32]{0,1:T(8,128)(2,1)S(1)} fusion(bf16[32,768]{1,0:T(8,128)(2,1)S(1)} %reshape.140, bf16[1,3072,768]{2,1,0:T(8,128)(2,1)} %param.16), kind=kOutput, calls=%fused_computation.30 | convolution fusion | flops 151093248 | bytes 4964352 | tf_op jit(solution)/shard_map/dot_general | solution.py:220
  100.3 4.3 %fusion.6 = bf16[512,3072]{1,0:T(8,128)(2,1)S(1)} fusion(f32[512,3072]{1,0:T(8,128)S(1)} %bitcast.136, bf16[32,512]{1,0:T(8,128)(2,1)S(1)} %convert_element_type.319, bf16[3072,32]{0,1:T(8,128)(2,1)S(1)} %fusion.18), kind=kOutput, calls=%fused_computation.16 | convolution fusion | flops 130547712 | bytes 9666560 | tf_op jit(solution)/shard_map/dot_general | solution.py:223
  104.6 2.9 %convolution_convert_fusion.1 = bf16[768,3072]{1,0:T(8,128)(2,1)S(1)} fusion(bf16[512,768]{1,0:T(8,128)(2,1)S(1)} %bitcast.139, bf16[512,3072]{1,0:T(8,128)(2,1)S(1)} %fusion.6), kind=kOutput, calls=%fused_computation.20 | convolution fusion | flops 2418278400 | bytes 8650752 | tf_op jit(solution)/shard_map/dot_general | solution.py:228
  108.3 1.5 bitcast_convert_fusion.1
  111.0 81.8 %while.44 = (s32[]{:T(128)}, f32[4,48,1536]{2,1,0:T(8,128)}, f32[4,192,384]{2,1,0:T(8,128)S(1)}, f32[4,48,1536]{2,1,0:T(8,128)}, f32[4,192,384]{2,1,0:T(8,128)S(...) while((s32[]{:T(128)}, f32[4,48,1536]{2,1,0:T(8,128)}, ...), condition=%wide.region_14.15_spmd, body=%wide.region_13.14_spmd.sunk | while | flops 4718638 | bytes 40108952 | solution.py:111
  112.0 3.0 %collective-permute-start.3 = (bf16[4,192,384]{2,1,0:T(8,128)(2,1)}, bf16[4,192,384]{2,1,0:T(8,128)(2,1)S(1)}, u32[]{:S(2)}, u32[]{:S(2)}) collective-permute-start(bf16[4,192,384]{2,1,0:T(8,128)(2,1)} %convert_element_type.418), channel_id=1, source_target_pairs={{0,192},{16,208},{32,224},{48,240},{64,0},{80,16},{96,32},{112,48}... | collective-permute-start | bytes 1769480 | tf_op jit(solution)/shard_map/while/body/eval_jaxpr/ppermute | solution.py:94
  115.9 2.9 %collective-permute-start.1 = (bf16[4,192,384]{2,1,0:T(8,128)(2,1)}, bf16[4,192,384]{2,1,0:T(8,128)(2,1)S(1)}, u32[]{:S(2)}, u32[]{:S(2)}) collective-permute-start(bf16[4,192,384]{2,1,0:T(8,128)(2,1)} %convert_element_type.416), channel_id=1, source_target_pairs={{0,48},{16,0},{32,16},{48,32},{64,112},{80,64},{96,80},{112,96},{1... | collective-permute-start | bytes 1769480 | tf_op jit(solution)/shard_map/while/body/eval_jaxpr/ppermute | solution.py:94
  119.8 8.6 %collective-permute-done.3 = bf16[4,192,384]{2,1,0:T(8,128)(2,1)S(1)} collective-permute-done((bf16[4,192,384]{2,1,0:T(8,128)(2,1)}, bf16[4,192,384]{2,1,0:T(8,128)(2,1)S(1)}, u32[]{:S(2)}, u32[]{:S(2)}) %collective-permute-start.3) | collective-permute-done | bytes 589856 | tf_op jit(solution)/shard_map/while/body/eval_jaxpr/ppermute | solution.py:94
  129.2 1.4 convert_add_fusion.11
  132.7 1.4 convert_add_fusion.9
  134.0 2.1 collective-permute-done.2
  136.2 2.4 convert_add_fusion.10
  138.6 2.4 convert_add_fusion.8
  143.3 2.6 %collective-permute-start.1 = (bf16[4,192,384]{2,1,0:T(8,128)(2,1)}, bf16[4,192,384]{2,1,0:T(8,128)(2,1)S(1)}, u32[]{:S(2)}, u32[]{:S(2)}) collective-permute-start(bf16[4,192,384]{2,1,0:T(8,128)(2,1)} %convert_element_type.416), channel_id=1, source_target_pairs={{0,48},{16,0},{32,16},{48,32},{64,112},{80,64},{96,80},{112,96},{1... | collective-permute-start | bytes 1769480 | tf_op jit(solution)/shard_map/while/body/eval_jaxpr/ppermute | solution.py:94
  147.9 8.4 %collective-permute-done.3 = bf16[4,192,384]{2,1,0:T(8,128)(2,1)S(1)} collective-permute-done((bf16[4,192,384]{2,1,0:T(8,128)(2,1)}, bf16[4,192,384]{2,1,0:T(8,128)(2,1)S(1)}, u32[]{:S(2)}, u32[]{:S(2)}) %collective-permute-start.3) | collective-permute-done | bytes 589856 | tf_op jit(solution)/shard_map/while/body/eval_jaxpr/ppermute | solution.py:94
  157.2 1.4 convert_add_fusion.11
  159.4 1.4 convert_add_fusion.9
  160.7 1.8 collective-permute-done.2
  162.5 2.4 convert_add_fusion.10
  164.9 2.4 convert_add_fusion.8
  169.7 2.6 %collective-permute-start.1 = (bf16[4,192,384]{2,1,0:T(8,128)(2,1)}, bf16[4,192,384]{2,1,0:T(8,128)(2,1)S(1)}, u32[]{:S(2)}, u32[]{:S(2)}) collective-permute-start(bf16[4,192,384]{2,1,0:T(8,128)(2,1)} %convert_element_type.416), channel_id=1, source_target_pairs={{0,48},{16,0},{32,16},{48,32},{64,112},{80,64},{96,80},{112,96},{1... | collective-permute-start | bytes 1769480 | tf_op jit(solution)/shard_map/while/body/eval_jaxpr/ppermute | solution.py:94
  174.3 7.6 %collective-permute-done.3 = bf16[4,192,384]{2,1,0:T(8,128)(2,1)S(1)} collective-permute-done((bf16[4,192,384]{2,1,0:T(8,128)(2,1)}, bf16[4,192,384]{2,1,0:T(8,128)(2,1)S(1)}, u32[]{:S(2)}, u32[]{:S(2)}) %collective-permute-start.3) | collective-permute-done | bytes 589856 | tf_op jit(solution)/shard_map/while/body/eval_jaxpr/ppermute | solution.py:94
  182.7 1.4 convert_add_fusion.11
  184.8 1.4 convert_add_fusion.9
  186.2 1.8 collective-permute-done.2
  188.0 2.4 convert_add_fusion.10
  190.4 2.4 convert_add_fusion.8
  192.9 1.8 dynamic-slice_bitcast_fusion.1
  194.7 47.4 %while.45 = (s32[]{:T(128)}, f32[48,1536]{1,0:T(8,128)}, f32[192,384]{1,0:T(8,128)S(1)}, f32[48,1536]{1,0:T(8,128)S(1)}, f32[192,384]{1,0:T(8,128)S(1)}, /*index...) while((s32[]{:T(128)}, f32[48,1536]{1,0:T(8,128)}, ...), condition=%wide.region_16.17_spmd, body=%wide.region_15.16_spmd.sunk | while | flops 884782 | bytes 8848269 | solution.py:111
  196.0 3.2 %collective-permute-start.7 = (bf16[192,384]{1,0:T(8,128)(2,1)}, bf16[192,384]{1,0:T(8,128)(2,1)S(1)}, u32[]{:S(2)}, u32[]{:S(2)}) collective-permute-start(bf16[192,384]{1,0:T(8,128)(2,1)} %convert_element_type.426), channel_id=1, source_target_pairs={{0,48},{16,0},{32,16},{48,32},{64,112},{80,64},{96,80},{112,96},{1... | collective-permute-start | bytes 442376 | tf_op jit(solution)/shard_map/while/body/eval_jaxpr/ppermute | solution.py:94
  201.4 1.6 collective-permute-start.4
  208.0 1.7 bitcast_add_fusion.8
  211.1 3.2 %collective-permute-start.7 = (bf16[192,384]{1,0:T(8,128)(2,1)}, bf16[192,384]{1,0:T(8,128)(2,1)S(1)}, u32[]{:S(2)}, u32[]{:S(2)}) collective-permute-start(bf16[192,384]{1,0:T(8,128)(2,1)} %convert_element_type.426), channel_id=1, source_target_pairs={{0,48},{16,0},{32,16},{48,32},{64,112},{80,64},{96,80},{112,96},{1... | collective-permute-start | bytes 442376 | tf_op jit(solution)/shard_map/while/body/eval_jaxpr/ppermute | solution.py:94
  215.0 1.7 collective-permute-start.5
  224.2 1.7 bitcast_add_fusion.8
  227.2 3.2 %collective-permute-start.7 = (bf16[192,384]{1,0:T(8,128)(2,1)}, bf16[192,384]{1,0:T(8,128)(2,1)S(1)}, u32[]{:S(2)}, u32[]{:S(2)}) collective-permute-start(bf16[192,384]{1,0:T(8,128)(2,1)} %convert_element_type.426), channel_id=1, source_target_pairs={{0,48},{16,0},{32,16},{48,32},{64,112},{80,64},{96,80},{112,96},{1... | collective-permute-start | bytes 442376 | tf_op jit(solution)/shard_map/while/body/eval_jaxpr/ppermute | solution.py:94
  231.2 1.7 collective-permute-start.5
  240.4 1.7 bitcast_add_fusion.8
  243.0 1.8 maximum_bitcast_fusion
  (193 shorter events, 66.9 us)
Async XLA Ops:
  7.2 3.7 %copy-start = (bf16[768,16]{0,1:T(8,128)(2,1)S(1)}, bf16[768,16]{0,1:T(8,128)(2,1)}, u32[]{:S(2)}) copy-start(bf16[768,16]{0,1:T(8,128)(2,1)} %param.14) | copy-start | bytes 73732
  7.2 64.9 %all-gather.3.cloned.1.call-start = ((), (), s32[]{:S(2)}) async-start(), calls=%async_computation.2 | async-start | bytes 3342336 | tf_op jit(solution)/shard_map/all_gather | solution.py:199
  14.3 10.8 %copy-start.15 = (s32[256,16]{0,1:T(8,128)S(1)}, s32[256,16]{0,1:T(8,128)}, u32[]{:S(2)}) copy-start(s32[256,16]{0,1:T(8,128)} %param.19) | copy-start | bytes 49156
  14.3 11.0 %copy-start.14 = (bf16[128,768]{1,0:T(8,128)(2,1)S(1)}, bf16[128,768]{1,0:T(8,128)(2,1)}, u32[]{:S(2)}) copy-start(bf16[128,768]{1,0:T(8,128)(2,1)} %param.12) | copy-start | bytes 589828
  15.8 30.4 %all-to-all-start = ((bf16[16,32,896]{2,1,0:T(8,128)(2,1)}), bf16[16,32,896]{2,1,0:T(8,128)(2,1)S(1)}, u32[]{:S(2)}, u32[]{:S(2)}) async-start(bf16[16,32,896]{2,1,0:T(8,128)(2,1)} %pad_maximum_fusion), calls=%async_computation | async-start | bytes 1835008 | tf_op jit(solution)/shard_map/all_to_all | solution.py:174
  46.8 7.8 %slice-start = ((s8[4718592]{0:T(1024)(128)(4,1)}), s8[524288]{0:T(1024)(128)(4,1)S(1)}, s32[]{:S(2)}) async-start(s8[4718592]{0:T(1024)(128)(4,1)} %bitcast.132), calls=%async_computation.3 | async-start | bytes 1048576
  51.3 3.2 %copy-start.10 = (f32[512,3072]{1,0:T(8,128)}, f32[512,3072]{1,0:T(8,128)S(1)}, u32[]{:S(2)}) copy-start(f32[512,3072]{1,0:T(8,128)S(1)} %fusion.13) | copy-start | bytes 18874372
  51.3 4.5 %slice-start.1 = ((s8[4718592]{0:T(1024)(128)(4,1)}), s8[4194304]{0:T(1024)(128)(4,1)S(1)}, s32[]{:S(2)}) async-start(s8[4718592]{0:T(1024)(128)(4,1)} %bitcast.132), calls=%async_computation.4 | async-start | bytes 8388608
  58.3 13.5 %all-to-all-start.1 = ((f32[16,2,768]{2,1,0:T(2,128)}), f32[16,2,768]{2,1,0:T(2,128)S(1)}, u32[]{:S(2)}, u32[]{:S(2)}) async-start(f32[16,2,768]{2,1,0:T(2,128)} %reshape.126), calls=%async_computation.1 | async-start | bytes 196608 | tf_op jit(solution)/shard_map/all_to_all | solution.py:187
  72.0 3.0 %copy-start.3 = (bf16[2048,768]{1,0:T(8,128)(2,1)S(1)}, bf16[2048,768]{1,0:T(8,128)(2,1)}, u32[]{:S(2)}) copy-start(bf16[2048,768]{1,0:T(8,128)(2,1)} %all-gather.3.cloned.1.call-done) | copy-start | bytes 9437188
  94.7 4.8 %slice-start.2 = ((s8[6291456]{0:T(1024)(128)(4,1)}), s8[4194304]{0:T(1024)(128)(4,1)S(1)}, s32[]{:S(2)}) async-start(s8[6291456]{0:T(1024)(128)(4,1)} %bitcast.135), calls=%async_computation.5 | async-start | bytes 8388608
  98.6 1.6 slice-start.3
  100.3 7.9 %copy-start.6 = (bf16[4,4,192,384]{3,2,1,0:T(8,128)(2,1)}, bf16[4,4,192,384]{3,2,1,0:T(8,128)(2,1)S(1)}, u32[]{:S(2)}) copy-start(bf16[4,4,192,384]{3,2,1,0:T(8,128)(2,1)S(1)} %get-tuple-element.942) | copy-start | bytes 7077892
  100.3 8.0 %copy-start.7 = (bf16[4,4,192,384]{3,2,1,0:T(8,128)(2,1)}, bf16[4,4,192,384]{3,2,1,0:T(8,128)(2,1)S(1)}, u32[]{:S(2)}) copy-start(bf16[4,4,192,384]{3,2,1,0:T(8,128)(2,1)S(1)} %get-tuple-element.938) | copy-start | bytes 7077892
  108.1 2.9 %copy-start.8 = (bf16[4,4,48,1536]{3,2,1,0:T(8,128)(2,1)}, bf16[4,4,48,1536]{3,2,1,0:T(8,128)(2,1)S(1)}, u32[]{:S(2)}) copy-start(bf16[4,4,48,1536]{3,2,1,0:T(8,128)(2,1)S(1)} %get-tuple-element.940) | copy-start | bytes 7077892
  108.1 2.9 %copy-start.9 = (bf16[4,4,48,1536]{3,2,1,0:T(8,128)(2,1)}, bf16[4,4,48,1536]{3,2,1,0:T(8,128)(2,1)S(1)}, u32[]{:S(2)}) copy-start(bf16[4,4,48,1536]{3,2,1,0:T(8,128)(2,1)S(1)} %get-tuple-element.936) | copy-start | bytes 7077892
  111.0 7.7 %copy-start.1 = (f32[4,48,1536]{2,1,0:T(8,128)S(1)}, f32[4,48,1536]{2,1,0:T(8,128)}, u32[]{:S(2)}) copy-start(f32[4,48,1536]{2,1,0:T(8,128)} %get-tuple-element.951) | copy-start | bytes 3538948 | tf_op jit(solution)/shard_map/while
  111.0 8.6 %copy-start.2 = (f32[4,48,1536]{2,1,0:T(8,128)S(1)}, f32[4,48,1536]{2,1,0:T(8,128)}, u32[]{:S(2)}) copy-start(f32[4,48,1536]{2,1,0:T(8,128)} %get-tuple-element.949) | copy-start | bytes 3538948 | tf_op jit(solution)/shard_map/while
  112.0 16.4 %collective-permute-start.3 = (bf16[4,192,384]{2,1,0:T(8,128)(2,1)}, bf16[4,192,384]{2,1,0:T(8,128)(2,1)S(1)}, u32[]{:S(2)}, u32[]{:S(2)}) collective-permute-start(bf16[4,192,384]{2,1,0:T(8,128)(2,1)} %convert_element_type.418), channel_id=1, source_target_pairs={{0,192},{16,208},{32,224},{48,240},{64,0},{80,16},{96,32},{112,48}... | collective-permute-start | bytes 1769480 | tf_op jit(solution)/shard_map/while/body/eval_jaxpr/ppermute | solution.py:94
  115.9 16.0 %collective-permute-start.1 = (bf16[4,192,384]{2,1,0:T(8,128)(2,1)}, bf16[4,192,384]{2,1,0:T(8,128)(2,1)S(1)}, u32[]{:S(2)}, u32[]{:S(2)}) collective-permute-start(bf16[4,192,384]{2,1,0:T(8,128)(2,1)} %convert_element_type.416), channel_id=1, source_target_pairs={{0,48},{16,0},{32,16},{48,32},{64,112},{80,64},{96,80},{112,96},{1... | collective-permute-start | bytes 1769480 | tf_op jit(solution)/shard_map/while/body/eval_jaxpr/ppermute | solution.py:94
  119.6 16.5 %collective-permute-start.2 = (bf16[4,48,1536]{2,1,0:T(8,128)(2,1)}, bf16[4,48,1536]{2,1,0:T(8,128)(2,1)}, u32[]{:S(2)}, u32[]{:S(2)}) collective-permute-start(bf16[4,48,1536]{2,1,0:T(8,128)(2,1)} %convert_element_type.417), channel_id=1, source_target_pairs={{0,64},{16,80},{32,96},{48,112},{64,128},{80,144},{96,160},{112,17... | collective-permute-start | bytes 1769480 | tf_op jit(solution)/shard_map/while/body/eval_jaxpr/ppermute | solution.py:93
  119.7 18.9 %collective-permute-start = (bf16[4,48,1536]{2,1,0:T(8,128)(2,1)S(1)}, bf16[4,48,1536]{2,1,0:T(8,128)(2,1)}, u32[]{:S(2)}, u32[]{:S(2)}) collective-permute-start(bf16[4,48,1536]{2,1,0:T(8,128)(2,1)S(1)} %convert_element_type.415), channel_id=1, source_target_pairs={{0,16},{16,32},{32,48},{48,0},{64,80},{80,96},{96,112},{112,64},{1... | collective-permute-start | bytes 1769480 | tf_op jit(solution)/shard_map/while/body/eval_jaxpr/ppermute | solution.py:93
  141.0 4.9 %copy-start.1 = (f32[4,48,1536]{2,1,0:T(8,128)S(1)}, f32[4,48,1536]{2,1,0:T(8,128)}, u32[]{:S(2)}) copy-start(f32[4,48,1536]{2,1,0:T(8,128)} %get-tuple-element.951) | copy-start | bytes 3538948 | tf_op jit(solution)/shard_map/while
  141.0 6.2 %copy-start.2 = (f32[4,48,1536]{2,1,0:T(8,128)S(1)}, f32[4,48,1536]{2,1,0:T(8,128)}, u32[]{:S(2)}) copy-start(f32[4,48,1536]{2,1,0:T(8,128)} %get-tuple-element.949) | copy-start | bytes 3538948 | tf_op jit(solution)/shard_map/while
  142.0 14.4 %collective-permute-start.3 = (bf16[4,192,384]{2,1,0:T(8,128)(2,1)}, bf16[4,192,384]{2,1,0:T(8,128)(2,1)S(1)}, u32[]{:S(2)}, u32[]{:S(2)}) collective-permute-start(bf16[4,192,384]{2,1,0:T(8,128)(2,1)} %convert_element_type.418), channel_id=1, source_target_pairs={{0,192},{16,208},{32,224},{48,240},{64,0},{80,16},{96,32},{112,48}... | collective-permute-start | bytes 1769480 | tf_op jit(solution)/shard_map/while/body/eval_jaxpr/ppermute | solution.py:94
  143.3 15.2 %collective-permute-start.1 = (bf16[4,192,384]{2,1,0:T(8,128)(2,1)}, bf16[4,192,384]{2,1,0:T(8,128)(2,1)S(1)}, u32[]{:S(2)}, u32[]{:S(2)}) collective-permute-start(bf16[4,192,384]{2,1,0:T(8,128)(2,1)} %convert_element_type.416), channel_id=1, source_target_pairs={{0,48},{16,0},{32,16},{48,32},{64,112},{80,64},{96,80},{112,96},{1... | collective-permute-start | bytes 1769480 | tf_op jit(solution)/shard_map/while/body/eval_jaxpr/ppermute | solution.py:94
  146.8 15.7 %collective-permute-start.2 = (bf16[4,48,1536]{2,1,0:T(8,128)(2,1)}, bf16[4,48,1536]{2,1,0:T(8,128)(2,1)}, u32[]{:S(2)}, u32[]{:S(2)}) collective-permute-start(bf16[4,48,1536]{2,1,0:T(8,128)(2,1)} %convert_element_type.417), channel_id=1, source_target_pairs={{0,64},{16,80},{32,96},{48,112},{64,128},{80,144},{96,160},{112,17... | collective-permute-start | bytes 1769480 | tf_op jit(solution)/shard_map/while/body/eval_jaxpr/ppermute | solution.py:93
  147.3 17.6 %collective-permute-start = (bf16[4,48,1536]{2,1,0:T(8,128)(2,1)S(1)}, bf16[4,48,1536]{2,1,0:T(8,128)(2,1)}, u32[]{:S(2)}, u32[]{:S(2)}) collective-permute-start(bf16[4,48,1536]{2,1,0:T(8,128)(2,1)S(1)} %convert_element_type.415), channel_id=1, source_target_pairs={{0,16},{16,32},{32,48},{48,0},{64,80},{80,96},{96,112},{112,64},{1... | collective-permute-start | bytes 1769480 | tf_op jit(solution)/shard_map/while/body/eval_jaxpr/ppermute | solution.py:93
  156.3 0.8 copy-start.5
  167.4 4.9 %copy-start.1 = (f32[4,48,1536]{2,1,0:T(8,128)S(1)}, f32[4,48,1536]{2,1,0:T(8,128)}, u32[]{:S(2)}) copy-start(f32[4,48,1536]{2,1,0:T(8,128)} %get-tuple-element.951) | copy-start | bytes 3538948 | tf_op jit(solution)/shard_map/while
  167.4 6.2 %copy-start.2 = (f32[4,48,1536]{2,1,0:T(8,128)S(1)}, f32[4,48,1536]{2,1,0:T(8,128)}, u32[]{:S(2)}) copy-start(f32[4,48,1536]{2,1,0:T(8,128)} %get-tuple-element.949) | copy-start | bytes 3538948 | tf_op jit(solution)/shard_map/while
  168.3 13.5 %collective-permute-start.3 = (bf16[4,192,384]{2,1,0:T(8,128)(2,1)}, bf16[4,192,384]{2,1,0:T(8,128)(2,1)S(1)}, u32[]{:S(2)}, u32[]{:S(2)}) collective-permute-start(bf16[4,192,384]{2,1,0:T(8,128)(2,1)} %convert_element_type.418), channel_id=1, source_target_pairs={{0,192},{16,208},{32,224},{48,240},{64,0},{80,16},{96,32},{112,48}... | collective-permute-start | bytes 1769480 | tf_op jit(solution)/shard_map/while/body/eval_jaxpr/ppermute | solution.py:94
  169.7 14.4 %collective-permute-start.1 = (bf16[4,192,384]{2,1,0:T(8,128)(2,1)}, bf16[4,192,384]{2,1,0:T(8,128)(2,1)S(1)}, u32[]{:S(2)}, u32[]{:S(2)}) collective-permute-start(bf16[4,192,384]{2,1,0:T(8,128)(2,1)} %convert_element_type.416), channel_id=1, source_target_pairs={{0,48},{16,0},{32,16},{48,32},{64,112},{80,64},{96,80},{112,96},{1... | collective-permute-start | bytes 1769480 | tf_op jit(solution)/shard_map/while/body/eval_jaxpr/ppermute | solution.py:94
  173.2 14.8 %collective-permute-start.2 = (bf16[4,48,1536]{2,1,0:T(8,128)(2,1)}, bf16[4,48,1536]{2,1,0:T(8,128)(2,1)}, u32[]{:S(2)}, u32[]{:S(2)}) collective-permute-start(bf16[4,48,1536]{2,1,0:T(8,128)(2,1)} %convert_element_type.417), channel_id=1, source_target_pairs={{0,64},{16,80},{32,96},{48,112},{64,128},{80,144},{96,160},{112,17... | collective-permute-start | bytes 1769480 | tf_op jit(solution)/shard_map/while/body/eval_jaxpr/ppermute | solution.py:93
  173.7 16.8 %collective-permute-start = (bf16[4,48,1536]{2,1,0:T(8,128)(2,1)S(1)}, bf16[4,48,1536]{2,1,0:T(8,128)(2,1)}, u32[]{:S(2)}, u32[]{:S(2)}) collective-permute-start(bf16[4,48,1536]{2,1,0:T(8,128)(2,1)S(1)} %convert_element_type.415), channel_id=1, source_target_pairs={{0,16},{16,32},{32,48},{48,0},{64,80},{80,96},{96,112},{112,64},{1... | collective-permute-start | bytes 1769480 | tf_op jit(solution)/shard_map/while/body/eval_jaxpr/ppermute | solution.py:93
  181.8 0.8 copy-start.5
  195.4 7.7 %collective-permute-start.6 = (bf16[48,1536]{1,0:T(8,128)(2,1)}, bf16[48,1536]{1,0:T(8,128)(2,1)S(1)}, u32[]{:S(2)}, u32[]{:S(2)}) collective-permute-start(bf16[48,1536]{1,0:T(8,128)(2,1)} %convert_element_type.425), channel_id=1, source_target_pairs={{0,16},{16,32},{32,48},{48,0},{64,80},{80,96},{96,112},{112,64},{1... | collective-permute-start | bytes 442376 | tf_op jit(solution)/shard_map/while/body/eval_jaxpr/ppermute | solution.py:93
  196.0 8.7 %collective-permute-start.7 = (bf16[192,384]{1,0:T(8,128)(2,1)}, bf16[192,384]{1,0:T(8,128)(2,1)S(1)}, u32[]{:S(2)}, u32[]{:S(2)}) collective-permute-start(bf16[192,384]{1,0:T(8,128)(2,1)} %convert_element_type.426), channel_id=1, source_target_pairs={{0,48},{16,0},{32,16},{48,32},{64,112},{80,64},{96,80},{112,96},{1... | collective-permute-start | bytes 442376 | tf_op jit(solution)/shard_map/while/body/eval_jaxpr/ppermute | solution.py:94
  200.0 6.4 %collective-permute-start.5 = (bf16[192,384]{1,0:T(8,128)(2,1)}, bf16[192,384]{1,0:T(8,128)(2,1)S(1)}, u32[]{:S(2)}, u32[]{:S(2)}) collective-permute-start(bf16[192,384]{1,0:T(8,128)(2,1)} %convert_element_type.424), channel_id=1, source_target_pairs={{0,192},{16,208},{32,224},{48,240},{64,0},{80,16},{96,32},{112,48}... | collective-permute-start | bytes 442376 | tf_op jit(solution)/shard_map/while/body/eval_jaxpr/ppermute | solution.py:94
  201.4 6.6 %collective-permute-start.4 = (bf16[48,1536]{1,0:T(8,128)(2,1)S(1)}, bf16[48,1536]{1,0:T(8,128)(2,1)}, u32[]{:S(2)}, u32[]{:S(2)}) collective-permute-start(bf16[48,1536]{1,0:T(8,128)(2,1)S(1)} %convert_element_type.423), channel_id=1, source_target_pairs={{0,64},{16,80},{32,96},{48,112},{64,128},{80,144},{96,160},{112,17... | collective-permute-start | bytes 442376 | tf_op jit(solution)/shard_map/while/body/eval_jaxpr/ppermute | solution.py:93
  210.4 7.7 %collective-permute-start.6 = (bf16[48,1536]{1,0:T(8,128)(2,1)}, bf16[48,1536]{1,0:T(8,128)(2,1)S(1)}, u32[]{:S(2)}, u32[]{:S(2)}) collective-permute-start(bf16[48,1536]{1,0:T(8,128)(2,1)} %convert_element_type.425), channel_id=1, source_target_pairs={{0,16},{16,32},{32,48},{48,0},{64,80},{80,96},{96,112},{112,64},{1... | collective-permute-start | bytes 442376 | tf_op jit(solution)/shard_map/while/body/eval_jaxpr/ppermute | solution.py:93
  211.1 8.6 %collective-permute-start.7 = (bf16[192,384]{1,0:T(8,128)(2,1)}, bf16[192,384]{1,0:T(8,128)(2,1)S(1)}, u32[]{:S(2)}, u32[]{:S(2)}) collective-permute-start(bf16[192,384]{1,0:T(8,128)(2,1)} %convert_element_type.426), channel_id=1, source_target_pairs={{0,48},{16,0},{32,16},{48,32},{64,112},{80,64},{96,80},{112,96},{1... | collective-permute-start | bytes 442376 | tf_op jit(solution)/shard_map/while/body/eval_jaxpr/ppermute | solution.py:94
  215.0 6.4 %collective-permute-start.5 = (bf16[192,384]{1,0:T(8,128)(2,1)}, bf16[192,384]{1,0:T(8,128)(2,1)S(1)}, u32[]{:S(2)}, u32[]{:S(2)}) collective-permute-start(bf16[192,384]{1,0:T(8,128)(2,1)} %convert_element_type.424), channel_id=1, source_target_pairs={{0,192},{16,208},{32,224},{48,240},{64,0},{80,16},{96,32},{112,48}... | collective-permute-start | bytes 442376 | tf_op jit(solution)/shard_map/while/body/eval_jaxpr/ppermute | solution.py:94
  217.6 6.5 %collective-permute-start.4 = (bf16[48,1536]{1,0:T(8,128)(2,1)S(1)}, bf16[48,1536]{1,0:T(8,128)(2,1)}, u32[]{:S(2)}, u32[]{:S(2)}) collective-permute-start(bf16[48,1536]{1,0:T(8,128)(2,1)S(1)} %convert_element_type.423), channel_id=1, source_target_pairs={{0,64},{16,80},{32,96},{48,112},{64,128},{80,144},{96,160},{112,17... | collective-permute-start | bytes 442376 | tf_op jit(solution)/shard_map/while/body/eval_jaxpr/ppermute | solution.py:93
  226.6 7.7 %collective-permute-start.6 = (bf16[48,1536]{1,0:T(8,128)(2,1)}, bf16[48,1536]{1,0:T(8,128)(2,1)S(1)}, u32[]{:S(2)}, u32[]{:S(2)}) collective-permute-start(bf16[48,1536]{1,0:T(8,128)(2,1)} %convert_element_type.425), channel_id=1, source_target_pairs={{0,16},{16,32},{32,48},{48,0},{64,80},{80,96},{96,112},{112,64},{1... | collective-permute-start | bytes 442376 | tf_op jit(solution)/shard_map/while/body/eval_jaxpr/ppermute | solution.py:93
  227.2 8.7 %collective-permute-start.7 = (bf16[192,384]{1,0:T(8,128)(2,1)}, bf16[192,384]{1,0:T(8,128)(2,1)S(1)}, u32[]{:S(2)}, u32[]{:S(2)}) collective-permute-start(bf16[192,384]{1,0:T(8,128)(2,1)} %convert_element_type.426), channel_id=1, source_target_pairs={{0,48},{16,0},{32,16},{48,32},{64,112},{80,64},{96,80},{112,96},{1... | collective-permute-start | bytes 442376 | tf_op jit(solution)/shard_map/while/body/eval_jaxpr/ppermute | solution.py:94
  231.2 6.4 %collective-permute-start.5 = (bf16[192,384]{1,0:T(8,128)(2,1)}, bf16[192,384]{1,0:T(8,128)(2,1)S(1)}, u32[]{:S(2)}, u32[]{:S(2)}) collective-permute-start(bf16[192,384]{1,0:T(8,128)(2,1)} %convert_element_type.424), channel_id=1, source_target_pairs={{0,192},{16,208},{32,224},{48,240},{64,0},{80,16},{96,32},{112,48}... | collective-permute-start | bytes 442376 | tf_op jit(solution)/shard_map/while/body/eval_jaxpr/ppermute | solution.py:94
  233.9 6.5 %collective-permute-start.4 = (bf16[48,1536]{1,0:T(8,128)(2,1)S(1)}, bf16[48,1536]{1,0:T(8,128)(2,1)}, u32[]{:S(2)}, u32[]{:S(2)}) collective-permute-start(bf16[48,1536]{1,0:T(8,128)(2,1)S(1)} %convert_element_type.423), channel_id=1, source_target_pairs={{0,64},{16,80},{32,96},{48,112},{64,128},{80,144},{96,160},{112,17... | collective-permute-start | bytes 442376 | tf_op jit(solution)/shard_map/while/body/eval_jaxpr/ppermute | solution.py:93
  (13 other events, 9.2 us)
Sparse Core Ops, SparseCore 0:
  10.4 55.3 all-gather.2

commit v4 on v2

--- a/solution.py
+++ b/solution.py
@@ -3,13 +3,13 @@
 from jax import lax
 from jax.sharding import PartitionSpec as P
 
+
 LEN = 64
 
 
 SCORE_SCALE = 20.0
 LOSS_SCALE = 64.0
 EPSILON = 1e-06
-HIGHEST = lax.Precision.HIGHEST
 
 
 def gelu_parts(pre_act):
@@ -126,9 +126,8 @@
     return total_in, total_out
 
 
-def on_device(tokens, expert_ids, router, weight_in, weight_out, premises, positive, tile_mask):
+def device_body(tokens, expert_ids, router, weight_in, weight_out, premises, positive, tile_mask):
     token_count, model_width = tokens.shape
-    ffn_width = weight_in.shape[2]
     experts = router.shape[1]
     expert_size = lax.axis_size("expert")
     dp_size = lax.axis_size("dp")
@@ -244,5 +243,5 @@
     )
     out_specs = (P("expert", "dp", None), P("expert", "dp", None))
     return jax.shard_map(
-        on_device, mesh=mesh, in_specs=in_specs, out_specs=out_specs, check_vma=False
-    )
+        device_body, mesh=mesh, in_specs=in_specs, out_specs=out_specs, check_vma=False
+    )

time: 190 us -> 190 us (level)
  no operation moved by 1% of the time
where the time goes in v4:
time: 190 us; the launch traced here: 187 us
  waiting for transfers between devices  58.8 us (31%)
  starting transfers between devices  53.2 us (28%)
  matrix products  26.3 us (14%)
  blocking collectives  16.1 us (8%)
  between operations  14.5 us (8%)
  other arithmetic  10.9 us (6%)
  local copies, waits for them, and re-layouts  7.46 us (4%)
    ppermute x12, waiting for transfers between devices, ring_step(): got_f = lax.ppermute(state['acc_f'].astype(jnp.bfloat16), 'dp', fwd_pairs)  29 us
    ppermute x12, starting transfers between devices, ring_step(): got_b = lax.ppermute(state['acc_b'].astype(jnp.bfloat16), 'dp', bwd_pairs)  28.4 us
    all_to_all x1, waiting for transfers between devices, device_body(): lax.all_to_all(outgoing, 'expert', split_axis=0, concat_axis=0, tiled=True)  20.8 us
    all_gather x1, blocking collectives, device_body(): delta_row = lax.all_gather(delta_seq, 'expert', axis=0, tiled=True)  16.1 us
    ppermute x12, starting transfers between devices, ring_step(): got_f = lax.ppermute(state['acc_f'].astype(jnp.bfloat16), 'dp', fwd_pairs)  9.37 us
    all_to_all x1, starting transfers between devices, device_body(): lax.all_to_all(outgoing, 'expert', split_axis=0, concat_axis=0, tiled=True)  8.59 us
    all_to_all x1, starting transfers between devices, device_body(): lax.all_to_all(moe_seq.reshape(expert_size, seq_count, model_width), 'exp...  6.8 us
    all_to_all x1, waiting for transfers between devices, device_body(): lax.all_to_all(moe_seq.reshape(expert_size, seq_count, model_width), 'exp...  6.67 us
  transfers between devices with their start and end apart: 27, of which 13 were waited for; matrix products, arithmetic and copies ran while one was open for 12% of the time, Pallas kernels for 0%

profile of v4, /device:TPU:32, one launch (start us, length us, event | category | flops | bytes accessed | tf_op | source)
XLA Modules:
  0.0 187.2 jit_solution(12813352929124780141)
XLA Ops:
  7.9 0.8 copy.66
  10.8 1.0 fusion.82
  11.9 0.8 select_reduce_fusion.1
  13.1 1.3 fusion.49
  14.8 1.0 pad_maximum_fusion
  15.8 8.6 %all-to-all-start = ((bf16[16,32,896]{2,1,0:T(8,128)(2,1)}), bf16[16,32,896]{2,1,0:T(8,128)(2,1)S(1)}, u32[]{:S(2)}, u32[]{:S(2)}) async-start(bf16[16,32,896]{2,1,0:T(8,128)(2,1)} %pad_maximum_fusion), calls=%async_computation | async-start | bytes 1835008 | tf_op jit(solution)/shard_map/all_to_all | solution.py:167
  24.4 0.8 dynamic_slice.110
  25.4 20.8 %all-to-all-done = bf16[16,32,896]{2,1,0:T(8,128)(2,1)S(1)} async-done(((bf16[16,32,896]{2,1,0:T(8,128)(2,1)}), bf16[16,32,896]{2,1,0:T(8,128)(2,1)S(1)}, u32[]{:S(2)}, u32[]{:S(2)}) %all-to-all-start) | async-done | bytes 917536 | tf_op jit(solution)/shard_map/all_to_all | solution.py:167
  46.8 4.5 %fusion.13 = f32[512,3072]{1,0:T(8,128)S(1)} fusion(bf16[512,768]{1,0:T(8,128)(2,1)S(1)} %bitcast.178, bf16[1,768,3072]{2,1,0:T(8,128)(2,1)} %param.11), kind=kOutput, calls=%fused_computation.19 | convolution fusion | flops 2415919104 | bytes 11796480 | tf_op jit(solution)/shard_map/dot_general | solution.py:175
  51.3 2.5 %fusion.21 = f32[32,3072]{1,0:T(8,128)S(1)} fusion(bf16[32,512]{1,0:T(8,128)(2,1)S(1)} %convert_element_type.307, f32[512,3072]{1,0:T(8,128)S(1)} %fusion.13), kind=kOutput, calls=%fused_computation.23 | convolution fusion | flops 114819072 | bytes 6717440 | tf_op jit(solution)/shard_map/dot_general | solution.py:178
  54.5 1.3 slice-done.1
  55.8 0.9 fusion.9
  56.7 0.9 fusion.32
  58.3 6.8 %all-to-all-start.1 = ((f32[16,2,768]{2,1,0:T(2,128)}), f32[16,2,768]{2,1,0:T(2,128)S(1)}, u32[]{:S(2)}, u32[]{:S(2)}) async-start(f32[16,2,768]{2,1,0:T(2,128)} %reshape.138), calls=%async_computation.1 | async-start | bytes 196608 | tf_op jit(solution)/shard_map/all_to_all | solution.py:180
  65.2 6.7 %all-to-all-done.1 = f32[16,2,768]{2,1,0:T(2,128)S(1)} async-done(((f32[16,2,768]{2,1,0:T(2,128)}), f32[16,2,768]{2,1,0:T(2,128)S(1)}, u32[]{:S(2)}, u32[]{:S(2)}) %all-to-all-start.1) | async-done | bytes 98336 | tf_op jit(solution)/shard_map/all_to_all | solution.py:180
  72.0 2.7 %multiply_reduce_fusion = f32[2048]{0:T(1024)S(1)} fusion(bf16[2048,768]{1,0:T(8,128)(2,1)} %all-gather.3.cloned.1.call-done), kind=kLoop, calls=%fused_computation.9 | loop fusion | flops 4716544 | bytes 3153920 | tf_op jit(solution)/shard_map/reduce_sum | solution.py:193
  75.0 1.0 fusion.81
  77.3 16.1 %all-gather = bf16[16,2,768]{2,1,0:T(2,128)(2,1)S(1)} all-gather(bf16[1,2,768]{2,1,0:T(2,128)(2,1)S(1)} %fusion.69), channel_id=1, replica_groups=mesh['dp'=16,'expert'=16] {'expert'}, dimensions={0}, use_global_device_ids=true | all-gather | bytes 52224 | tf_op jit(solution)/shard_map/all_gather | solution.py:210
  93.4 3.9 %fusion.18 = bf16[3072,32]{0,1:T(8,128)(2,1)S(1)} fusion(bf16[32,768]{1,0:T(8,128)(2,1)S(1)} %reshape.156, bf16[1,3072,768]{2,1,0:T(8,128)(2,1)} %param.12), kind=kOutput, calls=%fused_computation.22 | convolution fusion | flops 151093248 | bytes 4964352 | tf_op jit(solution)/shard_map/dot_general | solution.py:213
  97.4 1.5 convolution_convert_fusion
  98.9 4.3 %fusion.6 = bf16[512,3072]{1,0:T(8,128)(2,1)S(1)} fusion(f32[512,3072]{1,0:T(8,128)S(1)} %bitcast.176, bf16[32,512]{1,0:T(8,128)(2,1)S(1)} %convert_element_type.307, bf16[3072,32]{0,1:T(8,128)(2,1)S(1)} %fusion.18), kind=kOutput, calls=%fused_computation.8 | convolution fusion | flops 130547712 | bytes 9666560 | tf_op jit(solution)/shard_map/dot_general | solution.py:216
  103.2 2.9 %convolution_convert_fusion.1 = bf16[768,3072]{1,0:T(8,128)(2,1)S(1)} fusion(bf16[512,768]{1,0:T(8,128)(2,1)S(1)} %bitcast.179, bf16[512,3072]{1,0:T(8,128)(2,1)S(1)} %fusion.6), kind=kOutput, calls=%fused_computation.12 | convolution fusion | flops 2418278400 | bytes 8650752 | tf_op jit(solution)/shard_map/dot_general | solution.py:221
  106.8 1.6 collective-permute-start.6
  108.5 1.5 collective-permute-start
  110.0 0.8 fusion.79
  110.9 1.8 collective-permute-start.18
  112.8 1.8 collective-permute-start.12
  114.6 9.1 %collective-permute-done.6 = bf16[4,48,1536]{2,1,0:T(8,128)(2,1)S(1)} collective-permute-done((bf16[4,48,1536]{2,1,0:T(8,128)(2,1)S(1)}, bf16[4,48,1536]{2,1,0:T(8,128)(2,1)S(1)}, u32[]{:S(2)}, u32[]{:S(2)}) %collective-permute-start.6) | collective-permute-done | bytes 589856 | tf_op jit(solution)/shard_map/ppermute | solution.py:93
  124.2 0.8 collective-permute-done
  126.2 3.1 %collective-permute-start.19 = (bf16[4,192,384]{2,1,0:T(8,128)(2,1)S(1)}, bf16[4,192,384]{2,1,0:T(8,128)(2,1)S(1)}, u32[]{:S(2)}, u32[]{:S(2)}) collective-permute-start(bf16[4,192,384]{2,1,0:T(8,128)(2,1)S(1)} %fusion.25), channel_id=1, source_target_pairs={{0,192},{16,208},{32,224},{48,240},{64,0},{80,16},{96,32},{112,48}... | collective-permute-start | bytes 1769480 | tf_op jit(solution)/shard_map/ppermute | solution.py:94
  129.5 2.0 %collective-permute-start.13 = (bf16[4,192,384]{2,1,0:T(8,128)(2,1)S(1)}, bf16[4,192,384]{2,1,0:T(8,128)(2,1)S(1)}, u32[]{:S(2)}, u32[]{:S(2)}) collective-permute-start(bf16[4,192,384]{2,1,0:T(8,128)(2,1)S(1)} %fusion.27), channel_id=1, source_target_pairs={{0,48},{16,0},{32,16},{48,32},{64,112},{80,64},{96,80},{112,96},{1... | collective-permute-start | bytes 1769480 | tf_op jit(solution)/shard_map/ppermute | solution.py:94
  131.5 8.5 %collective-permute-done.7 = bf16[4,48,1536]{2,1,0:T(8,128)(2,1)S(1)} collective-permute-done((bf16[4,48,1536]{2,1,0:T(8,128)(2,1)S(1)}, bf16[4,48,1536]{2,1,0:T(8,128)(2,1)S(1)}, u32[]{:S(2)}, u32[]{:S(2)}) %collective-permute-start.7) | collective-permute-done | bytes 589856 | tf_op jit(solution)/shard_map/ppermute | solution.py:93
  141.1 1.0 collective-permute-start.2
  142.3 3.3 %collective-permute-start.20 = (bf16[4,192,384]{2,1,0:T(8,128)(2,1)S(1)}, bf16[4,192,384]{2,1,0:T(8,128)(2,1)S(1)}, u32[]{:S(2)}, u32[]{:S(2)}) collective-permute-start(bf16[4,192,384]{2,1,0:T(8,128)(2,1)S(1)} %fusion.24), channel_id=1, source_target_pairs={{0,192},{16,208},{32,224},{48,240},{64,0},{80,16},{96,32},{112,48}... | collective-permute-start | bytes 1769480 | tf_op jit(solution)/shard_map/ppermute | solution.py:94
  145.7 1.7 collective-permute-start.14
  147.4 7.9 %collective-permute-done.8 = bf16[4,48,1536]{2,1,0:T(8,128)(2,1)S(1)} collective-permute-done((bf16[4,48,1536]{2,1,0:T(8,128)(2,1)S(1)}, bf16[4,48,1536]{2,1,0:T(8,128)(2,1)S(1)}, u32[]{:S(2)}, u32[]{:S(2)}) %collective-permute-start.8) | collective-permute-done | bytes 589856 | tf_op jit(solution)/shard_map/ppermute | solution.py:93
  155.5 1.8 collective-permute-start.9
  157.6 0.9 collective-permute-start.3
  158.6 0.8 collective-permute-start.21
  159.9 3.0 %collective-permute-start.15 = (bf16[192,384]{1,0:T(8,128)(2,1)S(1)}, bf16[192,384]{1,0:T(8,128)(2,1)S(1)}, u32[]{:S(2)}, u32[]{:S(2)}) collective-permute-start(bf16[192,384]{1,0:T(8,128)(2,1)S(1)} %fusion.55), channel_id=1, source_target_pairs={{0,192},{16,208},{32,224},{48,240},{64,0},{80,16},{96,32},{112,48}... | collective-permute-start | bytes 442376 | tf_op jit(solution)/shard_map/ppermute | solution.py:94
  164.5 2.0 %collective-permute-start.22 = (bf16[192,384]{1,0:T(8,128)(2,1)S(1)}, bf16[192,384]{1,0:T(8,128)(2,1)S(1)}, u32[]{:S(2)}, u32[]{:S(2)}) collective-permute-start(bf16[192,384]{1,0:T(8,128)(2,1)S(1)} %fusion.40), channel_id=1, source_target_pairs={{0,48},{16,0},{32,16},{48,32},{64,112},{80,64},{96,80},{112,96},{1... | collective-permute-start | bytes 442376 | tf_op jit(solution)/shard_map/ppermute | solution.py:94
  166.5 3.3 %collective-permute-start.16 = (bf16[192,384]{1,0:T(8,128)(2,1)S(1)}, bf16[192,384]{1,0:T(8,128)(2,1)S(1)}, u32[]{:S(2)}, u32[]{:S(2)}) collective-permute-start(bf16[192,384]{1,0:T(8,128)(2,1)S(1)} %fusion.42), channel_id=1, source_target_pairs={{0,192},{16,208},{32,224},{48,240},{64,0},{80,16},{96,32},{112,48}... | collective-permute-start | bytes 442376 | tf_op jit(solution)/shard_map/ppermute | solution.py:94
  170.1 0.8 collective-permute-done.4
  171.1 2.3 %collective-permute-start.23 = (bf16[192,384]{1,0:T(8,128)(2,1)S(1)}, bf16[192,384]{1,0:T(8,128)(2,1)S(1)}, u32[]{:S(2)}, u32[]{:S(2)}) collective-permute-start(bf16[192,384]{1,0:T(8,128)(2,1)S(1)} %fusion.39), channel_id=1, source_target_pairs={{0,48},{16,0},{32,16},{48,32},{64,112},{80,64},{96,80},{112,96},{1... | collective-permute-start | bytes 442376 | tf_op jit(solution)/shard_map/ppermute | solution.py:94
  173.4 3.4 %collective-permute-start.17 = (bf16[192,384]{1,0:T(8,128)(2,1)S(1)}, bf16[192,384]{1,0:T(8,128)(2,1)S(1)}, u32[]{:S(2)}, u32[]{:S(2)}) collective-permute-start(bf16[192,384]{1,0:T(8,128)(2,1)S(1)} %fusion.41), channel_id=1, source_target_pairs={{0,192},{16,208},{32,224},{48,240},{64,0},{80,16},{96,32},{112,48}... | collective-permute-start | bytes 442376 | tf_op jit(solution)/shard_map/ppermute | solution.py:94
  177.4 0.9 maximum_bitcast_fusion
  178.3 1.2 collective-permute-done.17
  179.5 0.9 maximum_bitcast_fusion.1
  (121 shorter events, 15.4 us)
Async XLA Ops:
  7.2 3.7 %copy-start = (bf16[768,16]{0,1:T(8,128)(2,1)S(1)}, bf16[768,16]{0,1:T(8,128)(2,1)}, u32[]{:S(2)}) copy-start(bf16[768,16]{0,1:T(8,128)(2,1)} %param.10) | copy-start | bytes 73732
  7.2 64.8 %all-gather.3.cloned.1.call-start = ((), (), s32[]{:S(2)}) async-start(), calls=%async_computation.2 | async-start | bytes 3342336 | tf_op jit(solution)/shard_map/all_gather | solution.py:192
  14.4 10.7 %copy-start.5 = (s32[256,16]{0,1:T(8,128)S(1)}, s32[256,16]{0,1:T(8,128)}, u32[]{:S(2)}) copy-start(s32[256,16]{0,1:T(8,128)} %param.15) | copy-start | bytes 49156
  14.5 10.9 %copy-start.4 = (bf16[128,768]{1,0:T(8,128)(2,1)S(1)}, bf16[128,768]{1,0:T(8,128)(2,1)}, u32[]{:S(2)}) copy-start(bf16[128,768]{1,0:T(8,128)(2,1)} %param.8) | copy-start | bytes 589828
  15.8 30.4 %all-to-all-start = ((bf16[16,32,896]{2,1,0:T(8,128)(2,1)}), bf16[16,32,896]{2,1,0:T(8,128)(2,1)S(1)}, u32[]{:S(2)}, u32[]{:S(2)}) async-start(bf16[16,32,896]{2,1,0:T(8,128)(2,1)} %pad_maximum_fusion), calls=%async_computation | async-start | bytes 1835008 | tf_op jit(solution)/shard_map/all_to_all | solution.py:167
  46.8 7.8 %slice-start = ((s8[4718592]{0:T(1024)(128)(4,1)}), s8[524288]{0:T(1024)(128)(4,1)S(1)}, s32[]{:S(2)}) async-start(s8[4718592]{0:T(1024)(128)(4,1)} %bitcast.172), calls=%async_computation.3 | async-start | bytes 1048576
  51.3 3.2 %copy-start.3 = (f32[512,3072]{1,0:T(8,128)}, f32[512,3072]{1,0:T(8,128)S(1)}, u32[]{:S(2)}) copy-start(f32[512,3072]{1,0:T(8,128)S(1)} %fusion.13) | copy-start | bytes 18874372
  51.3 4.5 %slice-start.1 = ((s8[4718592]{0:T(1024)(128)(4,1)}), s8[4194304]{0:T(1024)(128)(4,1)S(1)}, s32[]{:S(2)}) async-start(s8[4718592]{0:T(1024)(128)(4,1)} %bitcast.172), calls=%async_computation.4 | async-start | bytes 8388608
  58.3 13.5 %all-to-all-start.1 = ((f32[16,2,768]{2,1,0:T(2,128)}), f32[16,2,768]{2,1,0:T(2,128)S(1)}, u32[]{:S(2)}, u32[]{:S(2)}) async-start(f32[16,2,768]{2,1,0:T(2,128)} %reshape.138), calls=%async_computation.1 | async-start | bytes 196608 | tf_op jit(solution)/shard_map/all_to_all | solution.py:180
  72.0 3.0 %copy-start.2 = (bf16[2048,768]{1,0:T(8,128)(2,1)S(1)}, bf16[2048,768]{1,0:T(8,128)(2,1)}, u32[]{:S(2)}) copy-start(bf16[2048,768]{1,0:T(8,128)(2,1)} %all-gather.3.cloned.1.call-done) | copy-start | bytes 9437188
  76.5 22.3 %slice-start.2 = ((s8[6291456]{0:T(1024)(128)(4,1)}), s8[2097152]{0:T(1024)(128)(4,1)S(1)}, s32[]{:S(2)}) async-start(s8[6291456]{0:T(1024)(128)(4,1)} %bitcast.175), calls=%async_computation.5 | async-start | bytes 4194304
  93.4 5.4 %slice-start.3 = ((s8[6291456]{0:T(1024)(128)(4,1)}), s8[4194304]{0:T(1024)(128)(4,1)S(1)}, s32[]{:S(2)}) async-start(s8[6291456]{0:T(1024)(128)(4,1)} %bitcast.175), calls=%async_computation.6 | async-start | bytes 8388608
  106.8 16.9 %collective-permute-start.6 = (bf16[4,48,1536]{2,1,0:T(8,128)(2,1)S(1)}, bf16[4,48,1536]{2,1,0:T(8,128)(2,1)S(1)}, u32[]{:S(2)}, u32[]{:S(2)}) collective-permute-start(bf16[4,48,1536]{2,1,0:T(8,128)(2,1)S(1)} %dynamic-slice_bitcast_fusion.2), channel_id=1, source_target_pairs={{0,64},{16,80},{32,96},{48,112},{64,128},{80,144},{96,160},{112,17... | collective-permute-start | bytes 1769480 | tf_op jit(solution)/shard_map/ppermute | solution.py:93
  108.5 16.6 %collective-permute-start = (bf16[4,48,1536]{2,1,0:T(8,128)(2,1)S(1)}, bf16[4,48,1536]{2,1,0:T(8,128)(2,1)S(1)}, u32[]{:S(2)}, u32[]{:S(2)}) collective-permute-start(bf16[4,48,1536]{2,1,0:T(8,128)(2,1)S(1)} %dynamic-slice_bitcast_fusion.3), channel_id=1, source_target_pairs={{0,16},{16,32},{32,48},{48,0},{64,80},{80,96},{96,112},{112,64},{1... | collective-permute-start | bytes 1769480 | tf_op jit(solution)/shard_map/ppermute | solution.py:93
  110.9 15.1 %collective-permute-start.18 = (bf16[4,192,384]{2,1,0:T(8,128)(2,1)S(1)}, bf16[4,192,384]{2,1,0:T(8,128)(2,1)S(1)}, u32[]{:S(2)}, u32[]{:S(2)}) collective-permute-start(bf16[4,192,384]{2,1,0:T(8,128)(2,1)S(1)} %dynamic-slice_bitcast_fusion), channel_id=1, source_target_pairs={{0,192},{16,208},{32,224},{48,240},{64,0},{80,16},{96,32},{112,48}... | collective-permute-start | bytes 1769480 | tf_op jit(solution)/shard_map/ppermute | solution.py:94
  112.8 16.6 %collective-permute-start.12 = (bf16[4,192,384]{2,1,0:T(8,128)(2,1)S(1)}, bf16[4,192,384]{2,1,0:T(8,128)(2,1)S(1)}, u32[]{:S(2)}, u32[]{:S(2)}) collective-permute-start(bf16[4,192,384]{2,1,0:T(8,128)(2,1)S(1)} %dynamic-slice_bitcast_fusion.1), channel_id=1, source_target_pairs={{0,48},{16,0},{32,16},{48,32},{64,112},{80,64},{96,80},{112,96},{1... | collective-permute-start | bytes 1769480 | tf_op jit(solution)/shard_map/ppermute | solution.py:94
  123.9 16.1 %collective-permute-start.7 = (bf16[4,48,1536]{2,1,0:T(8,128)(2,1)S(1)}, bf16[4,48,1536]{2,1,0:T(8,128)(2,1)S(1)}, u32[]{:S(2)}, u32[]{:S(2)}) collective-permute-start(bf16[4,48,1536]{2,1,0:T(8,128)(2,1)S(1)} %fusion.29), channel_id=1, source_target_pairs={{0,64},{16,80},{32,96},{48,112},{64,128},{80,144},{96,160},{112,17... | collective-permute-start | bytes 1769480 | tf_op jit(solution)/shard_map/ppermute | solution.py:93
  125.2 15.7 %collective-permute-start.1 = (bf16[4,48,1536]{2,1,0:T(8,128)(2,1)S(1)}, bf16[4,48,1536]{2,1,0:T(8,128)(2,1)S(1)}, u32[]{:S(2)}, u32[]{:S(2)}) collective-permute-start(bf16[4,48,1536]{2,1,0:T(8,128)(2,1)S(1)} %fusion.31), channel_id=1, source_target_pairs={{0,16},{16,32},{32,48},{48,0},{64,80},{80,96},{96,112},{112,64},{1... | collective-permute-start | bytes 1769480 | tf_op jit(solution)/shard_map/ppermute | solution.py:93
  126.2 15.9 %collective-permute-start.19 = (bf16[4,192,384]{2,1,0:T(8,128)(2,1)S(1)}, bf16[4,192,384]{2,1,0:T(8,128)(2,1)S(1)}, u32[]{:S(2)}, u32[]{:S(2)}) collective-permute-start(bf16[4,192,384]{2,1,0:T(8,128)(2,1)S(1)} %fusion.25), channel_id=1, source_target_pairs={{0,192},{16,208},{32,224},{48,240},{64,0},{80,16},{96,32},{112,48}... | collective-permute-start | bytes 1769480 | tf_op jit(solution)/shard_map/ppermute | solution.py:94
  129.5 16.1 %collective-permute-start.13 = (bf16[4,192,384]{2,1,0:T(8,128)(2,1)S(1)}, bf16[4,192,384]{2,1,0:T(8,128)(2,1)S(1)}, u32[]{:S(2)}, u32[]{:S(2)}) collective-permute-start(bf16[4,192,384]{2,1,0:T(8,128)(2,1)S(1)} %fusion.27), channel_id=1, source_target_pairs={{0,48},{16,0},{32,16},{48,32},{64,112},{80,64},{96,80},{112,96},{1... | collective-permute-start | bytes 1769480 | tf_op jit(solution)/shard_map/ppermute | solution.py:94
  140.1 15.2 %collective-permute-start.8 = (bf16[4,48,1536]{2,1,0:T(8,128)(2,1)S(1)}, bf16[4,48,1536]{2,1,0:T(8,128)(2,1)S(1)}, u32[]{:S(2)}, u32[]{:S(2)}) collective-permute-start(bf16[4,48,1536]{2,1,0:T(8,128)(2,1)S(1)} %fusion.28), channel_id=1, source_target_pairs={{0,64},{16,80},{32,96},{48,112},{64,128},{80,144},{96,160},{112,17... | collective-permute-start | bytes 1769480 | tf_op jit(solution)/shard_map/ppermute | solution.py:93
  141.1 16.3 %collective-permute-start.2 = (bf16[4,48,1536]{2,1,0:T(8,128)(2,1)S(1)}, bf16[4,48,1536]{2,1,0:T(8,128)(2,1)S(1)}, u32[]{:S(2)}, u32[]{:S(2)}) collective-permute-start(bf16[4,48,1536]{2,1,0:T(8,128)(2,1)S(1)} %fusion.30), channel_id=1, source_target_pairs={{0,16},{16,32},{32,48},{48,0},{64,80},{80,96},{96,112},{112,64},{1... | collective-permute-start | bytes 1769480 | tf_op jit(solution)/shard_map/ppermute | solution.py:93
  142.3 16.2 %collective-permute-start.20 = (bf16[4,192,384]{2,1,0:T(8,128)(2,1)S(1)}, bf16[4,192,384]{2,1,0:T(8,128)(2,1)S(1)}, u32[]{:S(2)}, u32[]{:S(2)}) collective-permute-start(bf16[4,192,384]{2,1,0:T(8,128)(2,1)S(1)} %fusion.24), channel_id=1, source_target_pairs={{0,192},{16,208},{32,224},{48,240},{64,0},{80,16},{96,32},{112,48}... | collective-permute-start | bytes 1769480 | tf_op jit(solution)/shard_map/ppermute | solution.py:94
  145.7 14.0 %collective-permute-start.14 = (bf16[4,192,384]{2,1,0:T(8,128)(2,1)S(1)}, bf16[4,192,384]{2,1,0:T(8,128)(2,1)S(1)}, u32[]{:S(2)}, u32[]{:S(2)}) collective-permute-start(bf16[4,192,384]{2,1,0:T(8,128)(2,1)S(1)} %fusion.26), channel_id=1, source_target_pairs={{0,48},{16,0},{32,16},{48,32},{64,112},{80,64},{96,80},{112,96},{1... | collective-permute-start | bytes 1769480 | tf_op jit(solution)/shard_map/ppermute | solution.py:94
  155.5 7.3 %collective-permute-start.9 = (bf16[48,1536]{1,0:T(8,128)(2,1)S(1)}, bf16[48,1536]{1,0:T(8,128)(2,1)S(1)}, u32[]{:S(2)}, u32[]{:S(2)}) collective-permute-start(bf16[48,1536]{1,0:T(8,128)(2,1)S(1)} %fusion.54), channel_id=1, source_target_pairs={{0,16},{16,32},{32,48},{48,0},{64,80},{80,96},{96,112},{112,64},{1... | collective-permute-start | bytes 442376 | tf_op jit(solution)/shard_map/ppermute | solution.py:93
  157.6 6.4 %collective-permute-start.3 = (bf16[48,1536]{1,0:T(8,128)(2,1)S(1)}, bf16[48,1536]{1,0:T(8,128)(2,1)S(1)}, u32[]{:S(2)}, u32[]{:S(2)}) collective-permute-start(bf16[48,1536]{1,0:T(8,128)(2,1)S(1)} %fusion.53), channel_id=1, source_target_pairs={{0,64},{16,80},{32,96},{48,112},{64,128},{80,144},{96,160},{112,17... | collective-permute-start | bytes 442376 | tf_op jit(solution)/shard_map/ppermute | solution.py:93
  158.6 5.8 %collective-permute-start.21 = (bf16[192,384]{1,0:T(8,128)(2,1)S(1)}, bf16[192,384]{1,0:T(8,128)(2,1)S(1)}, u32[]{:S(2)}, u32[]{:S(2)}) collective-permute-start(bf16[192,384]{1,0:T(8,128)(2,1)S(1)} %fusion.56), channel_id=1, source_target_pairs={{0,48},{16,0},{32,16},{48,32},{64,112},{80,64},{96,80},{112,96},{1... | collective-permute-start | bytes 442376 | tf_op jit(solution)/shard_map/ppermute | solution.py:94
  159.9 6.6 %collective-permute-start.15 = (bf16[192,384]{1,0:T(8,128)(2,1)S(1)}, bf16[192,384]{1,0:T(8,128)(2,1)S(1)}, u32[]{:S(2)}, u32[]{:S(2)}) collective-permute-start(bf16[192,384]{1,0:T(8,128)(2,1)S(1)} %fusion.55), channel_id=1, source_target_pairs={{0,192},{16,208},{32,224},{48,240},{64,0},{80,16},{96,32},{112,48}... | collective-permute-start | bytes 442376 | tf_op jit(solution)/shard_map/ppermute | solution.py:94
  162.9 6.9 %collective-permute-start.10 = (bf16[48,1536]{1,0:T(8,128)(2,1)S(1)}, bf16[48,1536]{1,0:T(8,128)(2,1)S(1)}, u32[]{:S(2)}, u32[]{:S(2)}) collective-permute-start(bf16[48,1536]{1,0:T(8,128)(2,1)S(1)} %fusion.44), channel_id=1, source_target_pairs={{0,16},{16,32},{32,48},{48,0},{64,80},{80,96},{96,112},{112,64},{1... | collective-permute-start | bytes 442376 | tf_op jit(solution)/shard_map/ppermute | solution.py:93
  164.1 6.9 %collective-permute-start.4 = (bf16[48,1536]{1,0:T(8,128)(2,1)S(1)}, bf16[48,1536]{1,0:T(8,128)(2,1)S(1)}, u32[]{:S(2)}, u32[]{:S(2)}) collective-permute-start(bf16[48,1536]{1,0:T(8,128)(2,1)S(1)} %fusion.46), channel_id=1, source_target_pairs={{0,64},{16,80},{32,96},{48,112},{64,128},{80,144},{96,160},{112,17... | collective-permute-start | bytes 442376 | tf_op jit(solution)/shard_map/ppermute | solution.py:93
  164.5 6.6 %collective-permute-start.22 = (bf16[192,384]{1,0:T(8,128)(2,1)S(1)}, bf16[192,384]{1,0:T(8,128)(2,1)S(1)}, u32[]{:S(2)}, u32[]{:S(2)}) collective-permute-start(bf16[192,384]{1,0:T(8,128)(2,1)S(1)} %fusion.40), channel_id=1, source_target_pairs={{0,48},{16,0},{32,16},{48,32},{64,112},{80,64},{96,80},{112,96},{1... | collective-permute-start | bytes 442376 | tf_op jit(solution)/shard_map/ppermute | solution.py:94
  166.5 6.9 %collective-permute-start.16 = (bf16[192,384]{1,0:T(8,128)(2,1)S(1)}, bf16[192,384]{1,0:T(8,128)(2,1)S(1)}, u32[]{:S(2)}, u32[]{:S(2)}) collective-permute-start(bf16[192,384]{1,0:T(8,128)(2,1)S(1)} %fusion.42), channel_id=1, source_target_pairs={{0,192},{16,208},{32,224},{48,240},{64,0},{80,16},{96,32},{112,48}... | collective-permute-start | bytes 442376 | tf_op jit(solution)/shard_map/ppermute | solution.py:94
  169.8 7.0 %collective-permute-start.11 = (bf16[48,1536]{1,0:T(8,128)(2,1)S(1)}, bf16[48,1536]{1,0:T(8,128)(2,1)S(1)}, u32[]{:S(2)}, u32[]{:S(2)}) collective-permute-start(bf16[48,1536]{1,0:T(8,128)(2,1)S(1)} %fusion.43), channel_id=1, source_target_pairs={{0,16},{16,32},{32,48},{48,0},{64,80},{80,96},{96,112},{112,64},{1... | collective-permute-start | bytes 442376 | tf_op jit(solution)/shard_map/ppermute | solution.py:93
  170.9 9.5 %copy-start.1 = (bf16[768,16]{0,1:T(8,128)(2,1)S(1)}, bf16[768,16]{0,1:T(8,128)(2,1)}, u32[]{:S(2)}) copy-start(bf16[768,16]{0,1:T(8,128)(2,1)} %param.10) | copy-start | bytes 73732
  171.0 6.4 %collective-permute-start.5 = (bf16[48,1536]{1,0:T(8,128)(2,1)S(1)}, bf16[48,1536]{1,0:T(8,128)(2,1)S(1)}, u32[]{:S(2)}, u32[]{:S(2)}) collective-permute-start(bf16[48,1536]{1,0:T(8,128)(2,1)S(1)} %fusion.45), channel_id=1, source_target_pairs={{0,64},{16,80},{32,96},{48,112},{64,128},{80,144},{96,160},{112,17... | collective-permute-start | bytes 442376 | tf_op jit(solution)/shard_map/ppermute | solution.py:93
  171.1 7.2 %collective-permute-start.23 = (bf16[192,384]{1,0:T(8,128)(2,1)S(1)}, bf16[192,384]{1,0:T(8,128)(2,1)S(1)}, u32[]{:S(2)}, u32[]{:S(2)}) collective-permute-start(bf16[192,384]{1,0:T(8,128)(2,1)S(1)} %fusion.39), channel_id=1, source_target_pairs={{0,48},{16,0},{32,16},{48,32},{64,112},{80,64},{96,80},{112,96},{1... | collective-permute-start | bytes 442376 | tf_op jit(solution)/shard_map/ppermute | solution.py:94
  173.4 6.0 %collective-permute-start.17 = (bf16[192,384]{1,0:T(8,128)(2,1)S(1)}, bf16[192,384]{1,0:T(8,128)(2,1)S(1)}, u32[]{:S(2)}, u32[]{:S(2)}) collective-permute-start(bf16[192,384]{1,0:T(8,128)(2,1)S(1)} %fusion.41), channel_id=1, source_target_pairs={{0,192},{16,208},{32,224},{48,240},{64,0},{80,16},{96,32},{112,48}... | collective-permute-start | bytes 442376 | tf_op jit(solution)/shard_map/ppermute | solution.py:94
Sparse Core Ops, SparseCore 0:
  10.4 55.4 all-gather.2

commit v5 on v2

--- a/solution.py
+++ b/solution.py
@@ -208,7 +208,10 @@
         delta_unit - unit_vec * jnp.sum(unit_vec * delta_unit, axis=1, keepdims=True)
     )
     delta_seq = (delta_pooled / LEN).astype(jnp.bfloat16)
-    delta_row = lax.all_gather(delta_seq, "expert", axis=0, tiled=True)
+    delta_row = lax.all_to_all(
+        jnp.broadcast_to(delta_seq[None], (expert_size,) + delta_seq.shape), "expert",
+        split_axis=0, concat_axis=0, tiled=True,
+    ).reshape(row_seqs, model_width)
 
     dims_t = (((0,), (0,)), ((), ()))
     spread_t = lax.optimization_barrier(lax.dot_general(

time: 190 us -> 186 us (0.979)
  blocking collectives: 16.1 us -> 0 us
  waiting for transfers between devices: 58.8 us -> 64.7 us
  starting transfers between devices: 53.2 us -> 58.5 us
    all_gather x1 -> x0, blocking collectives: 16.1 us -> none  [on_device(): delta_row = lax.all_gather(delta_seq, 'expert', axis=0, tiled=True)]
    all_to_all x0 -> x1, waiting for transfers between devices: none -> 6.39 us  [on_device(): lax.all_to_all(jnp.broadcast_to(delta_seq[None], (expert_size,) + delta_s...]
    all_to_all x0 -> x1, starting transfers between devices: none -> 4.97 us  [on_device(): lax.all_to_all(jnp.broadcast_to(delta_seq[None], (expert_size,) + delta_s...]
  transfers between devices with their start and end apart: 27 -> 28, of which waited for: 13 -> 14; matrix products, arithmetic and copies ran while one was open for 12% -> 13% of each run, Pallas kernels for 0% -> 0%
where the time goes in v5:
time: 186 us; the launch traced here: 183 us
  waiting for transfers between devices  64.7 us (35%)
  starting transfers between devices  58.5 us (31%)
  matrix products  26.3 us (14%)
  between operations  14.5 us (8%)
  other arithmetic  10.9 us (6%)
  local copies, waits for them, and re-layouts  8.12 us (4%)
    ppermute x12, starting transfers between devices, ring_step(): got_b = lax.ppermute(state['acc_b'].astype(jnp.bfloat16), 'dp', bwd_pairs)  29.1 us
    ppermute x12, waiting for transfers between devices, ring_step(): got_f = lax.ppermute(state['acc_f'].astype(jnp.bfloat16), 'dp', fwd_pairs)  28.2 us
    all_to_all x1, waiting for transfers between devices, on_device(): lax.all_to_all(outgoing, 'expert', split_axis=0, concat_axis=0, tiled=True)  20.8 us
    ppermute x12, starting transfers between devices, ring_step(): got_f = lax.ppermute(state['acc_f'].astype(jnp.bfloat16), 'dp', fwd_pairs)  9.02 us
    all_to_all x1, starting transfers between devices, on_device(): lax.all_to_all(outgoing, 'expert', split_axis=0, concat_axis=0, tiled=True)  8.59 us
    all_to_all x1, starting transfers between devices, on_device(): lax.all_to_all(moe_seq.reshape(expert_size, seq_count, model_width), 'exp...  6.8 us
    all_to_all x1, waiting for transfers between devices, on_device(): lax.all_to_all(moe_seq.reshape(expert_size, seq_count, model_width), 'exp...  6.67 us
    all_to_all x1, waiting for transfers between devices, on_device(): lax.all_to_all(jnp.broadcast_to(delta_seq[None], (expert_size,) + delta_s...  6.39 us
  transfers between devices with their start and end apart: 28, of which 14 were waited for; matrix products, arithmetic and copies ran while one was open for 13% of the time, Pallas kernels for 0%

profile of v5, /device:TPU:32, one launch (start us, length us, event | category | flops | bytes accessed | tf_op | source)
XLA Modules:
  0.0 183.1 jit_solution(11524116657088816075)
XLA Ops:
  7.9 0.8 copy.54
  10.8 1.0 fusion.81
  11.9 0.8 select_reduce_fusion.1
  13.1 1.4 fusion.49
  14.8 1.0 pad_maximum_fusion
  15.9 8.6 %all-to-all-start = ((bf16[16,32,896]{2,1,0:T(8,128)(2,1)}), bf16[16,32,896]{2,1,0:T(8,128)(2,1)S(1)}, u32[]{:S(2)}, u32[]{:S(2)}) async-start(bf16[16,32,896]{2,1,0:T(8,128)(2,1)} %pad_maximum_fusion), calls=%async_computation | async-start | bytes 1835008 | tf_op jit(solution)/shard_map/all_to_all | solution.py:168
  25.5 20.8 %all-to-all-done = bf16[16,32,896]{2,1,0:T(8,128)(2,1)S(1)} async-done(((bf16[16,32,896]{2,1,0:T(8,128)(2,1)}), bf16[16,32,896]{2,1,0:T(8,128)(2,1)S(1)}, u32[]{:S(2)}, u32[]{:S(2)}) %all-to-all-start) | async-done | bytes 917536 | tf_op jit(solution)/shard_map/all_to_all | solution.py:168
  46.8 4.5 %fusion.13 = f32[512,3072]{1,0:T(8,128)S(1)} fusion(bf16[512,768]{1,0:T(8,128)(2,1)S(1)} %bitcast.176, bf16[1,768,3072]{2,1,0:T(8,128)(2,1)} %param.11), kind=kOutput, calls=%fused_computation.19 | convolution fusion | flops 2415919104 | bytes 11796480 | tf_op jit(solution)/shard_map/dot_general | solution.py:176
  51.4 2.5 %fusion.21 = f32[32,3072]{1,0:T(8,128)S(1)} fusion(bf16[32,512]{1,0:T(8,128)(2,1)S(1)} %convert_element_type.307, f32[512,3072]{1,0:T(8,128)S(1)} %fusion.13), kind=kOutput, calls=%fused_computation.23 | convolution fusion | flops 114819072 | bytes 6717440 | tf_op jit(solution)/shard_map/dot_general | solution.py:179
  54.6 1.3 slice-done.1
  55.9 0.9 fusion.9
  56.8 0.9 fusion.32
  58.3 6.8 %all-to-all-start.1 = ((f32[16,2,768]{2,1,0:T(2,128)}), f32[16,2,768]{2,1,0:T(2,128)S(1)}, u32[]{:S(2)}, u32[]{:S(2)}) async-start(f32[16,2,768]{2,1,0:T(2,128)} %reshape.142), calls=%async_computation.1 | async-start | bytes 196608 | tf_op jit(solution)/shard_map/all_to_all | solution.py:181
  65.2 6.7 %all-to-all-done.1 = f32[16,2,768]{2,1,0:T(2,128)S(1)} async-done(((f32[16,2,768]{2,1,0:T(2,128)}), f32[16,2,768]{2,1,0:T(2,128)S(1)}, u32[]{:S(2)}, u32[]{:S(2)}) %all-to-all-start.1) | async-done | bytes 98336 | tf_op jit(solution)/shard_map/all_to_all | solution.py:181
  72.1 2.7 %multiply_reduce_fusion = f32[2048]{0:T(1024)S(1)} fusion(bf16[2048,768]{1,0:T(8,128)(2,1)} %all-gather.2.cloned.1.call-done), kind=kLoop, calls=%fused_computation.9 | loop fusion | flops 4716544 | bytes 3153920 | tf_op jit(solution)/shard_map/reduce_sum | solution.py:194
  75.0 1.0 fusion.80
  78.0 5.0 %all-to-all-start.2 = ((bf16[16,2,768]{2,1,0:T(2,128)(2,1)}), bf16[16,2,768]{2,1,0:T(2,128)(2,1)S(1)}, u32[]{:S(2)}, u32[]{:S(2)}) async-start(bf16[16,2,768]{2,1,0:T(2,128)(2,1)} %broadcast_in_dim.50), calls=%async_computation.2 | async-start | bytes 98304 | tf_op jit(solution)/shard_map/all_to_all | solution.py:211
  83.0 6.4 %all-to-all-done.2 = bf16[16,2,768]{2,1,0:T(2,128)(2,1)S(1)} async-done(((bf16[16,2,768]{2,1,0:T(2,128)(2,1)}), bf16[16,2,768]{2,1,0:T(2,128)(2,1)S(1)}, u32[]{:S(2)}, u32[]{:S(2)}) %all-to-all-start.2) | async-done | bytes 49184 | tf_op jit(solution)/shard_map/all_to_all | solution.py:211
  89.4 3.9 %fusion.18 = bf16[3072,32]{0,1:T(8,128)(2,1)S(1)} fusion(bf16[32,768]{1,0:T(8,128)(2,1)S(1)} %reshape.143, bf16[1,3072,768]{2,1,0:T(8,128)(2,1)} %param.12), kind=kOutput, calls=%fused_computation.22 | convolution fusion | flops 151093248 | bytes 4964352 | tf_op jit(solution)/shard_map/dot_general | solution.py:217
  93.4 1.5 convolution_convert_fusion
  94.8 4.3 %fusion.6 = bf16[512,3072]{1,0:T(8,128)(2,1)S(1)} fusion(f32[512,3072]{1,0:T(8,128)S(1)} %bitcast.174, bf16[32,512]{1,0:T(8,128)(2,1)S(1)} %convert_element_type.307, bf16[3072,32]{0,1:T(8,128)(2,1)S(1)} %fusion.18), kind=kOutput, calls=%fused_computation.8 | convolution fusion | flops 130547712 | bytes 9666560 | tf_op jit(solution)/shard_map/dot_general | solution.py:220
  99.2 2.9 %convolution_convert_fusion.1 = bf16[768,3072]{1,0:T(8,128)(2,1)S(1)} fusion(bf16[512,768]{1,0:T(8,128)(2,1)S(1)} %bitcast.177, bf16[512,3072]{1,0:T(8,128)(2,1)S(1)} %fusion.6), kind=kOutput, calls=%fused_computation.12 | convolution fusion | flops 2418278400 | bytes 8650752 | tf_op jit(solution)/shard_map/dot_general | solution.py:225
  102.8 1.6 collective-permute-start.6
  104.4 1.6 collective-permute-start
  106.0 0.8 fusion.78
  106.9 1.7 collective-permute-start.18
  108.7 1.9 %collective-permute-start.12 = (bf16[4,192,384]{2,1,0:T(8,128)(2,1)S(1)}, bf16[4,192,384]{2,1,0:T(8,128)(2,1)S(1)}, u32[]{:S(2)}, u32[]{:S(2)}) collective-permute-start(bf16[4,192,384]{2,1,0:T(8,128)(2,1)S(1)} %dynamic-slice_bitcast_fusion.1), channel_id=1, source_target_pairs={{0,48},{16,0},{32,16},{48,32},{64,112},{80,64},{96,80},{112,96},{1... | collective-permute-start | bytes 1769480 | tf_op jit(solution)/shard_map/ppermute | solution.py:94
  110.6 9.0 %collective-permute-done.6 = bf16[4,48,1536]{2,1,0:T(8,128)(2,1)S(1)} collective-permute-done((bf16[4,48,1536]{2,1,0:T(8,128)(2,1)S(1)}, bf16[4,48,1536]{2,1,0:T(8,128)(2,1)S(1)}, u32[]{:S(2)}, u32[]{:S(2)}) %collective-permute-start.6) | collective-permute-done | bytes 589856 | tf_op jit(solution)/shard_map/ppermute | solution.py:93
  120.0 0.8 collective-permute-done
  122.0 3.2 %collective-permute-start.19 = (bf16[4,192,384]{2,1,0:T(8,128)(2,1)S(1)}, bf16[4,192,384]{2,1,0:T(8,128)(2,1)S(1)}, u32[]{:S(2)}, u32[]{:S(2)}) collective-permute-start(bf16[4,192,384]{2,1,0:T(8,128)(2,1)S(1)} %fusion.25), channel_id=1, source_target_pairs={{0,192},{16,208},{32,224},{48,240},{64,0},{80,16},{96,32},{112,48}... | collective-permute-start | bytes 1769480 | tf_op jit(solution)/shard_map/ppermute | solution.py:94
  125.3 2.0 %collective-permute-start.13 = (bf16[4,192,384]{2,1,0:T(8,128)(2,1)S(1)}, bf16[4,192,384]{2,1,0:T(8,128)(2,1)S(1)}, u32[]{:S(2)}, u32[]{:S(2)}) collective-permute-start(bf16[4,192,384]{2,1,0:T(8,128)(2,1)S(1)} %fusion.27), channel_id=1, source_target_pairs={{0,48},{16,0},{32,16},{48,32},{64,112},{80,64},{96,80},{112,96},{1... | collective-permute-start | bytes 1769480 | tf_op jit(solution)/shard_map/ppermute | solution.py:94
  127.3 8.4 %collective-permute-done.7 = bf16[4,48,1536]{2,1,0:T(8,128)(2,1)S(1)} collective-permute-done((bf16[4,48,1536]{2,1,0:T(8,128)(2,1)S(1)}, bf16[4,48,1536]{2,1,0:T(8,128)(2,1)S(1)}, u32[]{:S(2)}, u32[]{:S(2)}) %collective-permute-start.7) | collective-permute-done | bytes 589856 | tf_op jit(solution)/shard_map/ppermute | solution.py:93
  136.7 1.1 collective-permute-start.2
  137.9 3.3 %collective-permute-start.20 = (bf16[4,192,384]{2,1,0:T(8,128)(2,1)S(1)}, bf16[4,192,384]{2,1,0:T(8,128)(2,1)S(1)}, u32[]{:S(2)}, u32[]{:S(2)}) collective-permute-start(bf16[4,192,384]{2,1,0:T(8,128)(2,1)S(1)} %fusion.24), channel_id=1, source_target_pairs={{0,192},{16,208},{32,224},{48,240},{64,0},{80,16},{96,32},{112,48}... | collective-permute-start | bytes 1769480 | tf_op jit(solution)/shard_map/ppermute | solution.py:94
  141.4 1.7 collective-permute-start.14
  143.1 7.8 %collective-permute-done.8 = bf16[4,48,1536]{2,1,0:T(8,128)(2,1)S(1)} collective-permute-done((bf16[4,48,1536]{2,1,0:T(8,128)(2,1)S(1)}, bf16[4,48,1536]{2,1,0:T(8,128)(2,1)S(1)}, u32[]{:S(2)}, u32[]{:S(2)}) %collective-permute-start.8) | collective-permute-done | bytes 589856 | tf_op jit(solution)/shard_map/ppermute | solution.py:93
  151.1 1.8 collective-permute-start.9
  153.1 0.8 collective-permute-start.3
  154.1 0.9 collective-permute-start.21
  155.6 2.9 %collective-permute-start.15 = (bf16[192,384]{1,0:T(8,128)(2,1)S(1)}, bf16[192,384]{1,0:T(8,128)(2,1)S(1)}, u32[]{:S(2)}, u32[]{:S(2)}) collective-permute-start(bf16[192,384]{1,0:T(8,128)(2,1)S(1)} %fusion.55), channel_id=1, source_target_pairs={{0,192},{16,208},{32,224},{48,240},{64,0},{80,16},{96,32},{112,48}... | collective-permute-start | bytes 442376 | tf_op jit(solution)/shard_map/ppermute | solution.py:94
  159.7 2.4 %collective-permute-start.22 = (bf16[192,384]{1,0:T(8,128)(2,1)S(1)}, bf16[192,384]{1,0:T(8,128)(2,1)S(1)}, u32[]{:S(2)}, u32[]{:S(2)}) collective-permute-start(bf16[192,384]{1,0:T(8,128)(2,1)S(1)} %fusion.40), channel_id=1, source_target_pairs={{0,48},{16,0},{32,16},{48,32},{64,112},{80,64},{96,80},{112,96},{1... | collective-permute-start | bytes 442376 | tf_op jit(solution)/shard_map/ppermute | solution.py:94
  162.1 3.3 %collective-permute-start.16 = (bf16[192,384]{1,0:T(8,128)(2,1)S(1)}, bf16[192,384]{1,0:T(8,128)(2,1)S(1)}, u32[]{:S(2)}, u32[]{:S(2)}) collective-permute-start(bf16[192,384]{1,0:T(8,128)(2,1)S(1)} %fusion.42), channel_id=1, source_target_pairs={{0,192},{16,208},{32,224},{48,240},{64,0},{80,16},{96,32},{112,48}... | collective-permute-start | bytes 442376 | tf_op jit(solution)/shard_map/ppermute | solution.py:94
  165.7 0.8 collective-permute-done.4
  166.7 2.2 %collective-permute-start.23 = (bf16[192,384]{1,0:T(8,128)(2,1)S(1)}, bf16[192,384]{1,0:T(8,128)(2,1)S(1)}, u32[]{:S(2)}, u32[]{:S(2)}) collective-permute-start(bf16[192,384]{1,0:T(8,128)(2,1)S(1)} %fusion.39), channel_id=1, source_target_pairs={{0,48},{16,0},{32,16},{48,32},{64,112},{80,64},{96,80},{112,96},{1... | collective-permute-start | bytes 442376 | tf_op jit(solution)/shard_map/ppermute | solution.py:94
  169.0 3.6 %collective-permute-start.17 = (bf16[192,384]{1,0:T(8,128)(2,1)S(1)}, bf16[192,384]{1,0:T(8,128)(2,1)S(1)}, u32[]{:S(2)}, u32[]{:S(2)}) collective-permute-start(bf16[192,384]{1,0:T(8,128)(2,1)S(1)} %fusion.41), channel_id=1, source_target_pairs={{0,192},{16,208},{32,224},{48,240},{64,0},{80,16},{96,32},{112,48}... | collective-permute-start | bytes 442376 | tf_op jit(solution)/shard_map/ppermute | solution.py:94
  173.1 0.9 maximum_bitcast_fusion
  174.0 1.4 collective-permute-done.17
  175.4 0.9 maximum_bitcast_fusion.1
  (123 shorter events, 16.2 us)
Async XLA Ops:
  7.2 3.7 %copy-start = (bf16[768,16]{0,1:T(8,128)(2,1)S(1)}, bf16[768,16]{0,1:T(8,128)(2,1)}, u32[]{:S(2)}) copy-start(bf16[768,16]{0,1:T(8,128)(2,1)} %param.10) | copy-start | bytes 73732
  7.2 64.9 %all-gather.2.cloned.1.call-start = ((), (), s32[]{:S(2)}) async-start(), calls=%async_computation.3 | async-start | bytes 3342336 | tf_op jit(solution)/shard_map/all_gather | solution.py:193
  13.1 12.1 %copy-start.5 = (s32[256,16]{0,1:T(8,128)S(1)}, s32[256,16]{0,1:T(8,128)}, u32[]{:S(2)}) copy-start(s32[256,16]{0,1:T(8,128)} %param.15) | copy-start | bytes 49156
  13.1 12.3 %copy-start.4 = (bf16[128,768]{1,0:T(8,128)(2,1)S(1)}, bf16[128,768]{1,0:T(8,128)(2,1)}, u32[]{:S(2)}) copy-start(bf16[128,768]{1,0:T(8,128)(2,1)} %param.8) | copy-start | bytes 589828
  15.9 30.4 %all-to-all-start = ((bf16[16,32,896]{2,1,0:T(8,128)(2,1)}), bf16[16,32,896]{2,1,0:T(8,128)(2,1)S(1)}, u32[]{:S(2)}, u32[]{:S(2)}) async-start(bf16[16,32,896]{2,1,0:T(8,128)(2,1)} %pad_maximum_fusion), calls=%async_computation | async-start | bytes 1835008 | tf_op jit(solution)/shard_map/all_to_all | solution.py:168
  46.8 7.8 %slice-start = ((s8[4718592]{0:T(1024)(128)(4,1)}), s8[524288]{0:T(1024)(128)(4,1)S(1)}, s32[]{:S(2)}) async-start(s8[4718592]{0:T(1024)(128)(4,1)} %bitcast.170), calls=%async_computation.4 | async-start | bytes 1048576
  51.4 3.2 %copy-start.3 = (f32[512,3072]{1,0:T(8,128)}, f32[512,3072]{1,0:T(8,128)S(1)}, u32[]{:S(2)}) copy-start(f32[512,3072]{1,0:T(8,128)S(1)} %fusion.13) | copy-start | bytes 18874372
  51.4 4.5 %slice-start.1 = ((s8[4718592]{0:T(1024)(128)(4,1)}), s8[4194304]{0:T(1024)(128)(4,1)S(1)}, s32[]{:S(2)}) async-start(s8[4718592]{0:T(1024)(128)(4,1)} %bitcast.170), calls=%async_computation.5 | async-start | bytes 8388608
  58.3 13.5 %all-to-all-start.1 = ((f32[16,2,768]{2,1,0:T(2,128)}), f32[16,2,768]{2,1,0:T(2,128)S(1)}, u32[]{:S(2)}, u32[]{:S(2)}) async-start(f32[16,2,768]{2,1,0:T(2,128)} %reshape.142), calls=%async_computation.1 | async-start | bytes 196608 | tf_op jit(solution)/shard_map/all_to_all | solution.py:181
  72.1 3.0 %copy-start.2 = (bf16[2048,768]{1,0:T(8,128)(2,1)S(1)}, bf16[2048,768]{1,0:T(8,128)(2,1)}, u32[]{:S(2)}) copy-start(bf16[2048,768]{1,0:T(8,128)(2,1)} %all-gather.2.cloned.1.call-done) | copy-start | bytes 9437188
  76.6 18.2 %slice-start.2 = ((s8[6291456]{0:T(1024)(128)(4,1)}), s8[2097152]{0:T(1024)(128)(4,1)S(1)}, s32[]{:S(2)}) async-start(s8[6291456]{0:T(1024)(128)(4,1)} %bitcast.173), calls=%async_computation.6 | async-start | bytes 4194304
  78.0 11.4 %all-to-all-start.2 = ((bf16[16,2,768]{2,1,0:T(2,128)(2,1)}), bf16[16,2,768]{2,1,0:T(2,128)(2,1)S(1)}, u32[]{:S(2)}, u32[]{:S(2)}) async-start(bf16[16,2,768]{2,1,0:T(2,128)(2,1)} %broadcast_in_dim.50), calls=%async_computation.2 | async-start | bytes 98304 | tf_op jit(solution)/shard_map/all_to_all | solution.py:211
  89.4 5.4 %slice-start.3 = ((s8[6291456]{0:T(1024)(128)(4,1)}), s8[4194304]{0:T(1024)(128)(4,1)S(1)}, s32[]{:S(2)}) async-start(s8[6291456]{0:T(1024)(128)(4,1)} %bitcast.173), calls=%async_computation.7 | async-start | bytes 8388608
  102.8 16.8 %collective-permute-start.6 = (bf16[4,48,1536]{2,1,0:T(8,128)(2,1)S(1)}, bf16[4,48,1536]{2,1,0:T(8,128)(2,1)S(1)}, u32[]{:S(2)}, u32[]{:S(2)}) collective-permute-start(bf16[4,48,1536]{2,1,0:T(8,128)(2,1)S(1)} %dynamic-slice_bitcast_fusion.2), channel_id=1, source_target_pairs={{0,64},{16,80},{32,96},{48,112},{64,128},{80,144},{96,160},{112,17... | collective-permute-start | bytes 1769480 | tf_op jit(solution)/shard_map/ppermute | solution.py:93
  104.4 16.4 %collective-permute-start = (bf16[4,48,1536]{2,1,0:T(8,128)(2,1)S(1)}, bf16[4,48,1536]{2,1,0:T(8,128)(2,1)S(1)}, u32[]{:S(2)}, u32[]{:S(2)}) collective-permute-start(bf16[4,48,1536]{2,1,0:T(8,128)(2,1)S(1)} %dynamic-slice_bitcast_fusion.3), channel_id=1, source_target_pairs={{0,16},{16,32},{32,48},{48,0},{64,80},{80,96},{96,112},{112,64},{1... | collective-permute-start | bytes 1769480 | tf_op jit(solution)/shard_map/ppermute | solution.py:93
  106.9 14.9 %collective-permute-start.18 = (bf16[4,192,384]{2,1,0:T(8,128)(2,1)S(1)}, bf16[4,192,384]{2,1,0:T(8,128)(2,1)S(1)}, u32[]{:S(2)}, u32[]{:S(2)}) collective-permute-start(bf16[4,192,384]{2,1,0:T(8,128)(2,1)S(1)} %dynamic-slice_bitcast_fusion), channel_id=1, source_target_pairs={{0,192},{16,208},{32,224},{48,240},{64,0},{80,16},{96,32},{112,48}... | collective-permute-start | bytes 1769480 | tf_op jit(solution)/shard_map/ppermute | solution.py:94
  108.7 16.4 %collective-permute-start.12 = (bf16[4,192,384]{2,1,0:T(8,128)(2,1)S(1)}, bf16[4,192,384]{2,1,0:T(8,128)(2,1)S(1)}, u32[]{:S(2)}, u32[]{:S(2)}) collective-permute-start(bf16[4,192,384]{2,1,0:T(8,128)(2,1)S(1)} %dynamic-slice_bitcast_fusion.1), channel_id=1, source_target_pairs={{0,48},{16,0},{32,16},{48,32},{64,112},{80,64},{96,80},{112,96},{1... | collective-permute-start | bytes 1769480 | tf_op jit(solution)/shard_map/ppermute | solution.py:94
  119.7 15.9 %collective-permute-start.7 = (bf16[4,48,1536]{2,1,0:T(8,128)(2,1)S(1)}, bf16[4,48,1536]{2,1,0:T(8,128)(2,1)S(1)}, u32[]{:S(2)}, u32[]{:S(2)}) collective-permute-start(bf16[4,48,1536]{2,1,0:T(8,128)(2,1)S(1)} %fusion.29), channel_id=1, source_target_pairs={{0,64},{16,80},{32,96},{48,112},{64,128},{80,144},{96,160},{112,17... | collective-permute-start | bytes 1769480 | tf_op jit(solution)/shard_map/ppermute | solution.py:93
  121.0 15.5 %collective-permute-start.1 = (bf16[4,48,1536]{2,1,0:T(8,128)(2,1)S(1)}, bf16[4,48,1536]{2,1,0:T(8,128)(2,1)S(1)}, u32[]{:S(2)}, u32[]{:S(2)}) collective-permute-start(bf16[4,48,1536]{2,1,0:T(8,128)(2,1)S(1)} %fusion.31), channel_id=1, source_target_pairs={{0,16},{16,32},{32,48},{48,0},{64,80},{80,96},{96,112},{112,64},{1... | collective-permute-start | bytes 1769480 | tf_op jit(solution)/shard_map/ppermute | solution.py:93
  122.0 15.8 %collective-permute-start.19 = (bf16[4,192,384]{2,1,0:T(8,128)(2,1)S(1)}, bf16[4,192,384]{2,1,0:T(8,128)(2,1)S(1)}, u32[]{:S(2)}, u32[]{:S(2)}) collective-permute-start(bf16[4,192,384]{2,1,0:T(8,128)(2,1)S(1)} %fusion.25), channel_id=1, source_target_pairs={{0,192},{16,208},{32,224},{48,240},{64,0},{80,16},{96,32},{112,48}... | collective-permute-start | bytes 1769480 | tf_op jit(solution)/shard_map/ppermute | solution.py:94
  125.3 15.9 %collective-permute-start.13 = (bf16[4,192,384]{2,1,0:T(8,128)(2,1)S(1)}, bf16[4,192,384]{2,1,0:T(8,128)(2,1)S(1)}, u32[]{:S(2)}, u32[]{:S(2)}) collective-permute-start(bf16[4,192,384]{2,1,0:T(8,128)(2,1)S(1)} %fusion.27), channel_id=1, source_target_pairs={{0,48},{16,0},{32,16},{48,32},{64,112},{80,64},{96,80},{112,96},{1... | collective-permute-start | bytes 1769480 | tf_op jit(solution)/shard_map/ppermute | solution.py:94
  135.8 15.1 %collective-permute-start.8 = (bf16[4,48,1536]{2,1,0:T(8,128)(2,1)S(1)}, bf16[4,48,1536]{2,1,0:T(8,128)(2,1)S(1)}, u32[]{:S(2)}, u32[]{:S(2)}) collective-permute-start(bf16[4,48,1536]{2,1,0:T(8,128)(2,1)S(1)} %fusion.28), channel_id=1, source_target_pairs={{0,64},{16,80},{32,96},{48,112},{64,128},{80,144},{96,160},{112,17... | collective-permute-start | bytes 1769480 | tf_op jit(solution)/shard_map/ppermute | solution.py:93
  136.7 16.2 %collective-permute-start.2 = (bf16[4,48,1536]{2,1,0:T(8,128)(2,1)S(1)}, bf16[4,48,1536]{2,1,0:T(8,128)(2,1)S(1)}, u32[]{:S(2)}, u32[]{:S(2)}) collective-permute-start(bf16[4,48,1536]{2,1,0:T(8,128)(2,1)S(1)} %fusion.30), channel_id=1, source_target_pairs={{0,16},{16,32},{32,48},{48,0},{64,80},{80,96},{96,112},{112,64},{1... | collective-permute-start | bytes 1769480 | tf_op jit(solution)/shard_map/ppermute | solution.py:93
  137.9 16.0 %collective-permute-start.20 = (bf16[4,192,384]{2,1,0:T(8,128)(2,1)S(1)}, bf16[4,192,384]{2,1,0:T(8,128)(2,1)S(1)}, u32[]{:S(2)}, u32[]{:S(2)}) collective-permute-start(bf16[4,192,384]{2,1,0:T(8,128)(2,1)S(1)} %fusion.24), channel_id=1, source_target_pairs={{0,192},{16,208},{32,224},{48,240},{64,0},{80,16},{96,32},{112,48}... | collective-permute-start | bytes 1769480 | tf_op jit(solution)/shard_map/ppermute | solution.py:94
  141.4 14.0 %collective-permute-start.14 = (bf16[4,192,384]{2,1,0:T(8,128)(2,1)S(1)}, bf16[4,192,384]{2,1,0:T(8,128)(2,1)S(1)}, u32[]{:S(2)}, u32[]{:S(2)}) collective-permute-start(bf16[4,192,384]{2,1,0:T(8,128)(2,1)S(1)} %fusion.26), channel_id=1, source_target_pairs={{0,48},{16,0},{32,16},{48,32},{64,112},{80,64},{96,80},{112,96},{1... | collective-permute-start | bytes 1769480 | tf_op jit(solution)/shard_map/ppermute | solution.py:94
  151.1 7.3 %collective-permute-start.9 = (bf16[48,1536]{1,0:T(8,128)(2,1)S(1)}, bf16[48,1536]{1,0:T(8,128)(2,1)S(1)}, u32[]{:S(2)}, u32[]{:S(2)}) collective-permute-start(bf16[48,1536]{1,0:T(8,128)(2,1)S(1)} %fusion.54), channel_id=1, source_target_pairs={{0,16},{16,32},{32,48},{48,0},{64,80},{80,96},{96,112},{112,64},{1... | collective-permute-start | bytes 442376 | tf_op jit(solution)/shard_map/ppermute | solution.py:93
  153.1 6.4 %collective-permute-start.3 = (bf16[48,1536]{1,0:T(8,128)(2,1)S(1)}, bf16[48,1536]{1,0:T(8,128)(2,1)S(1)}, u32[]{:S(2)}, u32[]{:S(2)}) collective-permute-start(bf16[48,1536]{1,0:T(8,128)(2,1)S(1)} %fusion.53), channel_id=1, source_target_pairs={{0,64},{16,80},{32,96},{48,112},{64,128},{80,144},{96,160},{112,17... | collective-permute-start | bytes 442376 | tf_op jit(solution)/shard_map/ppermute | solution.py:93
  154.1 5.6 %collective-permute-start.21 = (bf16[192,384]{1,0:T(8,128)(2,1)S(1)}, bf16[192,384]{1,0:T(8,128)(2,1)S(1)}, u32[]{:S(2)}, u32[]{:S(2)}) collective-permute-start(bf16[192,384]{1,0:T(8,128)(2,1)S(1)} %fusion.56), channel_id=1, source_target_pairs={{0,48},{16,0},{32,16},{48,32},{64,112},{80,64},{96,80},{112,96},{1... | collective-permute-start | bytes 442376 | tf_op jit(solution)/shard_map/ppermute | solution.py:94
  155.6 6.5 %collective-permute-start.15 = (bf16[192,384]{1,0:T(8,128)(2,1)S(1)}, bf16[192,384]{1,0:T(8,128)(2,1)S(1)}, u32[]{:S(2)}, u32[]{:S(2)}) collective-permute-start(bf16[192,384]{1,0:T(8,128)(2,1)S(1)} %fusion.55), channel_id=1, source_target_pairs={{0,192},{16,208},{32,224},{48,240},{64,0},{80,16},{96,32},{112,48}... | collective-permute-start | bytes 442376 | tf_op jit(solution)/shard_map/ppermute | solution.py:94
  158.5 6.9 %collective-permute-start.10 = (bf16[48,1536]{1,0:T(8,128)(2,1)S(1)}, bf16[48,1536]{1,0:T(8,128)(2,1)S(1)}, u32[]{:S(2)}, u32[]{:S(2)}) collective-permute-start(bf16[48,1536]{1,0:T(8,128)(2,1)S(1)} %fusion.44), channel_id=1, source_target_pairs={{0,16},{16,32},{32,48},{48,0},{64,80},{80,96},{96,112},{112,64},{1... | collective-permute-start | bytes 442376 | tf_op jit(solution)/shard_map/ppermute | solution.py:93
  159.5 7.0 %collective-permute-start.4 = (bf16[48,1536]{1,0:T(8,128)(2,1)S(1)}, bf16[48,1536]{1,0:T(8,128)(2,1)S(1)}, u32[]{:S(2)}, u32[]{:S(2)}) collective-permute-start(bf16[48,1536]{1,0:T(8,128)(2,1)S(1)} %fusion.46), channel_id=1, source_target_pairs={{0,64},{16,80},{32,96},{48,112},{64,128},{80,144},{96,160},{112,17... | collective-permute-start | bytes 442376 | tf_op jit(solution)/shard_map/ppermute | solution.py:93
  159.7 7.0 %collective-permute-start.22 = (bf16[192,384]{1,0:T(8,128)(2,1)S(1)}, bf16[192,384]{1,0:T(8,128)(2,1)S(1)}, u32[]{:S(2)}, u32[]{:S(2)}) collective-permute-start(bf16[192,384]{1,0:T(8,128)(2,1)S(1)} %fusion.40), channel_id=1, source_target_pairs={{0,48},{16,0},{32,16},{48,32},{64,112},{80,64},{96,80},{112,96},{1... | collective-permute-start | bytes 442376 | tf_op jit(solution)/shard_map/ppermute | solution.py:94
  162.1 6.9 %collective-permute-start.16 = (bf16[192,384]{1,0:T(8,128)(2,1)S(1)}, bf16[192,384]{1,0:T(8,128)(2,1)S(1)}, u32[]{:S(2)}, u32[]{:S(2)}) collective-permute-start(bf16[192,384]{1,0:T(8,128)(2,1)S(1)} %fusion.42), channel_id=1, source_target_pairs={{0,192},{16,208},{32,224},{48,240},{64,0},{80,16},{96,32},{112,48}... | collective-permute-start | bytes 442376 | tf_op jit(solution)/shard_map/ppermute | solution.py:94
  165.4 7.3 %collective-permute-start.11 = (bf16[48,1536]{1,0:T(8,128)(2,1)S(1)}, bf16[48,1536]{1,0:T(8,128)(2,1)S(1)}, u32[]{:S(2)}, u32[]{:S(2)}) collective-permute-start(bf16[48,1536]{1,0:T(8,128)(2,1)S(1)} %fusion.43), channel_id=1, source_target_pairs={{0,16},{16,32},{32,48},{48,0},{64,80},{80,96},{96,112},{112,64},{1... | collective-permute-start | bytes 442376 | tf_op jit(solution)/shard_map/ppermute | solution.py:93
  166.6 9.7 %copy-start.1 = (bf16[768,16]{0,1:T(8,128)(2,1)S(1)}, bf16[768,16]{0,1:T(8,128)(2,1)}, u32[]{:S(2)}) copy-start(bf16[768,16]{0,1:T(8,128)(2,1)} %param.10) | copy-start | bytes 73732
  166.6 6.4 %collective-permute-start.5 = (bf16[48,1536]{1,0:T(8,128)(2,1)S(1)}, bf16[48,1536]{1,0:T(8,128)(2,1)S(1)}, u32[]{:S(2)}, u32[]{:S(2)}) collective-permute-start(bf16[48,1536]{1,0:T(8,128)(2,1)S(1)} %fusion.45), channel_id=1, source_target_pairs={{0,64},{16,80},{32,96},{48,112},{64,128},{80,144},{96,160},{112,17... | collective-permute-start | bytes 442376 | tf_op jit(solution)/shard_map/ppermute | solution.py:93
  166.7 7.2 %collective-permute-start.23 = (bf16[192,384]{1,0:T(8,128)(2,1)S(1)}, bf16[192,384]{1,0:T(8,128)(2,1)S(1)}, u32[]{:S(2)}, u32[]{:S(2)}) collective-permute-start(bf16[192,384]{1,0:T(8,128)(2,1)S(1)} %fusion.39), channel_id=1, source_target_pairs={{0,48},{16,0},{32,16},{48,32},{64,112},{80,64},{96,80},{112,96},{1... | collective-permute-start | bytes 442376 | tf_op jit(solution)/shard_map/ppermute | solution.py:94
  169.0 6.3 %collective-permute-start.17 = (bf16[192,384]{1,0:T(8,128)(2,1)S(1)}, bf16[192,384]{1,0:T(8,128)(2,1)S(1)}, u32[]{:S(2)}, u32[]{:S(2)}) collective-permute-start(bf16[192,384]{1,0:T(8,128)(2,1)S(1)} %fusion.41), channel_id=1, source_target_pairs={{0,192},{16,208},{32,224},{48,240},{64,0},{80,16},{96,32},{112,48}... | collective-permute-start | bytes 442376 | tf_op jit(solution)/shard_map/ppermute | solution.py:94
Sparse Core Ops, SparseCore 0:
  10.4 55.3 all-gather.1

commit v6 on v5

--- a/solution.py
+++ b/solution.py
@@ -217,10 +217,10 @@
     spread_t = lax.optimization_barrier(lax.dot_general(
         weight_out[0], delta_row, (((1,), (1,)), ((), ())), preferred_element_type=jnp.float32
     ).astype(jnp.bfloat16))
-    dhidden = lax.dot_general(
-        sel_gate.astype(jnp.bfloat16), spread_t, (((0,), (1,)), ((), ())),
-        preferred_element_type=jnp.float32,
-    )
+    spread_src = spread_t.T.astype(jnp.float32).reshape(expert_size, seq_count, ffn_width)
+    dhidden = sum(
+        my_meta[:, :, sl, None] * spread_src[:, None, sl, :] for sl in range(seq_count)
+    ).reshape(expert_size * capacity, ffn_width)
     delta_pre = lax.optimization_barrier((dhidden * slope_flat).astype(jnp.bfloat16))
     grad_in_term = lax.dot_general(
         input_flat, delta_pre, dims_t, preferred_element_type=jnp.float32

time: 186 us -> 192 us (1.032)
  other arithmetic: 10.9 us -> 17.4 us
  starting transfers between devices: 58.5 us -> 63.5 us
  waiting for transfers between devices: 64.7 us -> 60.2 us
  matrix products: 26.3 us -> 24 us
    convert_element_type x0 -> x2, other arithmetic: none -> 6.45 us  [the longest x1 6.4 us: on_device(): (dhidden * slope_flat).astype(jnp.bfloat16)]
    ppermute x12, waiting for transfers between devices: 28.2 us -> 23 us  [ring_step(): got_f = lax.ppermute(state['acc_f'].astype(jnp.bfloat16), 'dp', fwd_pairs)]
    ppermute x12, starting transfers between devices: 29.1 us -> 34 us  [ring_step(): got_b = lax.ppermute(state['acc_b'].astype(jnp.bfloat16), 'dp', bwd_pairs)]
    dot_general x1 -> x0, matrix products: 4.32 us -> none  [on_device(): lax.dot_general(sel_gate.astype(jnp.bfloat16), spread_t, (((0,), (1,)), (...]
    dot_general x1, matrix products: 1.46 us -> 3.69 us  [on_device(): lax.dot_general(seq_hidden.astype(jnp.bfloat16), delta_row, dims_t, prefe...]
  transfers between devices with their start and end apart: 28 -> 28, of which waited for: 14 -> 11; matrix products, arithmetic and copies ran while one was open for 13% -> 13% of each run, Pallas kernels for 0% -> 0%
where the time goes in v6:
time: 192 us; the launch traced here: 189 us
  starting transfers between devices  63.5 us (33%)
  waiting for transfers between devices  60.2 us (31%)
  matrix products  24 us (12%)
  other arithmetic  17.4 us (9%)
  between operations  14.6 us (8%)
  local copies, waits for them, and re-layouts  9.18 us (5%)
    ppermute x12, starting transfers between devices, ring_step(): got_b = lax.ppermute(state['acc_b'].astype(jnp.bfloat16), 'dp', bwd_pairs)  34 us
    ppermute x12, waiting for transfers between devices, ring_step(): got_f = lax.ppermute(state['acc_f'].astype(jnp.bfloat16), 'dp', fwd_pairs)  23 us
    all_to_all x1, waiting for transfers between devices, on_device(): lax.all_to_all(outgoing, 'expert', split_axis=0, concat_axis=0, tiled=True)  20.8 us
    ppermute x12, starting transfers between devices, ring_step(): got_f = lax.ppermute(state['acc_f'].astype(jnp.bfloat16), 'dp', fwd_pairs)  9.12 us
    all_to_all x1, starting transfers between devices, on_device(): lax.all_to_all(outgoing, 'expert', split_axis=0, concat_axis=0, tiled=True)  8.59 us
    all_to_all x1, starting transfers between devices, on_device(): lax.all_to_all(moe_seq.reshape(expert_size, seq_count, model_width), 'exp...  6.8 us
    all_to_all x1, waiting for transfers between devices, on_device(): lax.all_to_all(moe_seq.reshape(expert_size, seq_count, model_width), 'exp...  6.67 us
    convert_element_type x1, other arithmetic, on_device(): (dhidden * slope_flat).astype(jnp.bfloat16)  6.4 us
  transfers between devices with their start and end apart: 28, of which 11 were waited for; matrix products, arithmetic and copies ran while one was open for 13% of the time, Pallas kernels for 0%

profile of v6, /device:TPU:32, one launch (start us, length us, event | category | flops | bytes accessed | tf_op | source)
XLA Modules:
  0.0 188.9 jit_solution(15869173517138811862)
XLA Ops:
  7.9 0.8 copy.67
  10.8 1.0 fusion.84
  11.9 0.8 select_reduce_fusion.1
  13.1 1.3 fusion.50
  14.8 1.0 pad_maximum_fusion
  15.8 8.6 %all-to-all-start = ((bf16[16,32,896]{2,1,0:T(8,128)(2,1)}), bf16[16,32,896]{2,1,0:T(8,128)(2,1)S(1)}, u32[]{:S(2)}, u32[]{:S(2)}) async-start(bf16[16,32,896]{2,1,0:T(8,128)(2,1)} %pad_maximum_fusion), calls=%async_computation | async-start | bytes 1835008 | tf_op jit(solution)/shard_map/all_to_all | solution.py:168
  25.4 20.8 %all-to-all-done = bf16[16,32,896]{2,1,0:T(8,128)(2,1)S(1)} async-done(((bf16[16,32,896]{2,1,0:T(8,128)(2,1)}), bf16[16,32,896]{2,1,0:T(8,128)(2,1)S(1)}, u32[]{:S(2)}, u32[]{:S(2)}) %all-to-all-start) | async-done | bytes 917536 | tf_op jit(solution)/shard_map/all_to_all | solution.py:168
  46.8 4.5 %fusion.14 = f32[512,3072]{1,0:T(8,128)S(1)} fusion(bf16[512,768]{1,0:T(8,128)(2,1)S(1)} %bitcast.190, bf16[1,768,3072]{2,1,0:T(8,128)(2,1)} %param.11), kind=kOutput, calls=%fused_computation.22 | convolution fusion | flops 2415919104 | bytes 11796480 | tf_op jit(solution)/shard_map/dot_general | solution.py:176
  51.4 2.5 %fusion.22 = f32[32,3072]{1,0:T(8,128)S(1)} fusion(bf16[32,512]{1,0:T(8,128)(2,1)S(1)} %convert_element_type.313, f32[512,3072]{1,0:T(8,128)S(1)} %fusion.14), kind=kOutput, calls=%fused_computation.26 | convolution fusion | flops 114819072 | bytes 6717440 | tf_op jit(solution)/shard_map/dot_general | solution.py:179
  54.5 1.3 slice-done.1
  55.9 0.9 fusion.10
  56.7 0.9 fusion.33
  58.3 6.8 %all-to-all-start.1 = ((f32[16,2,768]{2,1,0:T(2,128)}), f32[16,2,768]{2,1,0:T(2,128)S(1)}, u32[]{:S(2)}, u32[]{:S(2)}) async-start(f32[16,2,768]{2,1,0:T(2,128)} %reshape.155), calls=%async_computation.1 | async-start | bytes 196608 | tf_op jit(solution)/shard_map/all_to_all | solution.py:181
  65.2 6.7 %all-to-all-done.1 = f32[16,2,768]{2,1,0:T(2,128)S(1)} async-done(((f32[16,2,768]{2,1,0:T(2,128)}), f32[16,2,768]{2,1,0:T(2,128)S(1)}, u32[]{:S(2)}, u32[]{:S(2)}) %all-to-all-start.1) | async-done | bytes 98336 | tf_op jit(solution)/shard_map/all_to_all | solution.py:181
  72.1 2.7 %multiply_reduce_fusion = f32[2048]{0:T(1024)S(1)} fusion(bf16[2048,768]{1,0:T(8,128)(2,1)} %all-gather.2.cloned.1.call-done), kind=kLoop, calls=%fused_computation.12 | loop fusion | flops 4716544 | bytes 3153920 | tf_op jit(solution)/shard_map/reduce_sum | solution.py:194
  75.0 1.0 fusion.83
  78.0 5.0 %all-to-all-start.2 = ((bf16[16,2,768]{2,1,0:T(2,128)(2,1)}), bf16[16,2,768]{2,1,0:T(2,128)(2,1)S(1)}, u32[]{:S(2)}, u32[]{:S(2)}) async-start(bf16[16,2,768]{2,1,0:T(2,128)(2,1)} %broadcast_in_dim.50), calls=%async_computation.2 | async-start | bytes 98304 | tf_op jit(solution)/shard_map/all_to_all | solution.py:211
  83.4 5.9 %all-to-all-done.2 = bf16[16,2,768]{2,1,0:T(2,128)(2,1)S(1)} async-done(((bf16[16,2,768]{2,1,0:T(2,128)(2,1)}), bf16[16,2,768]{2,1,0:T(2,128)(2,1)S(1)}, u32[]{:S(2)}, u32[]{:S(2)}) %all-to-all-start.2) | async-done | bytes 49184 | tf_op jit(solution)/shard_map/all_to_all | solution.py:211
  89.4 3.8 %fusion.19 = bf16[3072,32]{0,1:T(8,128)(2,1)S(1)} fusion(bf16[32,768]{1,0:T(8,128)(2,1)S(1)} %reshape.156, bf16[1,3072,768]{2,1,0:T(8,128)(2,1)} %param.12), kind=kOutput, calls=%fused_computation.25 | convolution fusion | flops 151093248 | bytes 4964352 | tf_op jit(solution)/shard_map/dot_general | solution.py:217
  93.2 3.7 %convolution_convert_fusion = bf16[3072,768]{1,0:T(8,128)(2,1)} fusion(bf16[32,768]{1,0:T(8,128)(2,1)S(1)} %reshape.156, f32[32,3072]{1,0:T(8,128)S(1)} %fusion.22), kind=kOutput, calls=%fused_computation.14 | convolution fusion | flops 153452544 | bytes 5160960 | tf_op jit(solution)/shard_map/dot_general | solution.py:228
  97.5 6.4 %fusion.6 = bf16[512,3072]{1,0:T(8,128)(2,1)S(1)} fusion(f32[512,3072]{1,0:T(8,128)} %copy-done.3, f32[16,3072]{1,0:T(8,128)S(1)} %get-tuple-element.24, f32[512]{0:T(512)S(1)} %mul.232, f32[16,3072]{1,0:T(8,128)S(1)} %get-tuple-element.25, f32[512]{0:T(512)S(1)} %mul.194), kind=kLoop, calls=%fused_computation.8 | loop fusion | flops 34603008 | bytes 9834496 | tf_op jit(solution)/shard_map/convert_element_type | solution.py:224
  103.9 2.9 %convolution_convert_fusion.1 = bf16[768,3072]{1,0:T(8,128)(2,1)S(1)} fusion(bf16[512,768]{1,0:T(8,128)(2,1)S(1)} %bitcast.191, bf16[512,3072]{1,0:T(8,128)(2,1)S(1)} %fusion.6), kind=kOutput, calls=%fused_computation.15 | convolution fusion | flops 2418278400 | bytes 8650752 | tf_op jit(solution)/shard_map/dot_general | solution.py:225
  107.5 1.6 collective-permute-start.6
  109.2 1.6 collective-permute-start
  110.8 0.8 fusion.80
  111.7 1.7 collective-permute-start.18
  113.5 2.6 %collective-permute-start.12 = (bf16[4,192,384]{2,1,0:T(8,128)(2,1)S(1)}, bf16[4,192,384]{2,1,0:T(8,128)(2,1)S(1)}, u32[]{:S(2)}, u32[]{:S(2)}) collective-permute-start(bf16[4,192,384]{2,1,0:T(8,128)(2,1)S(1)} %dynamic-slice_bitcast_fusion.1), channel_id=1, source_target_pairs={{0,48},{16,0},{32,16},{48,32},{64,112},{80,64},{96,80},{112,96},{1... | collective-permute-start | bytes 1769480 | tf_op jit(solution)/shard_map/ppermute | solution.py:94
  116.2 8.1 %collective-permute-done.6 = bf16[4,48,1536]{2,1,0:T(8,128)(2,1)S(1)} collective-permute-done((bf16[4,48,1536]{2,1,0:T(8,128)(2,1)S(1)}, bf16[4,48,1536]{2,1,0:T(8,128)(2,1)S(1)}, u32[]{:S(2)}, u32[]{:S(2)}) %collective-permute-start.6) | collective-permute-done | bytes 589856 | tf_op jit(solution)/shard_map/ppermute | solution.py:93
  124.8 0.8 collective-permute-done
  126.8 3.5 %collective-permute-start.19 = (bf16[4,192,384]{2,1,0:T(8,128)(2,1)S(1)}, bf16[4,192,384]{2,1,0:T(8,128)(2,1)S(1)}, u32[]{:S(2)}, u32[]{:S(2)}) collective-permute-start(bf16[4,192,384]{2,1,0:T(8,128)(2,1)S(1)} %fusion.26), channel_id=1, source_target_pairs={{0,192},{16,208},{32,224},{48,240},{64,0},{80,16},{96,32},{112,48}... | collective-permute-start | bytes 1769480 | tf_op jit(solution)/shard_map/ppermute | solution.py:94
  130.4 2.9 %collective-permute-start.13 = (bf16[4,192,384]{2,1,0:T(8,128)(2,1)S(1)}, bf16[4,192,384]{2,1,0:T(8,128)(2,1)S(1)}, u32[]{:S(2)}, u32[]{:S(2)}) collective-permute-start(bf16[4,192,384]{2,1,0:T(8,128)(2,1)S(1)} %fusion.28), channel_id=1, source_target_pairs={{0,48},{16,0},{32,16},{48,32},{64,112},{80,64},{96,80},{112,96},{1... | collective-permute-start | bytes 1769480 | tf_op jit(solution)/shard_map/ppermute | solution.py:94
  133.3 7.1 %collective-permute-done.7 = bf16[4,48,1536]{2,1,0:T(8,128)(2,1)S(1)} collective-permute-done((bf16[4,48,1536]{2,1,0:T(8,128)(2,1)S(1)}, bf16[4,48,1536]{2,1,0:T(8,128)(2,1)S(1)}, u32[]{:S(2)}, u32[]{:S(2)}) %collective-permute-start.7) | collective-permute-done | bytes 589856 | tf_op jit(solution)/shard_map/ppermute | solution.py:93
  141.4 1.1 collective-permute-start.2
  142.6 3.3 %collective-permute-start.20 = (bf16[4,192,384]{2,1,0:T(8,128)(2,1)S(1)}, bf16[4,192,384]{2,1,0:T(8,128)(2,1)S(1)}, u32[]{:S(2)}, u32[]{:S(2)}) collective-permute-start(bf16[4,192,384]{2,1,0:T(8,128)(2,1)S(1)} %fusion.25), channel_id=1, source_target_pairs={{0,192},{16,208},{32,224},{48,240},{64,0},{80,16},{96,32},{112,48}... | collective-permute-start | bytes 1769480 | tf_op jit(solution)/shard_map/ppermute | solution.py:94
  146.1 3.1 %collective-permute-start.14 = (bf16[4,192,384]{2,1,0:T(8,128)(2,1)S(1)}, bf16[4,192,384]{2,1,0:T(8,128)(2,1)S(1)}, u32[]{:S(2)}, u32[]{:S(2)}) collective-permute-start(bf16[4,192,384]{2,1,0:T(8,128)(2,1)S(1)} %fusion.27), channel_id=1, source_target_pairs={{0,48},{16,0},{32,16},{48,32},{64,112},{80,64},{96,80},{112,96},{1... | collective-permute-start | bytes 1769480 | tf_op jit(solution)/shard_map/ppermute | solution.py:94
  149.2 6.3 %collective-permute-done.8 = bf16[4,48,1536]{2,1,0:T(8,128)(2,1)S(1)} collective-permute-done((bf16[4,48,1536]{2,1,0:T(8,128)(2,1)S(1)}, bf16[4,48,1536]{2,1,0:T(8,128)(2,1)S(1)}, u32[]{:S(2)}, u32[]{:S(2)}) %collective-permute-start.8) | collective-permute-done | bytes 589856 | tf_op jit(solution)/shard_map/ppermute | solution.py:93
  155.8 1.8 collective-permute-start.9
  157.8 1.0 collective-permute-start.3
  158.9 1.5 collective-permute-start.21
  160.4 1.3 collective-permute-done.14
  161.9 2.5 %collective-permute-start.15 = (bf16[192,384]{1,0:T(8,128)(2,1)S(1)}, bf16[192,384]{1,0:T(8,128)(2,1)S(1)}, u32[]{:S(2)}, u32[]{:S(2)}) collective-permute-start(bf16[192,384]{1,0:T(8,128)(2,1)S(1)} %fusion.56), channel_id=1, source_target_pairs={{0,192},{16,208},{32,224},{48,240},{64,0},{80,16},{96,32},{112,48}... | collective-permute-start | bytes 442376 | tf_op jit(solution)/shard_map/ppermute | solution.py:94
  164.9 3.1 %collective-permute-start.22 = (bf16[192,384]{1,0:T(8,128)(2,1)S(1)}, bf16[192,384]{1,0:T(8,128)(2,1)S(1)}, u32[]{:S(2)}, u32[]{:S(2)}) collective-permute-start(bf16[192,384]{1,0:T(8,128)(2,1)S(1)} %fusion.41), channel_id=1, source_target_pairs={{0,48},{16,0},{32,16},{48,32},{64,112},{80,64},{96,80},{112,96},{1... | collective-permute-start | bytes 442376 | tf_op jit(solution)/shard_map/ppermute | solution.py:94
  168.1 3.2 %collective-permute-start.16 = (bf16[192,384]{1,0:T(8,128)(2,1)S(1)}, bf16[192,384]{1,0:T(8,128)(2,1)S(1)}, u32[]{:S(2)}, u32[]{:S(2)}) collective-permute-start(bf16[192,384]{1,0:T(8,128)(2,1)S(1)} %fusion.43), channel_id=1, source_target_pairs={{0,192},{16,208},{32,224},{48,240},{64,0},{80,16},{96,32},{112,48}... | collective-permute-start | bytes 442376 | tf_op jit(solution)/shard_map/ppermute | solution.py:94
  172.0 3.2 %collective-permute-start.23 = (bf16[192,384]{1,0:T(8,128)(2,1)S(1)}, bf16[192,384]{1,0:T(8,128)(2,1)S(1)}, u32[]{:S(2)}, u32[]{:S(2)}) collective-permute-start(bf16[192,384]{1,0:T(8,128)(2,1)S(1)} %fusion.40), channel_id=1, source_target_pairs={{0,48},{16,0},{32,16},{48,32},{64,112},{80,64},{96,80},{112,96},{1... | collective-permute-start | bytes 442376 | tf_op jit(solution)/shard_map/ppermute | solution.py:94
  175.2 3.3 %collective-permute-start.17 = (bf16[192,384]{1,0:T(8,128)(2,1)S(1)}, bf16[192,384]{1,0:T(8,128)(2,1)S(1)}, u32[]{:S(2)}, u32[]{:S(2)}) collective-permute-start(bf16[192,384]{1,0:T(8,128)(2,1)S(1)} %fusion.42), channel_id=1, source_target_pairs={{0,192},{16,208},{32,224},{48,240},{64,0},{80,16},{96,32},{112,48}... | collective-permute-start | bytes 442376 | tf_op jit(solution)/shard_map/ppermute | solution.py:94
  178.6 0.9 maximum_bitcast_fusion
  179.5 1.7 collective-permute-done.17
  181.2 0.9 maximum_bitcast_fusion.1
  (130 shorter events, 16.1 us)
Async XLA Ops:
  7.2 3.7 %copy-start = (bf16[768,16]{0,1:T(8,128)(2,1)S(1)}, bf16[768,16]{0,1:T(8,128)(2,1)}, u32[]{:S(2)}) copy-start(bf16[768,16]{0,1:T(8,128)(2,1)} %param.10) | copy-start | bytes 73732
  7.2 64.9 %all-gather.2.cloned.1.call-start = ((), (), s32[]{:S(2)}) async-start(), calls=%async_computation.3 | async-start | bytes 3342336 | tf_op jit(solution)/shard_map/all_gather | solution.py:193
  14.4 10.7 %copy-start.5 = (s32[256,16]{0,1:T(8,128)S(1)}, s32[256,16]{0,1:T(8,128)}, u32[]{:S(2)}) copy-start(s32[256,16]{0,1:T(8,128)} %param.15) | copy-start | bytes 49156
  14.5 10.9 %copy-start.4 = (bf16[128,768]{1,0:T(8,128)(2,1)S(1)}, bf16[128,768]{1,0:T(8,128)(2,1)}, u32[]{:S(2)}) copy-start(bf16[128,768]{1,0:T(8,128)(2,1)} %param.8) | copy-start | bytes 589828
  15.8 30.4 %all-to-all-start = ((bf16[16,32,896]{2,1,0:T(8,128)(2,1)}), bf16[16,32,896]{2,1,0:T(8,128)(2,1)S(1)}, u32[]{:S(2)}, u32[]{:S(2)}) async-start(bf16[16,32,896]{2,1,0:T(8,128)(2,1)} %pad_maximum_fusion), calls=%async_computation | async-start | bytes 1835008 | tf_op jit(solution)/shard_map/all_to_all | solution.py:168
  46.8 7.8 %slice-start = ((s8[4718592]{0:T(1024)(128)(4,1)}), s8[524288]{0:T(1024)(128)(4,1)S(1)}, s32[]{:S(2)}) async-start(s8[4718592]{0:T(1024)(128)(4,1)} %bitcast.184), calls=%async_computation.4 | async-start | bytes 1048576
  51.3 3.2 %copy-start.3 = (f32[512,3072]{1,0:T(8,128)}, f32[512,3072]{1,0:T(8,128)S(1)}, u32[]{:S(2)}) copy-start(f32[512,3072]{1,0:T(8,128)S(1)} %fusion.14) | copy-start | bytes 18874372
  51.3 4.5 %slice-start.1 = ((s8[4718592]{0:T(1024)(128)(4,1)}), s8[4194304]{0:T(1024)(128)(4,1)S(1)}, s32[]{:S(2)}) async-start(s8[4718592]{0:T(1024)(128)(4,1)} %bitcast.184), calls=%async_computation.5 | async-start | bytes 8388608
  58.3 13.5 %all-to-all-start.1 = ((f32[16,2,768]{2,1,0:T(2,128)}), f32[16,2,768]{2,1,0:T(2,128)S(1)}, u32[]{:S(2)}, u32[]{:S(2)}) async-start(f32[16,2,768]{2,1,0:T(2,128)} %reshape.155), calls=%async_computation.1 | async-start | bytes 196608 | tf_op jit(solution)/shard_map/all_to_all | solution.py:181
  72.1 3.0 %copy-start.2 = (bf16[2048,768]{1,0:T(8,128)(2,1)S(1)}, bf16[2048,768]{1,0:T(8,128)(2,1)}, u32[]{:S(2)}) copy-start(bf16[2048,768]{1,0:T(8,128)(2,1)} %all-gather.2.cloned.1.call-done) | copy-start | bytes 9437188
  78.0 11.4 %all-to-all-start.2 = ((bf16[16,2,768]{2,1,0:T(2,128)(2,1)}), bf16[16,2,768]{2,1,0:T(2,128)(2,1)S(1)}, u32[]{:S(2)}, u32[]{:S(2)}) async-start(bf16[16,2,768]{2,1,0:T(2,128)(2,1)} %broadcast_in_dim.50), calls=%async_computation.2 | async-start | bytes 98304 | tf_op jit(solution)/shard_map/all_to_all | solution.py:211
  106.8 4.0 %slice-start.2 = ((s8[4718592]{0:T(1024)(128)(4,1)}), s8[4194304]{0:T(1024)(128)(4,1)S(1)}, s32[]{:S(2)}) async-start(s8[4718592]{0:T(1024)(128)(4,1)} %bitcast.186), calls=%async_computation.6 | async-start | bytes 8388608
  106.8 4.0 %slice-start.3 = ((s8[4718592]{0:T(1024)(128)(4,1)}), s8[524288]{0:T(1024)(128)(4,1)S(1)}, s32[]{:S(2)}) async-start(s8[4718592]{0:T(1024)(128)(4,1)} %bitcast.186), calls=%async_computation.7 | async-start | bytes 1048576
  107.5 16.8 %collective-permute-start.6 = (bf16[4,48,1536]{2,1,0:T(8,128)(2,1)S(1)}, bf16[4,48,1536]{2,1,0:T(8,128)(2,1)S(1)}, u32[]{:S(2)}, u32[]{:S(2)}) collective-permute-start(bf16[4,48,1536]{2,1,0:T(8,128)(2,1)S(1)} %dynamic-slice_bitcast_fusion.2), channel_id=1, source_target_pairs={{0,64},{16,80},{32,96},{48,112},{64,128},{80,144},{96,160},{112,17... | collective-permute-start | bytes 1769480 | tf_op jit(solution)/shard_map/ppermute | solution.py:93
  109.2 16.4 %collective-permute-start = (bf16[4,48,1536]{2,1,0:T(8,128)(2,1)S(1)}, bf16[4,48,1536]{2,1,0:T(8,128)(2,1)S(1)}, u32[]{:S(2)}, u32[]{:S(2)}) collective-permute-start(bf16[4,48,1536]{2,1,0:T(8,128)(2,1)S(1)} %dynamic-slice_bitcast_fusion.3), channel_id=1, source_target_pairs={{0,16},{16,32},{32,48},{48,0},{64,80},{80,96},{96,112},{112,64},{1... | collective-permute-start | bytes 1769480 | tf_op jit(solution)/shard_map/ppermute | solution.py:93
  111.7 14.9 %collective-permute-start.18 = (bf16[4,192,384]{2,1,0:T(8,128)(2,1)S(1)}, bf16[4,192,384]{2,1,0:T(8,128)(2,1)S(1)}, u32[]{:S(2)}, u32[]{:S(2)}) collective-permute-start(bf16[4,192,384]{2,1,0:T(8,128)(2,1)S(1)} %dynamic-slice_bitcast_fusion), channel_id=1, source_target_pairs={{0,192},{16,208},{32,224},{48,240},{64,0},{80,16},{96,32},{112,48}... | collective-permute-start | bytes 1769480 | tf_op jit(solution)/shard_map/ppermute | solution.py:94
  113.5 16.7 %collective-permute-start.12 = (bf16[4,192,384]{2,1,0:T(8,128)(2,1)S(1)}, bf16[4,192,384]{2,1,0:T(8,128)(2,1)S(1)}, u32[]{:S(2)}, u32[]{:S(2)}) collective-permute-start(bf16[4,192,384]{2,1,0:T(8,128)(2,1)S(1)} %dynamic-slice_bitcast_fusion.1), channel_id=1, source_target_pairs={{0,48},{16,0},{32,16},{48,32},{64,112},{80,64},{96,80},{112,96},{1... | collective-permute-start | bytes 1769480 | tf_op jit(solution)/shard_map/ppermute | solution.py:94
  124.5 15.9 %collective-permute-start.7 = (bf16[4,48,1536]{2,1,0:T(8,128)(2,1)S(1)}, bf16[4,48,1536]{2,1,0:T(8,128)(2,1)S(1)}, u32[]{:S(2)}, u32[]{:S(2)}) collective-permute-start(bf16[4,48,1536]{2,1,0:T(8,128)(2,1)S(1)} %fusion.30), channel_id=1, source_target_pairs={{0,64},{16,80},{32,96},{48,112},{64,128},{80,144},{96,160},{112,17... | collective-permute-start | bytes 1769480 | tf_op jit(solution)/shard_map/ppermute | solution.py:93
  125.7 15.5 %collective-permute-start.1 = (bf16[4,48,1536]{2,1,0:T(8,128)(2,1)S(1)}, bf16[4,48,1536]{2,1,0:T(8,128)(2,1)S(1)}, u32[]{:S(2)}, u32[]{:S(2)}) collective-permute-start(bf16[4,48,1536]{2,1,0:T(8,128)(2,1)S(1)} %fusion.32), channel_id=1, source_target_pairs={{0,16},{16,32},{32,48},{48,0},{64,80},{80,96},{96,112},{112,64},{1... | collective-permute-start | bytes 1769480 | tf_op jit(solution)/shard_map/ppermute | solution.py:93
  126.8 15.7 %collective-permute-start.19 = (bf16[4,192,384]{2,1,0:T(8,128)(2,1)S(1)}, bf16[4,192,384]{2,1,0:T(8,128)(2,1)S(1)}, u32[]{:S(2)}, u32[]{:S(2)}) collective-permute-start(bf16[4,192,384]{2,1,0:T(8,128)(2,1)S(1)} %fusion.26), channel_id=1, source_target_pairs={{0,192},{16,208},{32,224},{48,240},{64,0},{80,16},{96,32},{112,48}... | collective-permute-start | bytes 1769480 | tf_op jit(solution)/shard_map/ppermute | solution.py:94
  130.4 15.6 %collective-permute-start.13 = (bf16[4,192,384]{2,1,0:T(8,128)(2,1)S(1)}, bf16[4,192,384]{2,1,0:T(8,128)(2,1)S(1)}, u32[]{:S(2)}, u32[]{:S(2)}) collective-permute-start(bf16[4,192,384]{2,1,0:T(8,128)(2,1)S(1)} %fusion.28), channel_id=1, source_target_pairs={{0,48},{16,0},{32,16},{48,32},{64,112},{80,64},{96,80},{112,96},{1... | collective-permute-start | bytes 1769480 | tf_op jit(solution)/shard_map/ppermute | solution.py:94
  140.5 15.0 %collective-permute-start.8 = (bf16[4,48,1536]{2,1,0:T(8,128)(2,1)S(1)}, bf16[4,48,1536]{2,1,0:T(8,128)(2,1)S(1)}, u32[]{:S(2)}, u32[]{:S(2)}) collective-permute-start(bf16[4,48,1536]{2,1,0:T(8,128)(2,1)S(1)} %fusion.29), channel_id=1, source_target_pairs={{0,64},{16,80},{32,96},{48,112},{64,128},{80,144},{96,160},{112,17... | collective-permute-start | bytes 1769480 | tf_op jit(solution)/shard_map/ppermute | solution.py:93
  141.4 16.1 %collective-permute-start.2 = (bf16[4,48,1536]{2,1,0:T(8,128)(2,1)S(1)}, bf16[4,48,1536]{2,1,0:T(8,128)(2,1)S(1)}, u32[]{:S(2)}, u32[]{:S(2)}) collective-permute-start(bf16[4,48,1536]{2,1,0:T(8,128)(2,1)S(1)} %fusion.31), channel_id=1, source_target_pairs={{0,16},{16,32},{32,48},{48,0},{64,80},{80,96},{96,112},{112,64},{1... | collective-permute-start | bytes 1769480 | tf_op jit(solution)/shard_map/ppermute | solution.py:93
  142.6 16.1 %collective-permute-start.20 = (bf16[4,192,384]{2,1,0:T(8,128)(2,1)S(1)}, bf16[4,192,384]{2,1,0:T(8,128)(2,1)S(1)}, u32[]{:S(2)}, u32[]{:S(2)}) collective-permute-start(bf16[4,192,384]{2,1,0:T(8,128)(2,1)S(1)} %fusion.25), channel_id=1, source_target_pairs={{0,192},{16,208},{32,224},{48,240},{64,0},{80,16},{96,32},{112,48}... | collective-permute-start | bytes 1769480 | tf_op jit(solution)/shard_map/ppermute | solution.py:94
  146.1 15.6 %collective-permute-start.14 = (bf16[4,192,384]{2,1,0:T(8,128)(2,1)S(1)}, bf16[4,192,384]{2,1,0:T(8,128)(2,1)S(1)}, u32[]{:S(2)}, u32[]{:S(2)}) collective-permute-start(bf16[4,192,384]{2,1,0:T(8,128)(2,1)S(1)} %fusion.27), channel_id=1, source_target_pairs={{0,48},{16,0},{32,16},{48,32},{64,112},{80,64},{96,80},{112,96},{1... | collective-permute-start | bytes 1769480 | tf_op jit(solution)/shard_map/ppermute | solution.py:94
  155.8 8.6 %collective-permute-start.9 = (bf16[48,1536]{1,0:T(8,128)(2,1)S(1)}, bf16[48,1536]{1,0:T(8,128)(2,1)S(1)}, u32[]{:S(2)}, u32[]{:S(2)}) collective-permute-start(bf16[48,1536]{1,0:T(8,128)(2,1)S(1)} %fusion.55), channel_id=1, source_target_pairs={{0,16},{16,32},{32,48},{48,0},{64,80},{80,96},{96,112},{112,64},{1... | collective-permute-start | bytes 442376 | tf_op jit(solution)/shard_map/ppermute | solution.py:93
  157.8 6.7 %collective-permute-start.3 = (bf16[48,1536]{1,0:T(8,128)(2,1)S(1)}, bf16[48,1536]{1,0:T(8,128)(2,1)S(1)}, u32[]{:S(2)}, u32[]{:S(2)}) collective-permute-start(bf16[48,1536]{1,0:T(8,128)(2,1)S(1)} %fusion.54), channel_id=1, source_target_pairs={{0,64},{16,80},{32,96},{48,112},{64,128},{80,144},{96,160},{112,17... | collective-permute-start | bytes 442376 | tf_op jit(solution)/shard_map/ppermute | solution.py:93
  158.9 6.0 %collective-permute-start.21 = (bf16[192,384]{1,0:T(8,128)(2,1)S(1)}, bf16[192,384]{1,0:T(8,128)(2,1)S(1)}, u32[]{:S(2)}, u32[]{:S(2)}) collective-permute-start(bf16[192,384]{1,0:T(8,128)(2,1)S(1)} %fusion.57), channel_id=1, source_target_pairs={{0,48},{16,0},{32,16},{48,32},{64,112},{80,64},{96,80},{112,96},{1... | collective-permute-start | bytes 442376 | tf_op jit(solution)/shard_map/ppermute | solution.py:94
  161.9 6.2 %collective-permute-start.15 = (bf16[192,384]{1,0:T(8,128)(2,1)S(1)}, bf16[192,384]{1,0:T(8,128)(2,1)S(1)}, u32[]{:S(2)}, u32[]{:S(2)}) collective-permute-start(bf16[192,384]{1,0:T(8,128)(2,1)S(1)} %fusion.56), channel_id=1, source_target_pairs={{0,192},{16,208},{32,224},{48,240},{64,0},{80,16},{96,32},{112,48}... | collective-permute-start | bytes 442376 | tf_op jit(solution)/shard_map/ppermute | solution.py:94
  164.4 6.9 %collective-permute-start.10 = (bf16[48,1536]{1,0:T(8,128)(2,1)S(1)}, bf16[48,1536]{1,0:T(8,128)(2,1)S(1)}, u32[]{:S(2)}, u32[]{:S(2)}) collective-permute-start(bf16[48,1536]{1,0:T(8,128)(2,1)S(1)} %fusion.45), channel_id=1, source_target_pairs={{0,16},{16,32},{32,48},{48,0},{64,80},{80,96},{96,112},{112,64},{1... | collective-permute-start | bytes 442376 | tf_op jit(solution)/shard_map/ppermute | solution.py:93
  164.5 7.1 %collective-permute-start.4 = (bf16[48,1536]{1,0:T(8,128)(2,1)S(1)}, bf16[48,1536]{1,0:T(8,128)(2,1)S(1)}, u32[]{:S(2)}, u32[]{:S(2)}) collective-permute-start(bf16[48,1536]{1,0:T(8,128)(2,1)S(1)} %fusion.47), channel_id=1, source_target_pairs={{0,64},{16,80},{32,96},{48,112},{64,128},{80,144},{96,160},{112,17... | collective-permute-start | bytes 442376 | tf_op jit(solution)/shard_map/ppermute | solution.py:93
  164.9 7.0 %collective-permute-start.22 = (bf16[192,384]{1,0:T(8,128)(2,1)S(1)}, bf16[192,384]{1,0:T(8,128)(2,1)S(1)}, u32[]{:S(2)}, u32[]{:S(2)}) collective-permute-start(bf16[192,384]{1,0:T(8,128)(2,1)S(1)} %fusion.41), channel_id=1, source_target_pairs={{0,48},{16,0},{32,16},{48,32},{64,112},{80,64},{96,80},{112,96},{1... | collective-permute-start | bytes 442376 | tf_op jit(solution)/shard_map/ppermute | solution.py:94
  168.1 7.1 %collective-permute-start.16 = (bf16[192,384]{1,0:T(8,128)(2,1)S(1)}, bf16[192,384]{1,0:T(8,128)(2,1)S(1)}, u32[]{:S(2)}, u32[]{:S(2)}) collective-permute-start(bf16[192,384]{1,0:T(8,128)(2,1)S(1)} %fusion.43), channel_id=1, source_target_pairs={{0,192},{16,208},{32,224},{48,240},{64,0},{80,16},{96,32},{112,48}... | collective-permute-start | bytes 442376 | tf_op jit(solution)/shard_map/ppermute | solution.py:94
  171.3 7.2 %collective-permute-start.11 = (bf16[48,1536]{1,0:T(8,128)(2,1)S(1)}, bf16[48,1536]{1,0:T(8,128)(2,1)S(1)}, u32[]{:S(2)}, u32[]{:S(2)}) collective-permute-start(bf16[48,1536]{1,0:T(8,128)(2,1)S(1)} %fusion.44), channel_id=1, source_target_pairs={{0,16},{16,32},{32,48},{48,0},{64,80},{80,96},{96,112},{112,64},{1... | collective-permute-start | bytes 442376 | tf_op jit(solution)/shard_map/ppermute | solution.py:93
  171.7 10.4 %copy-start.1 = (bf16[768,16]{0,1:T(8,128)(2,1)S(1)}, bf16[768,16]{0,1:T(8,128)(2,1)}, u32[]{:S(2)}) copy-start(bf16[768,16]{0,1:T(8,128)(2,1)} %param.10) | copy-start | bytes 73732
  171.7 6.8 %collective-permute-start.5 = (bf16[48,1536]{1,0:T(8,128)(2,1)S(1)}, bf16[48,1536]{1,0:T(8,128)(2,1)S(1)}, u32[]{:S(2)}, u32[]{:S(2)}) collective-permute-start(bf16[48,1536]{1,0:T(8,128)(2,1)S(1)} %fusion.46), channel_id=1, source_target_pairs={{0,64},{16,80},{32,96},{48,112},{64,128},{80,144},{96,160},{112,17... | collective-permute-start | bytes 442376 | tf_op jit(solution)/shard_map/ppermute | solution.py:93
  172.0 7.4 %collective-permute-start.23 = (bf16[192,384]{1,0:T(8,128)(2,1)S(1)}, bf16[192,384]{1,0:T(8,128)(2,1)S(1)}, u32[]{:S(2)}, u32[]{:S(2)}) collective-permute-start(bf16[192,384]{1,0:T(8,128)(2,1)S(1)} %fusion.40), channel_id=1, source_target_pairs={{0,48},{16,0},{32,16},{48,32},{64,112},{80,64},{96,80},{112,96},{1... | collective-permute-start | bytes 442376 | tf_op jit(solution)/shard_map/ppermute | solution.py:94
  175.2 6.0 %collective-permute-start.17 = (bf16[192,384]{1,0:T(8,128)(2,1)S(1)}, bf16[192,384]{1,0:T(8,128)(2,1)S(1)}, u32[]{:S(2)}, u32[]{:S(2)}) collective-permute-start(bf16[192,384]{1,0:T(8,128)(2,1)S(1)} %fusion.42), channel_id=1, source_target_pairs={{0,192},{16,208},{32,224},{48,240},{64,0},{80,16},{96,32},{112,48}... | collective-permute-start | bytes 442376 | tf_op jit(solution)/shard_map/ppermute | solution.py:94
Sparse Core Ops, SparseCore 0:
  10.4 55.3 all-gather.1
